TPU v7x, 256 devices: a whole 4x4x8 slice. The times are simulated.
256 devices in a mesh: req: 8 (over z), exp: 32 (over y, x, core).
Axes of the slice: x: 4, y: 4, z: 8, core: 2. Of those that a mesh axis runs over, the one named last changes fastest.
Arguments:
- residual: bfloat16 [32768, 1536], P(('req', 'exp')), may hold values from -2 to 2
- queries: bfloat16 [32768, 1536], P(('req', 'exp')), may hold values from -8 to 8
- suffix_key_values: bfloat16 [2, 32768, 256], P(None, ('req', 'exp')), may hold values from -8 to 8
- prefix_key_values: bfloat16 [2, 4096, 256], P(None, ('req', 'exp')), may hold values from -6 to 6
- request_ids: int32 [256, 128], P(('req', 'exp')), may hold values from 0 to 3, never falling along the last dimension, each value on 1 to 64 neighbouring positions
- out_weight: bfloat16 [1536, 1536], P('req'), may hold values from -0.15625 to 0.15625
- norm_gain: float32 [1536], replicated, may hold values from 0.5 to 1.5
- expert_routes: int32 [32768, 4], P(('req', 'exp')), may hold values from 0 to 31, all different within a row; in each aligned block of 128 rows (0 to 127, 128 to 255, ...) at most 24 rows name the same one
- route_gates: float32 [32768, 4], P(('req', 'exp')), may hold values from 0.1 to 0.6
- gate_experts: bfloat16 [32, 1536, 768], P('exp'), may hold values from -0.15625 to 0.15625
- up_experts: bfloat16 [32, 1536, 768], P('exp'), may hold values from -0.15625 to 0.15625
- down_experts: bfloat16 [32, 768, 1536], P('exp'), may hold values from -0.21875 to 0.21875
Outputs:
- layer_out: bfloat16 [32768, 1536], P(('req', 'exp'))
Inputs may be any that keep to these rules, and one draw needn't show every extreme that they name: `expert_routes`: in the rows of one device no expert is named by more than 24 routes, a bound that some block reaches of them; a row names 4 different experts. `request_ids`: along a row the numbers never fall; each number marks one request of 1 to 64 tokens, and one request in the row has exactly 64.
All inputs are finite; a program needn't handle non-finite values.
Results may differ from a plain program's by a relative error of at most 0.013.
Values may be sent and summed in bfloat16 or wider, within the bound.
No kernel may reach another device: no remote copies, remote signals or barrier semaphores. Data moves between devices by JAX's collectives and lax.ppermute only.
A program may use at most 64 MiB of HBM per device.

v0:
```python
import math

import jax
import jax.numpy as jnp
from jax import lax
from jax.sharding import PartitionSpec as P

QUERY_HEADS = 12
KEY_VALUE_HEADS = 2
HEAD_SIZE = 128


EPSILON = 1e-06
MASKED_SCORE = -1e30


def attend_keys(softmax_state, query_head_rows, key_matrix_rows, value_matrix_rows, allowed):
    row_peak, row_total, summed = softmax_state
    scores = jnp.einsum(
        "tgjd,rgd->gjtr", query_head_rows, key_matrix_rows, preferred_element_type=jnp.float32
    ) * (1.0 / math.sqrt(query_head_rows.shape[3]))
    if allowed is not None:
        scores = jnp.where(allowed, scores, MASKED_SCORE)
    new_peak = jnp.maximum(row_peak, jnp.max(scores, axis=3))
    weights = jnp.exp(scores - new_peak[..., None])
    rescale = jnp.exp(row_peak - new_peak)
    row_total = row_total * rescale + jnp.sum(weights, axis=3)
    summed = summed * rescale[..., None] + jnp.einsum(
        "gjtr,rgd->gjtd",
        weights.astype(jnp.bfloat16),
        value_matrix_rows,
        preferred_element_type=jnp.float32,
    )
    return (new_peak, row_total, summed)


def on_device(
    residual,
    queries,
    suffix_key_values,
    prefix_key_values,
    request_ids,
    out_weight,
    norm_gain,
    expert_routes,
    route_gates,
    gate_experts,
    up_experts,
    down_experts,
):
    local_count = queries.shape[0]
    model_width = queries.shape[1]
    queries_per_group = QUERY_HEADS // KEY_VALUE_HEADS
    query_head_rows = queries.reshape(local_count, KEY_VALUE_HEADS, queries_per_group, HEAD_SIZE)
    segment = request_ids[0]
    position = jnp.arange(local_count, dtype=jnp.int32)
    allowed = (segment[:, None] == segment[None, :]) & (position[:, None] >= position[None, :])
    start_state = (
        jnp.full((KEY_VALUE_HEADS, queries_per_group, local_count), MASKED_SCORE, jnp.float32),
        jnp.zeros((KEY_VALUE_HEADS, queries_per_group, local_count), jnp.float32),
        jnp.zeros((KEY_VALUE_HEADS, queries_per_group, local_count, HEAD_SIZE), jnp.float32),
    )
    local_keys = suffix_key_values[0].reshape(local_count, KEY_VALUE_HEADS, HEAD_SIZE)
    local_values = suffix_key_values[1].reshape(local_count, KEY_VALUE_HEADS, HEAD_SIZE)
    softmax_state = attend_keys(start_state, query_head_rows, local_keys, local_values, allowed)
    running = softmax_state
    slice_part = lax.all_gather(prefix_key_values, ("req", "exp"), axis=1, tiled=True)
    suffix_length = slice_part.shape[1]
    rows_in_block = 512
    mask_blocked = slice_part.reshape(
        2, suffix_length // rows_in_block, rows_in_block, KEY_VALUE_HEADS, HEAD_SIZE
    )

    def step(running_inner, block_index):
        section = lax.dynamic_index_in_dim(mask_blocked, block_index, 1, keepdims=False)
        return (attend_keys(running_inner, query_head_rows, section[0], section[1], None), None)

    running, unused = lax.scan(step, running, jnp.arange(suffix_length // rows_in_block))
    softmax_state = running
    row_peak, row_total, summed = softmax_state
    attended = (
        jnp.transpose(summed / row_total[..., None], (2, 0, 1, 3))
        .reshape(local_count, model_width)
        .astype(jnp.bfloat16)
    )
    section = attended
    projected = jnp.dot(
        section,
        lax.all_gather(out_weight, "req", axis=0, tiled=True),
        preferred_element_type=jnp.float32,
    )
    stream = residual.astype(jnp.float32) + projected
    inverse_rms = lax.rsqrt(jnp.mean(stream * stream, axis=1, keepdims=True) + EPSILON)
    normed = (stream * inverse_rms * norm_gain[None, :]).astype(jnp.bfloat16)
    top_count = expert_routes.shape[1]
    expert_count = gate_experts.shape[0] * lax.axis_size("exp")
    capacity = 3 * top_count * local_count // (2 * expert_count)
    flat_routes = expert_routes.reshape(-1)
    matches = (flat_routes[:, None] == jnp.arange(expert_count, dtype=jnp.int32)[None, :]).astype(
        jnp.int32
    )
    slot_rank = jnp.sum((jnp.cumsum(matches, axis=0) - 1) * matches, axis=1)
    slot_of_route = flat_routes * capacity + slot_rank
    route_index = jnp.arange(flat_routes.shape[0], dtype=jnp.int32)
    sources = (
        jnp.zeros((expert_count * capacity,), jnp.int32)
        .at[slot_of_route]
        .set(route_index // top_count)
    )
    filled = jnp.zeros((expert_count * capacity,), jnp.bool_).at[slot_of_route].set(True)
    outgoing = jnp.where(filled[:, None], normed[sources], jnp.zeros((), jnp.bfloat16)).reshape(
        expert_count, capacity, model_width
    )
    slot_rows = lax.all_to_all(outgoing, "exp", split_axis=0, concat_axis=0, tiled=True)
    senders, slot_count, features = slot_rows.shape
    flat_rows = slot_rows.reshape(senders * slot_count, features)
    gated = jnp.dot(flat_rows, gate_experts[0], preferred_element_type=jnp.float32)
    lifted = jnp.dot(flat_rows, up_experts[0], preferred_element_type=jnp.float32)
    active = (jnp.maximum(gated, 0.0) * lifted).astype(jnp.bfloat16)
    produced = jnp.dot(active, down_experts[0], preferred_element_type=jnp.float32).astype(
        jnp.bfloat16
    )
    computed = produced.reshape(senders, slot_count, features)
    returned = lax.all_to_all(computed, "exp", split_axis=0, concat_axis=0, tiled=True)
    picked = returned.reshape(expert_count * capacity, model_width)[slot_of_route].reshape(
        local_count, top_count, model_width
    )
    combined = jnp.sum(picked.astype(jnp.float32) * route_gates[:, :, None], axis=1)
    return (stream + combined).astype(jnp.bfloat16)


def solution(mesh):
    placed = (
        P(("req", "exp"), None),
        P(("req", "exp"), None),
        P(None, ("req", "exp"), None),
        P(None, ("req", "exp"), None),
        P(("req", "exp"), None),
        P("req", None),
        P(),
        P(("req", "exp"), None),
        P(("req", "exp"), None),
        P("exp", None, None),
        P("exp", None, None),
        P("exp", None, None),
    )
    return jax.shard_map(
        on_device, mesh=mesh, in_specs=placed, out_specs=P(("req", "exp"), None), check_vma=False
    )
```

profile of v0, /device:TPU:1, one launch (start us, length us, event | category | flops | bytes accessed | tf_op | source)
XLA Modules:
  0.0 308.1 jit_solution(13446459053044513230)
XLA Ops:
  9.7 1.2 copy.18
  10.9 0.9 fusion.40
  13.3 0.9 copy-done.1
  15.7 1.2 reduce-window.6
  17.5 2.4 scatter_custom_fusion.1
  20.6 2.4 scatter_custom_fusion
  23.7 1.6 convolution_add_fusion.1
  25.3 97.2 %all-gather.3.cloned.1.call-done = bf16[2,4096,256]{2,1,0:T(8,128)(2,1)} async-done(((bf16[2,16,256]{2,1,0:T(8,128)(2,1)}), bf16[2,4096,256]{2,1,0:T(8,128)(2,1)}) %all-gather.3.cloned.1.call-update) | async-done | bytes 4194320 | tf_op jit(solution)/shard_map/all_gather | solution.py:67
  122.5 7.0 %reshape.145 = bf16[2,8,512,2,128]{4,3,2,1,0:T(2,128)(2,1)} reshape(bf16[2,4096,256]{2,1,0:T(8,128)(2,1)} %all-gather.3.cloned.1.call-done) | data formatting | bytes 8388608 | tf_op jit(solution)/shard_map/reshape | solution.py:70
  130.0 55.7 %while.14 = (s32[]{:T(128)}, f32[2,6,128]{2,1,0:T(8,128)S(1)}, f32[2,6,128]{2,1,0:T(8,128)S(1)}, f32[2,6,128,128]{3,2,1,0:T(8,128)S(1)}, s32[8]{0:T(128)}, /*ind...) while((s32[]{:T(128)}, f32[2,6,128]{2,1,0:T(8,128)S(1)}, ...), condition=%wide.region_5.6_spmd, body=%wide.region_2.5_spmd.sunk | while | flops 409340928 | bytes 13074607 | solution.py:78
  130.0 1.3 dynamic_slice.9
  133.2 1.4 constant_dynamic-slice_fusion.3
  135.7 1.2 fusion.57
  136.9 1.3 dynamic_slice.9
  140.1 1.4 constant_dynamic-slice_fusion.3
  142.7 1.2 fusion.57
  143.9 1.3 dynamic_slice.9
  147.1 1.4 constant_dynamic-slice_fusion.3
  149.6 1.2 fusion.57
  150.9 1.3 dynamic_slice.9
  154.0 1.4 constant_dynamic-slice_fusion.3
  156.6 1.2 fusion.57
  157.8 1.3 dynamic_slice.9
  161.0 1.4 constant_dynamic-slice_fusion.3
  163.6 1.2 fusion.57
  164.8 1.3 dynamic_slice.9
  168.0 1.4 constant_dynamic-slice_fusion.3
  170.5 1.2 fusion.57
  171.7 1.3 dynamic_slice.9
  174.9 1.4 constant_dynamic-slice_fusion.3
  177.5 1.2 fusion.57
  178.7 1.3 dynamic_slice.9
  181.9 1.4 constant_dynamic-slice_fusion.3
  184.5 1.2 fusion.57
  185.7 1.2 copy.27
  186.8 1.2 divide_convert_fusion
  188.1 3.3 %multiply_reduce_fusion.1 = (f32[128]{0:T(128)S(1)}, f32[128,1536]{1,0:T(8,128)S(1)}) fusion(bf16[128,1536]{0,1:T(8,128)(2,1)S(1)} %bitcast.110, bf16[1536,1536]{1,0:T(8,128)(2,1)} %all-gather.5.cloned.1.call-done, bf16[128,1536]{1,0:T(8,128)(2,1)} %param.14), kind=kOutput, calls=%fused_computation.37 | convolution fusion | flops 604766080 | bytes 6291968 | tf_op jit(solution)/shard_map/dot_general | solution.py:87
  191.6 3.8 %gather_fusion = bf16[768,1536]{1,0:T(8,128)(2,1)} fusion(bf16[128,1536]{1,0:T(8,128)(2,1)S(1)} %multiply_convert_fusion.1, s32[1024]{0:T(1024)S(1)} %copy-done.3), kind=kCustom, calls=%fused_computation | custom fusion | bytes 4721664 | tf_op jit(solution)/shard_map/gather | solution.py:111
  195.4 1.9 broadcast_select_fusion
  197.3 38.4 %all_to_all.10 = bf16[32,24,1536]{2,1,0:T(8,128)(2,1)S(1)} all-to-all(bf16[32,24,1536]{2,1,0:T(8,128)(2,1)S(1)} %broadcast_select_fusion), channel_id=1, replica_groups=mesh['req'=8,'exp'=32] {'exp'}, dimensions={0} | all-to-all | bytes 4718592 | tf_op jit(solution)/shard_map/all_to_all | solution.py:114
  235.7 1.4 copy-done.2
  237.2 3.4 %fusion.13 = f32[768,768]{1,0:T(8,128)} fusion(bf16[768,1536]{1,0:T(8,128)(2,1)S(1)} %bitcast.108, bf16[1,1536,768]{2,1,0:T(8,128)(2,1)S(1)} %copy-done.9), kind=kOutput, calls=%fused_computation.25 | convolution fusion | flops 1811939328 | bytes 7077888 | tf_op jit(solution)/shard_map/dot_general | solution.py:118
  240.5 9.1 %convolution_convert_fusion = bf16[768,1536]{1,0:T(8,128)(2,1)} fusion(bf16[1,768,1536]{2,1,0:T(8,128)(2,1)S(1)} %copy-done, f32[768,768]{1,0:T(8,128)} %fusion.13, bf16[768,1536]{1,0:T(8,128)(2,1)} %bitcast.109, bf16[1,1536,768]{2,1,0:T(8,128)(2,1)} %param.23), kind=kOutput, calls=%fused_computation.21 | convolution fusion | flops 3626827776 | bytes 11796480 | tf_op jit(solution)/shard_map/dot_general | solution.py:120
  249.6 4.7 %all-to-all-start.1 = ((bf16[32,24,1536]{2,1,0:T(8,128)(2,1)}), bf16[32,24,1536]{2,1,0:T(8,128)(2,1)}, u32[]{:S(2)}, u32[]{:S(2)}) async-start(bf16[32,24,1536]{2,1,0:T(8,128)(2,1)} %bitcast.107), calls=%async_computation.1 | async-start | bytes 4718592 | tf_op jit(solution)/shard_map/all_to_all | solution.py:124
  254.5 31.1 %all-to-all-done.1 = bf16[32,24,1536]{2,1,0:T(8,128)(2,1)} async-done(((bf16[32,24,1536]{2,1,0:T(8,128)(2,1)}), bf16[32,24,1536]{2,1,0:T(8,128)(2,1)}, u32[]{:S(2)}, u32[]{:S(2)}) %all-to-all-start.1) | async-done | bytes 2359328 | tf_op jit(solution)/shard_map/all_to_all | solution.py:124
  285.6 6.4 %gather_fusion.1 = bf16[512,1536]{1,0:T(8,128)(2,1)} fusion(bf16[768,1536]{1,0:T(8,128)(2,1)} %bitcast.26, s32[1024]{0:T(1024)S(1)} %pad_clamp_fusion), kind=kCustom, calls=%fused_computation.1 | custom fusion | bytes 3147776 | tf_op jit(solution)/shard_map/gather | solution.py:125
  292.0 4.2 %reshape.107 = f32[128,4,1536]{2,1,0:T(4,128)} reshape(bf16[512,1536]{1,0:T(8,128)(2,1)} %gather_fusion.1) | data formatting | bytes 4718592 | tf_op jit(solution)/shard_map/convert_element_type | solution.py:128
  296.2 4.2 %multiply_reduce_fusion = f32[128,1536]{1,0:T(8,128)S(1)} fusion(f32[128,4,1536]{2,1,0:T(4,128)} %reshape.107, f32[128,4]{1,0:T(8,128)S(1)} %copy.32), kind=kLoop, calls=%fused_computation.22 | loop fusion | flops 1376256 | bytes 3934208 | tf_op jit(solution)/shard_map/reduce_sum | solution.py:128
  (94 shorter events, 18.7 us)
Async XLA Ops:
  6.5 234.0 %copy-start = (bf16[1,768,1536]{2,1,0:T(8,128)(2,1)S(1)}, bf16[1,768,1536]{2,1,0:T(8,128)(2,1)}, u32[]{:S(2)}) copy-start(bf16[1,768,1536]{2,1,0:T(8,128)(2,1)} %param.25) | copy-start | bytes 7077892
  6.5 116.0 %all-gather.3.cloned.1.call-start = ((), (), s32[]{:S(2)}) async-start(), calls=%async_computation.2 | async-start | bytes 4210688 | tf_op jit(solution)/shard_map/all_gather | solution.py:67
  7.3 180.8 %all-gather.5.cloned.1.call-start = ((), (), s32[]{:S(2)}) async-start(), calls=%async_computation.3 | async-start | bytes 5308416 | tf_op jit(solution)/shard_map/all_gather | solution.py:89
  13.3 0.9 copy-start.1
  17.5 6.2 %copy-start.6 = (s32[512,1]{0,1:T(1,128)}, s32[512,1]{0,1:T(1,128)S(1)}, u32[]{:S(2)}) copy-start(s32[512,1]{0,1:T(1,128)S(1)} %compare_select_fusion) | copy-start | bytes 6148
  188.1 3.3 %copy-start.5 = (f32[1536]{0:T(1024)S(1)}, f32[1536]{0:T(1024)}, u32[]{:S(2)}) copy-start(f32[1536]{0:T(1024)} %param.20) | copy-start | bytes 18436
  188.1 3.5 %copy-start.3 = (s32[1024]{0:T(1024)S(1)}, s32[1024]{0:T(1024)}, u32[]{:S(2)}) copy-start(s32[1024]{0:T(1024)} %pad_clamp_fusion.1) | copy-start | bytes 12292
  191.6 3.8 %copy-start.4 = (pred[32,24]{1,0:T(8,128)(4,1)S(1)}, pred[32,24]{1,0:T(8,128)(4,1)}, u32[]{:S(2)}) copy-start(pred[32,24]{1,0:T(8,128)(4,1)} %broadcast_in_dim.59) | copy-start | bytes 2308
  197.3 39.8 %copy-start.9 = (bf16[1,1536,768]{2,1,0:T(8,128)(2,1)S(1)}, bf16[1,1536,768]{2,1,0:T(8,128)(2,1)}, u32[]{:S(2)}) copy-start(bf16[1,1536,768]{2,1,0:T(8,128)(2,1)} %param.24) | copy-start | bytes 7077892
  235.7 1.4 copy-start.2
  249.6 4.7 %copy-start.8 = (f32[128,4]{0,1:T(4,128)S(1)}, f32[128,4]{0,1:T(4,128)}, u32[]{:S(2)}) copy-start(f32[128,4]{0,1:T(4,128)} %param.22) | copy-start | bytes 6148
  249.6 4.9 %copy-start.7 = (s32[512,1]{0,1:T(1,128)S(1)}, s32[512,1]{0,1:T(1,128)}, u32[]{:S(2)}) copy-start(s32[512,1]{0,1:T(1,128)} %copy-done.6) | copy-start | bytes 6148
  249.6 36.0 %all-to-all-start.1 = ((bf16[32,24,1536]{2,1,0:T(8,128)(2,1)}), bf16[32,24,1536]{2,1,0:T(8,128)(2,1)}, u32[]{:S(2)}, u32[]{:S(2)}) async-start(bf16[32,24,1536]{2,1,0:T(8,128)(2,1)} %bitcast.107), calls=%async_computation.1 | async-start | bytes 4718592 | tf_op jit(solution)/shard_map/all_to_all | solution.py:124
Sparse Core Ops, SparseCore 0:
  11.1 111.3 all-gather.2
  124.3 58.2 all-gather.4
where the time goes:
time: 310 us; the launch traced here: 308 us
  waiting for transfers between devices  130 us (42%)
  local copies, waits for them, and re-layouts  57.1 us (18%)
  blocking collectives  38.4 us (12%)
  matrix products  31.8 us (10%)
  other arithmetic  16.8 us (5%)
  loops' own time  15.8 us (5%)
  between operations  13.7 us (4%)
  starting transfers between devices  4.77 us (2%)
    all_gather x1, waiting for transfers between devices, on_device(): lax.all_gather(prefix_key_values, ('req', 'exp'), axis=1, tiled=True)  97.2 us
    all_to_all x1, blocking collectives, on_device(): lax.all_to_all(outgoing, 'exp', split_axis=0, concat_axis=0, tiled=True)  38.4 us
    all_to_all x1, waiting for transfers between devices, on_device(): lax.all_to_all(computed, 'exp', split_axis=0, concat_axis=0, tiled=True)  31.1 us
    another operation x1, loops' own time, on_device(): lax.scan(step, running, jnp.arange(suffix_length // rows_in_block))  15.8 us
    slice x8, local copies, waits for them, and re-layouts, step(): section[1]  11.2 us
    dot_general x9, matrix products, attend_keys(): jnp.einsum('gjtr,rgd->gjtd', weights.astype(jnp.bfloat16), value_matrix_r...  11.1 us
    dynamic_slice x8, local copies, waits for them, and re-layouts, on_device(): lax.scan(step, running, jnp.arange(suffix_length // rows_in_block))  10.2 us
    dot_general x1, matrix products, on_device(): jnp.dot(active, down_experts[0], preferred_element_type=jnp.float32)  9.06 us
  transfers between devices with their start and end apart: 3, of which 2 were waited for; matrix products, arithmetic and copies ran while one was open for 21% of the time, Pallas kernels for 0%

commit v1 on v0

--- a/solution.py
+++ b/solution.py
@@ -4,6 +4,8 @@
 import jax.numpy as jnp
 from jax import lax
 from jax.sharding import PartitionSpec as P
+from jax.experimental import pallas as pl
+from jax.experimental.pallas import tpu as pltpu
 
 QUERY_HEADS = 12
 KEY_VALUE_HEADS = 2
@@ -14,24 +16,65 @@
 MASKED_SCORE = -1e30
 
 
-def attend_keys(softmax_state, query_head_rows, key_matrix_rows, value_matrix_rows, allowed):
-    row_peak, row_total, summed = softmax_state
-    scores = jnp.einsum(
-        "tgjd,rgd->gjtr", query_head_rows, key_matrix_rows, preferred_element_type=jnp.float32
-    ) * (1.0 / math.sqrt(query_head_rows.shape[3]))
-    if allowed is not None:
-        scores = jnp.where(allowed, scores, MASKED_SCORE)
-    new_peak = jnp.maximum(row_peak, jnp.max(scores, axis=3))
-    weights = jnp.exp(scores - new_peak[..., None])
-    rescale = jnp.exp(row_peak - new_peak)
-    row_total = row_total * rescale + jnp.sum(weights, axis=3)
-    summed = summed * rescale[..., None] + jnp.einsum(
-        "gjtr,rgd->gjtd",
-        weights.astype(jnp.bfloat16),
-        value_matrix_rows,
-        preferred_element_type=jnp.float32,
-    )
-    return (new_peak, row_total, summed)
+def attention_kernel(rid_col_ref, rid_row_ref, q_ref, pkv_ref, skv_ref, out_ref):
+    local_count = q_ref.shape[0]
+    scale = 1.0 / math.sqrt(HEAD_SIZE)
+    position = lax.broadcasted_iota(jnp.int32, (local_count, local_count), 0)
+    key_position = lax.broadcasted_iota(jnp.int32, (local_count, local_count), 1)
+    allowed = (rid_col_ref[...] == rid_row_ref[...]) & (position >= key_position)
+    prefix_keys = pkv_ref[0]
+    prefix_values = pkv_ref[1]
+    suffix_keys = skv_ref[0]
+    suffix_values = skv_ref[1]
+    contract = (((1,), (1,)), ((), ()))
+    for head in range(QUERY_HEADS // KEY_VALUE_HEADS):
+        columns = slice(head * HEAD_SIZE, (head + 1) * HEAD_SIZE)
+        query_rows = q_ref[:, columns]
+        prefix_scores = (
+            lax.dot_general(query_rows, prefix_keys, contract, preferred_element_type=jnp.float32)
+            * scale
+        )
+        suffix_scores = (
+            lax.dot_general(query_rows, suffix_keys, contract, preferred_element_type=jnp.float32)
+            * scale
+        )
+        suffix_scores = jnp.where(allowed, suffix_scores, MASKED_SCORE)
+        peak = jnp.maximum(
+            jnp.max(prefix_scores, axis=1, keepdims=True),
+            jnp.max(suffix_scores, axis=1, keepdims=True),
+        )
+        prefix_weights = jnp.exp(prefix_scores - peak)
+        suffix_weights = jnp.where(allowed, jnp.exp(suffix_scores - peak), 0.0)
+        total = jnp.sum(prefix_weights, axis=1, keepdims=True) + jnp.sum(
+            suffix_weights, axis=1, keepdims=True
+        )
+        summed = jnp.dot(
+            prefix_weights.astype(jnp.bfloat16), prefix_values, preferred_element_type=jnp.float32
+        ) + jnp.dot(
+            suffix_weights.astype(jnp.bfloat16), suffix_values, preferred_element_type=jnp.float32
+        )
+        out_ref[:, columns] = (summed / total).astype(out_ref.dtype)
+
+
+def attend(queries, prefix_key_values, suffix_key_values, request_ids):
+    local_count, model_width = queries.shape
+    prefix_count = prefix_key_values.shape[1]
+    group_width = model_width // KEY_VALUE_HEADS
+    return pl.pallas_call(
+        attention_kernel,
+        grid=(KEY_VALUE_HEADS,),
+        in_specs=[
+            pl.BlockSpec((local_count, 1), lambda g: (0, 0)),
+            pl.BlockSpec((1, local_count), lambda g: (0, 0)),
+            pl.BlockSpec((local_count, group_width), lambda g: (0, g)),
+            pl.BlockSpec((2, prefix_count, HEAD_SIZE), lambda g: (0, 0, g)),
+            pl.BlockSpec((2, local_count, HEAD_SIZE), lambda g: (0, 0, g)),
+        ],
+        out_specs=pl.BlockSpec((local_count, group_width), lambda g: (0, g)),
+        out_shape=jax.ShapeDtypeStruct((local_count, model_width), jnp.bfloat16),
+        compiler_params=pltpu.CompilerParams(vmem_limit_bytes=48 * 1024 * 1024),
+    )(request_ids.reshape(local_count, 1), request_ids.reshape(1, local_count), queries,
+      prefix_key_values, suffix_key_values)
 
 
 def on_device(
@@ -50,39 +93,12 @@
 ):
     local_count = queries.shape[0]
     model_width = queries.shape[1]
-    queries_per_group = QUERY_HEADS // KEY_VALUE_HEADS
-    query_head_rows = queries.reshape(local_count, KEY_VALUE_HEADS, queries_per_group, HEAD_SIZE)
-    segment = request_ids[0]
-    position = jnp.arange(local_count, dtype=jnp.int32)
-    allowed = (segment[:, None] == segment[None, :]) & (position[:, None] >= position[None, :])
-    start_state = (
-        jnp.full((KEY_VALUE_HEADS, queries_per_group, local_count), MASKED_SCORE, jnp.float32),
-        jnp.zeros((KEY_VALUE_HEADS, queries_per_group, local_count), jnp.float32),
-        jnp.zeros((KEY_VALUE_HEADS, queries_per_group, local_count, HEAD_SIZE), jnp.float32),
-    )
-    local_keys = suffix_key_values[0].reshape(local_count, KEY_VALUE_HEADS, HEAD_SIZE)
-    local_values = suffix_key_values[1].reshape(local_count, KEY_VALUE_HEADS, HEAD_SIZE)
-    softmax_state = attend_keys(start_state, query_head_rows, local_keys, local_values, allowed)
-    running = softmax_state
-    slice_part = lax.all_gather(prefix_key_values, ("req", "exp"), axis=1, tiled=True)
-    suffix_length = slice_part.shape[1]
-    rows_in_block = 512
-    mask_blocked = slice_part.reshape(
-        2, suffix_length // rows_in_block, rows_in_block, KEY_VALUE_HEADS, HEAD_SIZE
-    )
-
-    def step(running_inner, block_index):
-        section = lax.dynamic_index_in_dim(mask_blocked, block_index, 1, keepdims=False)
-        return (attend_keys(running_inner, query_head_rows, section[0], section[1], None), None)
-
-    running, unused = lax.scan(step, running, jnp.arange(suffix_length // rows_in_block))
-    softmax_state = running
-    row_peak, row_total, summed = softmax_state
-    attended = (
-        jnp.transpose(summed / row_total[..., None], (2, 0, 1, 3))
-        .reshape(local_count, model_width)
-        .astype(jnp.bfloat16)
-    )
+    exp_count = lax.axis_size("exp")
+    by_req = lax.all_gather(prefix_key_values, "req", axis=1, tiled=True)
+    spread = jnp.broadcast_to(by_req[:, None], (2, exp_count) + by_req.shape[1:])
+    gathered = lax.all_to_all(spread, "exp", split_axis=1, concat_axis=1, tiled=True)
+    all_prefix = gathered.reshape(2, exp_count * by_req.shape[1], by_req.shape[2])
+    attended = attend(queries, all_prefix, suffix_key_values, request_ids)
     section = attended
     projected = jnp.dot(
         section,

time: 310 us -> 236 us (0.76)
  waiting for transfers between devices: 130 us -> 75 us
  local copies, waits for them, and re-layouts: 57.1 us -> 28.1 us
  blocking collectives: 38.4 us -> 61.8 us
  matrix products: 31.8 us -> 15.7 us
  loops' own time: 15.8 us -> 0 us
  Pallas kernels: 0 us -> 14.3 us
  starting transfers between devices: 4.77 us -> 18.4 us
  other arithmetic: 16.8 us -> 8.44 us
    all_gather x1 -> x0, waiting for transfers between devices: 97.2 us -> none  [on_device(): lax.all_gather(prefix_key_values, ('req', 'exp'), axis=1, tiled=True)]
    all_to_all x0 -> x1, waiting for transfers between devices: none -> 43.2 us  [on_device(): lax.all_to_all(spread, 'exp', split_axis=1, concat_axis=1, tiled=True)]
    all_gather x0 -> x1, blocking collectives: none -> 24 us  [on_device(): by_req = lax.all_gather(prefix_key_values, 'req', axis=1, tiled=True)]
    dot_general x18 -> x0, matrix products: 16.1 us -> none  [the longest x9 11.1 us: attend_keys(): jnp.einsum('gjtr,rgd->gjtd', weights.astype(jnp.bfloat16), value_matrix_r...]
    another operation x1 -> x0, loops' own time: 15.8 us -> none  [on_device(): lax.scan(step, running, jnp.arange(suffix_length // rows_in_block))]
    pallas_call x0 -> x1, Pallas kernels: none -> 14.3 us  [attend(): pl.pallas_call(attention_kernel, grid=(KEY_VALUE_HEADS,), in_specs=[pl.Bl...]
    all_to_all x0 -> x1, starting transfers between devices: none -> 13.7 us  [on_device(): lax.all_to_all(spread, 'exp', split_axis=1, concat_axis=1, tiled=True)]
    slice x10 -> x1, local copies, waits for them, and re-layouts: 12.3 us -> 0.22 us  [the longest x8 11.2 us: step(): section[1]]
  transfers between devices with their start and end apart: 3 -> 3, of which waited for: 2 -> 2; matrix products, arithmetic and copies ran while one was open for 21% -> 5% of each run, Pallas kernels for 0% -> 6%
where the time goes in v1:
time: 236 us; the launch traced here: 235 us
  waiting for transfers between devices  75 us (32%)
  blocking collectives  61.8 us (26%)
  local copies, waits for them, and re-layouts  28.1 us (12%)
  starting transfers between devices  18.4 us (8%)
  matrix products  15.7 us (7%)
  Pallas kernels  14.3 us (6%)
  between operations  13.6 us (6%)
  other arithmetic  8.44 us (4%)
    all_to_all x1, waiting for transfers between devices, on_device(): lax.all_to_all(spread, 'exp', split_axis=1, concat_axis=1, tiled=True)  43.2 us
    all_to_all x1, blocking collectives, on_device(): lax.all_to_all(outgoing, 'exp', split_axis=0, concat_axis=0, tiled=True)  37.8 us
    all_to_all x1, waiting for transfers between devices, on_device(): lax.all_to_all(computed, 'exp', split_axis=0, concat_axis=0, tiled=True)  31.1 us
    all_gather x1, blocking collectives, on_device(): by_req = lax.all_gather(prefix_key_values, 'req', axis=1, tiled=True)  24 us
    pallas_call x1, Pallas kernels, attend(): pl.pallas_call(attention_kernel, grid=(KEY_VALUE_HEADS,), in_specs=[pl.Bl...  14.3 us
    all_to_all x1, starting transfers between devices, on_device(): lax.all_to_all(spread, 'exp', split_axis=1, concat_axis=1, tiled=True)  13.7 us
    dot_general x1, matrix products, on_device(): jnp.dot(active, down_experts[0], preferred_element_type=jnp.float32)  9.06 us
    gather x1, local copies, waits for them, and re-layouts, on_device(): returned.reshape(expert_count * capacity, model_width)[slot_of_route]  6.42 us
  transfers between devices with their start and end apart: 3, of which 2 were waited for; matrix products, arithmetic and copies ran while one was open for 5% of the time, Pallas kernels for 6%

profile of v1, /device:TPU:1, one launch (start us, length us, event | category | flops | bytes accessed | tf_op | source)
XLA Modules:
  0.0 235.4 jit_solution(15840451891211241940)
XLA Ops:
  6.5 0.0 copy-start
  6.5 0.0 all-gather.2.cloned.1.call-start
  6.5 0.7 all-gather.2.cloned.1.call-update
  7.3 24.0 %all_gather.6 = bf16[2,128,256]{2,1,0:T(8,128)(2,1)S(1)} all-gather(bf16[2,16,256]{2,1,0:T(8,128)(2,1)} %param.15), channel_id=1, replica_groups=mesh['req'=8,'exp'=32] {'req'}, dimensions={1}, use_global_device_ids=true | all-gather | bytes 147456 | tf_op jit(solution)/shard_map/all_gather | solution.py:97
  31.2 2.5 %broadcast_in_dim.22 = bf16[2,32,128,256]{3,2,0,1:T(8,128)(2,1)} broadcast(bf16[2,128,256]{2,1,0:T(8,128)(2,1)S(1)} %all_gather.6), dimensions={0,2,3} | broadcast | bytes 4325376 | tf_op jit(solution)/shard_map/broadcast_in_dim | solution.py:98
  33.7 13.7 %all-to-all-start = ((bf16[2,32,128,256]{3,2,0,1:T(8,128)(2,1)}), bf16[2,32,128,256]{3,2,0,1:T(8,128)(2,1)}, u32[]{:S(2)}, u32[]{:S(2)}) async-start(bf16[2,32,128,256]{3,2,0,1:T(8,128)(2,1)} %broadcast_in_dim.22), calls=%async_computation | async-start | bytes 8388608 | tf_op jit(solution)/shard_map/all_to_all | solution.py:99
  47.4 0.0 copy-done.8
  47.4 0.1 copy.24
  47.5 0.1 eq.29
  47.7 0.1 eq.25
  47.8 1.2 reduce-window.6
  48.9 0.2 slice_reduce_fusion
  49.2 0.1 copy.23
  49.3 0.1 mul.51
  49.4 0.0 copy-done.3
  49.5 0.1 copy.22.rid_col_ref
  49.6 0.1 fusion.10
  49.7 2.4 %scatter_custom_fusion.1 = s32[768]{0:T(1024)S(1)} fusion(s32[512]{0:T(512)S(1)} %bitcast.46, s32[512]{0:T(512)S(1)} %add_select_fusion, s32[]{:T(128)} %constant.18.clone.1), kind=kCustom, calls=%fused_computation.35 | custom fusion | bytes 3076 | tf_op jit(solution)/shard_map/scatter | solution.py:124
  52.2 2.6 %scatter_custom_fusion = pred[768]{0:T(1024)(128)(4,1)S(1)} fusion(s32[512]{0:T(512)S(1)} %bitcast.47, pred[512]{0:T(512)(128)(4,1)S(1)} %broadcast.89, pred[]{:T(512)} %constant.15.clone.1), kind=kCustom, calls=%fused_computation.38 | custom fusion | bytes 769 | tf_op jit(solution)/shard_map/scatter | solution.py:126
  54.8 0.1 broadcast_in_dim.40
  54.9 0.0 copy-start.1
  54.9 0.0 copy-start.2
  54.9 43.2 %all-to-all-done = bf16[2,32,128,256]{3,2,0,1:T(8,128)(2,1)} async-done(((bf16[2,32,128,256]{3,2,0,1:T(8,128)(2,1)}), bf16[2,32,128,256]{3,2,0,1:T(8,128)(2,1)}, u32[]{:S(2)}, u32[]{:S(2)}) %all-to-all-start) | async-done | bytes 4194336 | tf_op jit(solution)/shard_map/all_to_all | solution.py:99
  98.1 2.7 %copy.21 = bf16[2,32,128,256]{3,2,1,0:T(8,128)(2,1)S(1)} copy(bf16[2,32,128,256]{3,2,0,1:T(8,128)(2,1)} %all-to-all-done) | data formatting | bytes 8388608 | tf_op jit(solution)/shard_map/all_to_all | solution.py:99
  100.8 0.0 copy-done.1
  100.8 14.3 %shard_map.118 = bf16[128,1536]{1,0:T(8,128)(2,1)S(1)} custom-call(s32[128,1]{1,0:T(8,128)S(1)} %copy.22.rid_col_ref, s32[1,128]{1,0:T(1,128)S(1)} %copy-done.3, bf16[128,1536]{1,0:T(8,128)(2,1)S(1)} %copy-done.1, bf16[2,4096,256]{2,1,0:T(8,128)(2,1)S(1)} %bitcast.40, bf16[2,128,256]{2,1,0:T(8,128)(2,1)S(1)} %copy-done.2), custom_call_target="tpu_custom_call" | custom-call | tf_op jit(solution)/shard_map/pallas_call | solution.py:63
  115.1 0.0 copy-start.7
  115.1 0.0 all-gather.2.cloned.1.call-done
  115.2 3.3 %multiply_reduce_fusion.1 = (f32[128]{0:T(128)S(1)}, f32[128,1536]{1,0:T(8,128)S(1)}) fusion(bf16[128,1536]{1,0:T(8,128)(2,1)S(1)} %shard_map.118, bf16[1536,1536]{1,0:T(8,128)(2,1)} %all-gather.2.cloned.1.call-done, bf16[128,1536]{1,0:T(8,128)(2,1)} %param.12), kind=kOutput, calls=%fused_computation.16 | convolution fusion | flops 604766080 | bytes 6291968 | tf_op jit(solution)/shard_map/dot_general | solution.py:103
  118.5 0.9 copy-done.4
  119.3 0.0 copy-done.7
  119.3 0.1 multiply_convert_fusion.1
  119.5 3.8 %gather_fusion = bf16[768,1536]{1,0:T(8,128)(2,1)} fusion(bf16[128,1536]{1,0:T(8,128)(2,1)S(1)} %multiply_convert_fusion.1, s32[1024]{0:T(1024)S(1)} %pad_clamp_fusion.1), kind=kCustom, calls=%fused_computation | custom fusion | bytes 4721664 | tf_op jit(solution)/shard_map/gather | solution.py:127
  123.3 1.9 broadcast_select_fusion
  125.2 0.0 copy-start.10
  125.2 37.8 %all_to_all.15 = bf16[32,24,1536]{2,1,0:T(8,128)(2,1)S(1)} all-to-all(bf16[32,24,1536]{2,1,0:T(8,128)(2,1)S(1)} %broadcast_select_fusion), channel_id=1, replica_groups=mesh['req'=8,'exp'=32] {'exp'}, dimensions={0} | all-to-all | bytes 4718592 | tf_op jit(solution)/shard_map/all_to_all | solution.py:130
  163.0 1.4 copy-done.6
  164.5 3.4 %fusion.1 = f32[768,768]{1,0:T(8,128)} fusion(bf16[768,1536]{1,0:T(8,128)(2,1)S(1)} %bitcast.44, bf16[1,1536,768]{2,1,0:T(8,128)(2,1)S(1)} %copy-done.10), kind=kOutput, calls=%fused_computation.8 | convolution fusion | flops 1811939328 | bytes 7077888 | tf_op jit(solution)/shard_map/dot_general | solution.py:134
  167.9 9.1 %convolution_convert_fusion = bf16[768,1536]{1,0:T(8,128)(2,1)} fusion(bf16[1,768,1536]{2,1,0:T(8,128)(2,1)S(1)} %copy-done, f32[768,768]{1,0:T(8,128)} %fusion.1, bf16[768,1536]{1,0:T(8,128)(2,1)} %bitcast.45, bf16[1,1536,768]{2,1,0:T(8,128)(2,1)} %param.21), kind=kOutput, calls=%fused_computation.4 | convolution fusion | flops 3626827776 | bytes 11796480 | tf_op jit(solution)/shard_map/dot_general | solution.py:136
  176.9 4.7 %all-to-all-start.2 = ((bf16[32,24,1536]{2,1,0:T(8,128)(2,1)}), bf16[32,24,1536]{2,1,0:T(8,128)(2,1)}, u32[]{:S(2)}, u32[]{:S(2)}) async-start(bf16[32,24,1536]{2,1,0:T(8,128)(2,1)} %bitcast.43), calls=%async_computation.2 | async-start | bytes 4718592 | tf_op jit(solution)/shard_map/all_to_all | solution.py:140
  181.6 0.0 copy-done.9
  181.7 0.1 copy.27
  181.8 31.1 %all-to-all-done.2 = bf16[32,24,1536]{2,1,0:T(8,128)(2,1)} async-done(((bf16[32,24,1536]{2,1,0:T(8,128)(2,1)}), bf16[32,24,1536]{2,1,0:T(8,128)(2,1)}, u32[]{:S(2)}, u32[]{:S(2)}) %all-to-all-start.2) | async-done | bytes 2359328 | tf_op jit(solution)/shard_map/all_to_all | solution.py:140
  212.9 6.4 %gather_fusion.1 = bf16[512,1536]{1,0:T(8,128)(2,1)} fusion(bf16[768,1536]{1,0:T(8,128)(2,1)} %bitcast.11, s32[1024]{0:T(1024)S(1)} %pad_clamp_fusion), kind=kCustom, calls=%fused_computation.1 | custom fusion | bytes 3147776 | tf_op jit(solution)/shard_map/gather | solution.py:141
  219.3 4.2 %reshape.91 = f32[128,4,1536]{2,1,0:T(4,128)} reshape(bf16[512,1536]{1,0:T(8,128)(2,1)} %gather_fusion.1) | data formatting | bytes 4718592 | tf_op jit(solution)/shard_map/convert_element_type | solution.py:144
  223.5 4.2 %multiply_reduce_fusion = f32[128,1536]{1,0:T(8,128)S(1)} fusion(f32[128,4,1536]{2,1,0:T(4,128)} %reshape.91, f32[128,4]{1,0:T(8,128)S(1)} %copy.27), kind=kLoop, calls=%fused_computation.5 | loop fusion | flops 1376256 | bytes 3934208 | tf_op jit(solution)/shard_map/reduce_sum | solution.py:144
  227.7 0.0 copy-done.5
  227.7 0.8 add_convert_fusion
  (20 shorter events, 0.1 us)
Async XLA Ops:
  6.5 161.3 %copy-start = (bf16[1,768,1536]{2,1,0:T(8,128)(2,1)S(1)}, bf16[1,768,1536]{2,1,0:T(8,128)(2,1)}, u32[]{:S(2)}) copy-start(bf16[1,768,1536]{2,1,0:T(8,128)(2,1)} %param.23) | copy-start | bytes 7077892
  6.5 108.6 %all-gather.2.cloned.1.call-start = ((), (), s32[]{:S(2)}) async-start(), calls=%async_computation.3 | async-start | bytes 5308416 | tf_op jit(solution)/shard_map/all_gather | solution.py:105
  33.7 13.7 %copy-start.8 = (s32[128,4]{0,1:T(4,128)S(1)}, s32[128,4]{0,1:T(4,128)}, u32[]{:S(2)}) copy-start(s32[128,4]{0,1:T(4,128)} %param.19) | copy-start | bytes 6148
  33.7 15.7 %copy-start.3 = (s32[1,128]{1,0:T(1,128)S(1)}, s32[1,128]{1,0:T(1,128)}, u32[]{:S(2)}) copy-start(s32[1,128]{1,0:T(1,128)} %rid_row_ref.1) | copy-start | bytes 1540
  33.7 64.4 %all-to-all-start = ((bf16[2,32,128,256]{3,2,0,1:T(8,128)(2,1)}), bf16[2,32,128,256]{3,2,0,1:T(8,128)(2,1)}, u32[]{:S(2)}, u32[]{:S(2)}) async-start(bf16[2,32,128,256]{3,2,0,1:T(8,128)(2,1)} %broadcast_in_dim.22), calls=%async_computation | async-start | bytes 8388608 | tf_op jit(solution)/shard_map/all_to_all | solution.py:99
  54.9 45.9 %copy-start.1 = (bf16[128,1536]{1,0:T(8,128)(2,1)S(1)}, bf16[128,1536]{1,0:T(8,128)(2,1)}, u32[]{:S(2)}) copy-start(bf16[128,1536]{1,0:T(8,128)(2,1)} %q_ref.1) | copy-start | bytes 1179652
  54.9 45.9 %copy-start.2 = (bf16[2,128,256]{2,1,0:T(8,128)(2,1)S(1)}, bf16[2,128,256]{2,1,0:T(8,128)(2,1)}, u32[]{:S(2)}) copy-start(bf16[2,128,256]{2,1,0:T(8,128)(2,1)} %skv_ref.1) | copy-start | bytes 393220
  115.1 4.2 %copy-start.7 = (f32[1536]{0:T(1024)S(1)}, f32[1536]{0:T(1024)}, u32[]{:S(2)}) copy-start(f32[1536]{0:T(1024)} %param.18) | copy-start | bytes 18436
  118.5 0.9 copy-start.4
  125.2 39.3 %copy-start.10 = (bf16[1,1536,768]{2,1,0:T(8,128)(2,1)S(1)}, bf16[1,1536,768]{2,1,0:T(8,128)(2,1)}, u32[]{:S(2)}) copy-start(bf16[1,1536,768]{2,1,0:T(8,128)(2,1)} %param.22) | copy-start | bytes 7077892
  163.0 1.4 copy-start.6
  176.9 4.7 %copy-start.9 = (f32[128,4]{0,1:T(4,128)S(1)}, f32[128,4]{0,1:T(4,128)}, u32[]{:S(2)}) copy-start(f32[128,4]{0,1:T(4,128)} %param.20) | copy-start | bytes 6148
  176.9 36.0 %all-to-all-start.2 = ((bf16[32,24,1536]{2,1,0:T(8,128)(2,1)}), bf16[32,24,1536]{2,1,0:T(8,128)(2,1)}, u32[]{:S(2)}, u32[]{:S(2)}) async-start(bf16[32,24,1536]{2,1,0:T(8,128)(2,1)} %bitcast.43), calls=%async_computation.2 | async-start | bytes 4718592 | tf_op jit(solution)/shard_map/all_to_all | solution.py:140
  223.5 4.3 %copy-start.5 = (f32[128,1536]{1,0:T(8,128)S(1)}, f32[128,1536]{1,0:T(8,128)}, u32[]{:S(2)}) copy-start(f32[128,1536]{1,0:T(8,128)} %copy-done.4) | copy-start | bytes 2359300
Sparse Core Ops, SparseCore 0:
  9.1 63.7 all-gather.1

commit v2 on v1

--- a/solution.py
+++ b/solution.py
@@ -94,7 +94,14 @@
     local_count = queries.shape[0]
     model_width = queries.shape[1]
     exp_count = lax.axis_size("exp")
-    by_req = lax.all_gather(prefix_key_values, "req", axis=1, tiled=True)
+    req_count = lax.axis_size("req")
+    by_req = lax.all_to_all(
+        jnp.broadcast_to(prefix_key_values[:, None], (2, req_count) + prefix_key_values.shape[1:]),
+        "req",
+        split_axis=1,
+        concat_axis=1,
+        tiled=True,
+    ).reshape(2, req_count * prefix_key_values.shape[1], prefix_key_values.shape[2])
     spread = jnp.broadcast_to(by_req[:, None], (2, exp_count) + by_req.shape[1:])
     gathered = lax.all_to_all(spread, "exp", split_axis=1, concat_axis=1, tiled=True)
     all_prefix = gathered.reshape(2, exp_count * by_req.shape[1], by_req.shape[2])
@@ -117,15 +124,13 @@
     )
     slot_rank = jnp.sum((jnp.cumsum(matches, axis=0) - 1) * matches, axis=1)
     slot_of_route = flat_routes * capacity + slot_rank
-    route_index = jnp.arange(flat_routes.shape[0], dtype=jnp.int32)
-    sources = (
-        jnp.zeros((expert_count * capacity,), jnp.int32)
-        .at[slot_of_route]
-        .set(route_index // top_count)
-    )
-    filled = jnp.zeros((expert_count * capacity,), jnp.bool_).at[slot_of_route].set(True)
-    outgoing = jnp.where(filled[:, None], normed[sources], jnp.zeros((), jnp.bfloat16)).reshape(
-        expert_count, capacity, model_width
+    slot_ids = jnp.arange(expert_count * capacity, dtype=jnp.int32)
+    hit = slot_of_route.reshape(local_count, top_count)[:, :, None] == slot_ids[None, None, :]
+    dispatch = jnp.any(hit, axis=1).astype(jnp.bfloat16)
+    outgoing = (
+        jnp.einsum("ts,tf->sf", dispatch, normed, preferred_element_type=jnp.float32)
+        .astype(jnp.bfloat16)
+        .reshape(expert_count, capacity, model_width)
     )
     slot_rows = lax.all_to_all(outgoing, "exp", split_axis=0, concat_axis=0, tiled=True)
     senders, slot_count, features = slot_rows.shape
@@ -138,10 +143,13 @@
     )
     computed = produced.reshape(senders, slot_count, features)
     returned = lax.all_to_all(computed, "exp", split_axis=0, concat_axis=0, tiled=True)
-    picked = returned.reshape(expert_count * capacity, model_width)[slot_of_route].reshape(
-        local_count, top_count, model_width
+    slot_gates = jnp.sum(jnp.where(hit, route_gates[:, :, None], 0.0), axis=1)
+    combined = jnp.dot(
+        slot_gates,
+        returned.reshape(expert_count * capacity, model_width).astype(jnp.float32),
+        precision=lax.Precision.HIGHEST,
+        preferred_element_type=jnp.float32,
     )
-    combined = jnp.sum(picked.astype(jnp.float32) * route_gates[:, :, None], axis=1)
     return (stream + combined).astype(jnp.bfloat16)
 
 

time: 236 us -> 207 us (0.88)
  local copies, waits for them, and re-layouts: 28.1 us -> 8.24 us
  blocking collectives: 61.8 us -> 54.4 us
  other arithmetic: 8.44 us -> 1.85 us
  waiting for transfers between devices: 75 us -> 79.9 us
  matrix products: 15.7 us -> 20.1 us
  starting transfers between devices: 18.4 us -> 14.3 us
    all_gather x1 -> x0, blocking collectives: 24 us -> none  [on_device(): by_req = lax.all_gather(prefix_key_values, 'req', axis=1, tiled=True)]
    all_to_all x0 -> x1, blocking collectives: none -> 16.6 us  [on_device(): lax.all_to_all(jnp.broadcast_to(prefix_key_values[:, None], (2, req_count...]
    gather x2 -> x0, local copies, waits for them, and re-layouts: 10.2 us -> none  [the longest x1 6.42 us: on_device(): returned.reshape(expert_count * capacity, model_width)[slot_of_route]]
    scatter x2 -> x0, local copies, waits for them, and re-layouts: 5.07 us -> none  [the longest x1 2.63 us: on_device(): jnp.zeros((expert_count * capacity,), jnp.bool_).at[slot_of_route].set(True)]
    all_to_all x1, waiting for transfers between devices: 43.2 us -> 48.1 us  [on_device(): lax.all_to_all(spread, 'exp', split_axis=1, concat_axis=1, tiled=True)]
    dot_general x0 -> x2, matrix products: none -> 4.37 us  [the longest x1 3.51 us: on_device(): jnp.dot(slot_gates, returned.reshape(expert_count * capacity, model_width...]
    convert_element_type x1 -> x0, local copies, waits for them, and re-layouts: 4.19 us -> none  [on_device(): picked.astype(jnp.float32) * route_gates[:, :, None]]
    all_to_all x1, starting transfers between devices: 13.7 us -> 9.57 us  [on_device(): lax.all_to_all(spread, 'exp', split_axis=1, concat_axis=1, tiled=True)]
  transfers between devices with their start and end apart: 3 -> 3, of which waited for: 2 -> 2; matrix products, arithmetic and copies ran while one was open for 5% -> 4% of each run, Pallas kernels for 6% -> 7%
where the time goes in v2:
time: 207 us
  waiting for transfers between devices  79.9 us (39%)
  blocking collectives  54.4 us (26%)
  matrix products  20.1 us (10%)
  starting transfers between devices  14.3 us (7%)
  Pallas kernels  14.3 us (7%)
  between operations  13.6 us (7%)
  local copies, waits for them, and re-layouts  8.24 us (4%)
    all_to_all x1, waiting for transfers between devices, on_device(): lax.all_to_all(spread, 'exp', split_axis=1, concat_axis=1, tiled=True)  48.1 us
    all_to_all x1, blocking collectives, on_device(): lax.all_to_all(outgoing, 'exp', split_axis=0, concat_axis=0, tiled=True)  37.8 us
    all_to_all x1, waiting for transfers between devices, on_device(): lax.all_to_all(computed, 'exp', split_axis=0, concat_axis=0, tiled=True)  31 us
    all_to_all x1, blocking collectives, on_device(): lax.all_to_all(jnp.broadcast_to(prefix_key_values[:, None], (2, req_count...  16.6 us
    pallas_call x1, Pallas kernels, attend(): pl.pallas_call(attention_kernel, grid=(KEY_VALUE_HEADS,), in_specs=[pl.Bl...  14.3 us
    all_to_all x1, starting transfers between devices, on_device(): lax.all_to_all(spread, 'exp', split_axis=1, concat_axis=1, tiled=True)  9.57 us
    dot_general x1, matrix products, on_device(): jnp.dot(active, down_experts[0], preferred_element_type=jnp.float32)  9.06 us
    all_to_all x1, starting transfers between devices, on_device(): lax.all_to_all(computed, 'exp', split_axis=0, concat_axis=0, tiled=True)  4.73 us
  transfers between devices with their start and end apart: 3, of which 2 were waited for; matrix products, arithmetic and copies ran while one was open for 4% of the time, Pallas kernels for 7%

profile of v2, /device:TPU:1, one launch (start us, length us, event | category | flops | bytes accessed | tf_op | source)
XLA Modules:
  0.0 206.6 jit_solution(401252910114610982)
XLA Ops:
  6.5 0.0 copy-start
  6.5 0.0 all-gather.2.cloned.1.call-start
  6.5 0.7 all-gather.2.cloned.1.call-update
  7.3 0.7 broadcast_in_dim.14
  8.0 16.6 %all_to_all.20 = bf16[2,8,16,256]{3,2,0,1:T(8,128)(2,1)S(1)} all-to-all(bf16[2,8,16,256]{3,2,0,1:T(8,128)(2,1)S(1)} %broadcast_in_dim.14), channel_id=1, replica_groups=mesh['req'=8,'exp'=32] {'req'}, dimensions={1} | all-to-all | bytes 262144 | tf_op jit(solution)/shard_map/all_to_all | solution.py:98
  24.6 2.5 %broadcast_in_dim.32 = bf16[2,32,128,256]{3,2,0,1:T(8,128)(2,1)} broadcast(bf16[2,128,256]{2,1,0:T(8,128)(2,1)S(1)} %bitcast.48), dimensions={0,2,3} | broadcast | bytes 4325376 | tf_op jit(solution)/shard_map/broadcast_in_dim | solution.py:105
  27.1 0.0 copy-start.8
  27.1 0.0 copy-start.3
  27.1 9.6 %all-to-all-start.1 = ((bf16[2,32,128,256]{3,2,0,1:T(8,128)(2,1)}), bf16[2,32,128,256]{3,2,0,1:T(8,128)(2,1)}, u32[]{:S(2)}, u32[]{:S(2)}) async-start(bf16[2,32,128,256]{3,2,0,1:T(8,128)(2,1)} %broadcast_in_dim.32), calls=%async_computation.1 | async-start | bytes 8388608 | tf_op jit(solution)/shard_map/all_to_all | solution.py:106
  36.6 0.0 copy-done.8
  36.6 0.1 copy.52
  36.8 0.1 eq.38
  36.9 0.1 eq.42
  37.0 0.0 copy-done.3
  37.0 0.1 copy.51.rid_col_ref
  37.1 1.2 reduce-window.6
  38.3 0.2 slice_reduce_fusion
  38.5 0.1 fusion.14
  38.7 0.1 reduce_sum.30
  38.8 0.1 copy.55
  38.8 0.3 fusion.8
  39.1 0.0 copy-start.1
  39.2 0.0 copy-start.2
  39.2 48.1 %all-to-all-done.1 = bf16[2,32,128,256]{3,2,0,1:T(8,128)(2,1)} async-done(((bf16[2,32,128,256]{3,2,0,1:T(8,128)(2,1)}), bf16[2,32,128,256]{3,2,0,1:T(8,128)(2,1)}, u32[]{:S(2)}, u32[]{:S(2)}) %all-to-all-start.1) | async-done | bytes 4194336 | tf_op jit(solution)/shard_map/all_to_all | solution.py:106
  87.3 2.7 %copy.50 = bf16[2,32,128,256]{3,2,1,0:T(8,128)(2,1)S(1)} copy(bf16[2,32,128,256]{3,2,0,1:T(8,128)(2,1)} %all-to-all-done.1) | data formatting | bytes 8388608 | tf_op jit(solution)/shard_map/all_to_all | solution.py:106
  90.0 0.0 copy-done.1
  90.0 0.0 copy-done.2
  90.0 14.3 %shard_map.118 = bf16[128,1536]{1,0:T(8,128)(2,1)S(1)} custom-call(s32[128,1]{1,0:T(8,128)S(1)} %copy.51.rid_col_ref, s32[1,128]{1,0:T(1,128)S(1)} %copy-done.3, bf16[128,1536]{1,0:T(8,128)(2,1)S(1)} %copy-done.1, bf16[2,4096,256]{2,1,0:T(8,128)(2,1)S(1)} %bitcast.42, bf16[2,128,256]{2,1,0:T(8,128)(2,1)S(1)} %copy-done.2), custom_call_target="tpu_custom_call" | custom-call | tf_op jit(solution)/shard_map/pallas_call | solution.py:63
  104.3 0.0 copy-start.7
  104.3 0.0 all-gather.2.cloned.1.call-done
  104.4 3.3 %multiply_reduce_fusion = (f32[128]{0:T(128)S(1)}, f32[128,1536]{1,0:T(8,128)S(1)}) fusion(bf16[128,1536]{1,0:T(8,128)(2,1)S(1)} %shard_map.118, bf16[1536,1536]{1,0:T(8,128)(2,1)} %all-gather.2.cloned.1.call-done, bf16[128,1536]{1,0:T(8,128)(2,1)} %param.12), kind=kOutput, calls=%fused_computation.15 | convolution fusion | flops 604766080 | bytes 6291968 | tf_op jit(solution)/shard_map/dot_general | solution.py:110
  107.7 0.0 copy-start.4
  107.7 0.0 copy-done.7
  107.7 0.9 convolution_convert_fusion.1
  108.6 0.0 copy-start.10
  108.6 37.8 %all_to_all.21 = bf16[32,24,1536]{2,1,0:T(8,128)(2,1)S(1)} all-to-all(bf16[32,24,1536]{2,1,0:T(8,128)(2,1)S(1)} %bitcast.44), channel_id=1, replica_groups=mesh['req'=8,'exp'=32] {'exp'}, dimensions={0} | all-to-all | bytes 4718592 | tf_op jit(solution)/shard_map/all_to_all | solution.py:135
  146.4 0.0 copy-done.4
  146.4 1.4 copy-done.6
  147.9 0.0 copy-done.10
  147.9 3.4 %fusion.2 = f32[768,768]{1,0:T(8,128)} fusion(bf16[768,1536]{1,0:T(8,128)(2,1)S(1)} %bitcast.46, bf16[1,1536,768]{2,1,0:T(8,128)(2,1)S(1)} %copy-done.10), kind=kOutput, calls=%fused_computation.6 | convolution fusion | flops 1811939328 | bytes 7077888 | tf_op jit(solution)/shard_map/dot_general | solution.py:139
  151.2 0.0 copy-done
  151.2 9.1 %convolution_convert_fusion = bf16[768,1536]{1,0:T(8,128)(2,1)} fusion(bf16[1,768,1536]{2,1,0:T(8,128)(2,1)S(1)} %copy-done, f32[768,768]{1,0:T(8,128)} %fusion.2, bf16[768,1536]{1,0:T(8,128)(2,1)} %bitcast.47, bf16[1,1536,768]{2,1,0:T(8,128)(2,1)} %param.21), kind=kOutput, calls=%fused_computation | convolution fusion | flops 3626827776 | bytes 11796480 | tf_op jit(solution)/shard_map/dot_general | solution.py:141
  160.3 4.7 %all-to-all-start.3 = ((bf16[32,24,1536]{2,1,0:T(8,128)(2,1)}), bf16[32,24,1536]{2,1,0:T(8,128)(2,1)}, u32[]{:S(2)}, u32[]{:S(2)}) async-start(bf16[32,24,1536]{2,1,0:T(8,128)(2,1)} %bitcast.45), calls=%async_computation.3 | async-start | bytes 4718592 | tf_op jit(solution)/shard_map/all_to_all | solution.py:145
  165.0 0.0 copy-done.9
  165.0 0.2 select_reduce_fusion
  165.3 31.0 %all-to-all-done.3 = bf16[32,24,1536]{2,1,0:T(8,128)(2,1)} async-done(((bf16[32,24,1536]{2,1,0:T(8,128)(2,1)}), bf16[32,24,1536]{2,1,0:T(8,128)(2,1)}, u32[]{:S(2)}, u32[]{:S(2)}) %all-to-all-start.3) | async-done | bytes 2359328 | tf_op jit(solution)/shard_map/all_to_all | solution.py:145
  196.3 0.0 copy-done.5
  196.3 3.5 %fusion = bf16[128,1536]{1,0:T(8,128)(2,1)} fusion(f32[128,1536]{1,0:T(8,128)S(1)} %copy-done.5, f32[128,768]{1,0:T(8,128)S(1)} %select_reduce_fusion, bf16[768,1536]{1,0:T(8,128)(2,1)} %bitcast.10), kind=kOutput, calls=%fused_computation.4 | convolution fusion | flops 1812332544 | bytes 3932160 | tf_op jit(solution)/shard_map/dot_general | solution.py:147
  (9 shorter events, 0.1 us)
Async XLA Ops:
  6.5 144.7 %copy-start = (bf16[1,768,1536]{2,1,0:T(8,128)(2,1)S(1)}, bf16[1,768,1536]{2,1,0:T(8,128)(2,1)}, u32[]{:S(2)}) copy-start(bf16[1,768,1536]{2,1,0:T(8,128)(2,1)} %param.23) | copy-start | bytes 7077892
  6.5 97.8 %all-gather.2.cloned.1.call-start = ((), (), s32[]{:S(2)}) async-start(), calls=%async_computation.4 | async-start | bytes 5308416 | tf_op jit(solution)/shard_map/all_gather | solution.py:112
  27.1 9.6 %copy-start.8 = (s32[128,4]{0,1:T(4,128)S(1)}, s32[128,4]{0,1:T(4,128)}, u32[]{:S(2)}) copy-start(s32[128,4]{0,1:T(4,128)} %param.19) | copy-start | bytes 6148
  27.1 9.9 %copy-start.3 = (s32[1,128]{1,0:T(1,128)S(1)}, s32[1,128]{1,0:T(1,128)}, u32[]{:S(2)}) copy-start(s32[1,128]{1,0:T(1,128)} %rid_row_ref.1) | copy-start | bytes 1540
  27.1 60.3 %all-to-all-start.1 = ((bf16[2,32,128,256]{3,2,0,1:T(8,128)(2,1)}), bf16[2,32,128,256]{3,2,0,1:T(8,128)(2,1)}, u32[]{:S(2)}, u32[]{:S(2)}) async-start(bf16[2,32,128,256]{3,2,0,1:T(8,128)(2,1)} %broadcast_in_dim.32), calls=%async_computation.1 | async-start | bytes 8388608 | tf_op jit(solution)/shard_map/all_to_all | solution.py:106
  39.1 50.9 %copy-start.1 = (bf16[128,1536]{1,0:T(8,128)(2,1)S(1)}, bf16[128,1536]{1,0:T(8,128)(2,1)}, u32[]{:S(2)}) copy-start(bf16[128,1536]{1,0:T(8,128)(2,1)} %q_ref.1) | copy-start | bytes 1179652
  39.2 50.9 %copy-start.2 = (bf16[2,128,256]{2,1,0:T(8,128)(2,1)S(1)}, bf16[2,128,256]{2,1,0:T(8,128)(2,1)}, u32[]{:S(2)}) copy-start(bf16[2,128,256]{2,1,0:T(8,128)(2,1)} %skv_ref.1) | copy-start | bytes 393220
  104.3 3.4 %copy-start.7 = (f32[1536]{0:T(1024)S(1)}, f32[1536]{0:T(1024)}, u32[]{:S(2)}) copy-start(f32[1536]{0:T(1024)} %param.18) | copy-start | bytes 18436
  107.7 38.7 %copy-start.4 = (f32[128,1536]{1,0:T(8,128)}, f32[128,1536]{1,0:T(8,128)S(1)}, u32[]{:S(2)}) copy-start(f32[128,1536]{1,0:T(8,128)S(1)} %get-tuple-element.6) | copy-start | bytes 2359300
  108.6 39.3 %copy-start.10 = (bf16[1,1536,768]{2,1,0:T(8,128)(2,1)S(1)}, bf16[1,1536,768]{2,1,0:T(8,128)(2,1)}, u32[]{:S(2)}) copy-start(bf16[1,1536,768]{2,1,0:T(8,128)(2,1)} %param.22) | copy-start | bytes 7077892
  146.4 1.4 copy-start.6
  160.3 4.7 %copy-start.9 = (f32[128,4]{0,1:T(4,128)S(1)}, f32[128,4]{0,1:T(4,128)}, u32[]{:S(2)}) copy-start(f32[128,4]{0,1:T(4,128)} %param.20) | copy-start | bytes 6148
  160.3 36.0 %copy-start.5 = (f32[128,1536]{1,0:T(8,128)S(1)}, f32[128,1536]{1,0:T(8,128)}, u32[]{:S(2)}) copy-start(f32[128,1536]{1,0:T(8,128)} %copy-done.4) | copy-start | bytes 2359300
  160.3 36.0 %all-to-all-start.3 = ((bf16[32,24,1536]{2,1,0:T(8,128)(2,1)}), bf16[32,24,1536]{2,1,0:T(8,128)(2,1)}, u32[]{:S(2)}, u32[]{:S(2)}) async-start(bf16[32,24,1536]{2,1,0:T(8,128)(2,1)} %bitcast.45), calls=%async_computation.3 | async-start | bytes 4718592 | tf_op jit(solution)/shard_map/all_to_all | solution.py:145
Sparse Core Ops, SparseCore 0:
  9.1 63.2 all-gather.1

commit v3 on v2

--- a/solution.py
+++ b/solution.py
@@ -3,7 +3,7 @@
 import jax
 import jax.numpy as jnp
 from jax import lax
-from jax.sharding import PartitionSpec as P
+from jax.sharding import Mesh, PartitionSpec as P
 from jax.experimental import pallas as pl
 from jax.experimental.pallas import tpu as pltpu
 
@@ -14,6 +14,7 @@
 
 EPSILON = 1e-06
 MASKED_SCORE = -1e30
+EXP = ("chip", "core")
 
 
 def attention_kernel(rid_col_ref, rid_row_ref, q_ref, pkv_ref, skv_ref, out_ref):
@@ -93,7 +94,8 @@
 ):
     local_count = queries.shape[0]
     model_width = queries.shape[1]
-    exp_count = lax.axis_size("exp")
+    chip_count = lax.axis_size("chip")
+    core_count = lax.axis_size("core")
     req_count = lax.axis_size("req")
     by_req = lax.all_to_all(
         jnp.broadcast_to(prefix_key_values[:, None], (2, req_count) + prefix_key_values.shape[1:]),
@@ -102,9 +104,14 @@
         concat_axis=1,
         tiled=True,
     ).reshape(2, req_count * prefix_key_values.shape[1], prefix_key_values.shape[2])
-    spread = jnp.broadcast_to(by_req[:, None], (2, exp_count) + by_req.shape[1:])
-    gathered = lax.all_to_all(spread, "exp", split_axis=1, concat_axis=1, tiled=True)
-    all_prefix = gathered.reshape(2, exp_count * by_req.shape[1], by_req.shape[2])
+    spread = jnp.broadcast_to(by_req[:, None], (2, chip_count) + by_req.shape[1:])
+    by_chip = lax.all_to_all(spread, "chip", split_axis=1, concat_axis=1, tiled=True).reshape(
+        2, chip_count * by_req.shape[1], by_req.shape[2]
+    )
+    paired = jnp.broadcast_to(by_chip[:, None], (2, core_count) + by_chip.shape[1:])
+    all_prefix = lax.all_to_all(paired, "core", split_axis=1, concat_axis=1, tiled=True).reshape(
+        2, core_count * by_chip.shape[1], by_chip.shape[2]
+    )
     attended = attend(queries, all_prefix, suffix_key_values, request_ids)
     section = attended
     projected = jnp.dot(
@@ -116,7 +123,7 @@
     inverse_rms = lax.rsqrt(jnp.mean(stream * stream, axis=1, keepdims=True) + EPSILON)
     normed = (stream * inverse_rms * norm_gain[None, :]).astype(jnp.bfloat16)
     top_count = expert_routes.shape[1]
-    expert_count = gate_experts.shape[0] * lax.axis_size("exp")
+    expert_count = gate_experts.shape[0] * lax.axis_size(EXP)
     capacity = 3 * top_count * local_count // (2 * expert_count)
     flat_routes = expert_routes.reshape(-1)
     matches = (flat_routes[:, None] == jnp.arange(expert_count, dtype=jnp.int32)[None, :]).astype(
@@ -132,7 +139,7 @@
         .astype(jnp.bfloat16)
         .reshape(expert_count, capacity, model_width)
     )
-    slot_rows = lax.all_to_all(outgoing, "exp", split_axis=0, concat_axis=0, tiled=True)
+    slot_rows = lax.all_to_all(outgoing, EXP, split_axis=0, concat_axis=0, tiled=True)
     senders, slot_count, features = slot_rows.shape
     flat_rows = slot_rows.reshape(senders * slot_count, features)
     gated = jnp.dot(flat_rows, gate_experts[0], preferred_element_type=jnp.float32)
@@ -142,7 +149,7 @@
         jnp.bfloat16
     )
     computed = produced.reshape(senders, slot_count, features)
-    returned = lax.all_to_all(computed, "exp", split_axis=0, concat_axis=0, tiled=True)
+    returned = lax.all_to_all(computed, EXP, split_axis=0, concat_axis=0, tiled=True)
     slot_gates = jnp.sum(jnp.where(hit, route_gates[:, :, None], 0.0), axis=1)
     combined = jnp.dot(
         slot_gates,
@@ -155,19 +162,23 @@
 
 def solution(mesh):
     placed = (
-        P(("req", "exp"), None),
-        P(("req", "exp"), None),
-        P(None, ("req", "exp"), None),
-        P(None, ("req", "exp"), None),
-        P(("req", "exp"), None),
+        P(("req", "chip", "core"), None),
+        P(("req", "chip", "core"), None),
+        P(None, ("req", "chip", "core"), None),
+        P(None, ("req", "chip", "core"), None),
+        P(("req", "chip", "core"), None),
         P("req", None),
         P(),
-        P(("req", "exp"), None),
-        P(("req", "exp"), None),
-        P("exp", None, None),
-        P("exp", None, None),
-        P("exp", None, None),
+        P(("req", "chip", "core"), None),
+        P(("req", "chip", "core"), None),
+        P(EXP, None, None),
+        P(EXP, None, None),
+        P(EXP, None, None),
+    )
+    req_count, exp_count = mesh.devices.shape
+    split_mesh = Mesh(
+        mesh.devices.reshape(req_count, exp_count // 2, 2), ("req", "chip", "core")
     )
     return jax.shard_map(
-        on_device, mesh=mesh, in_specs=placed, out_specs=P(("req", "exp"), None), check_vma=False
+        on_device, mesh=split_mesh, in_specs=placed, out_specs=P(("req", "chip", "core"), None), check_vma=False
     )

time: 207 us -> 188 us (0.908)
  waiting for transfers between devices: 79.9 us -> 54.9 us
  blocking collectives: 54.4 us -> 63.7 us
  starting transfers between devices: 14.3 us -> 11.7 us
    all_to_all x2, waiting for transfers between devices: 79.1 us -> 54.2 us  [the longest x1 31 us: on_device(): lax.all_to_all(computed, EXP, split_axis=0, concat_axis=0, tiled=True)]
    all_to_all x1 -> x2, blocking collectives: 37.8 us -> 47.1 us  [the longest x1 34.7 us: on_device(): lax.all_to_all(outgoing, EXP, split_axis=0, concat_axis=0, tiled=True)]
    all_to_all x2, starting transfers between devices: 14.3 us -> 11.7 us  [the longest x1 6.94 us: on_device(): lax.all_to_all(spread, 'chip', split_axis=1, concat_axis=1, tiled=True)]
  transfers between devices with their start and end apart: 3 -> 3, of which waited for: 2 -> 2; matrix products, arithmetic and copies ran while one was open for 4% -> 4% of each run, Pallas kernels for 7% -> 8%
where the time goes in v3:
time: 188 us
  blocking collectives  63.7 us (34%)
  waiting for transfers between devices  54.9 us (29%)
  matrix products  20 us (11%)
  Pallas kernels  14.3 us (8%)
  between operations  13.6 us (7%)
  starting transfers between devices  11.7 us (6%)
  local copies, waits for them, and re-layouts  7.7 us (4%)
    all_to_all x1, blocking collectives, on_device(): lax.all_to_all(outgoing, EXP, split_axis=0, concat_axis=0, tiled=True)  34.7 us
    all_to_all x1, waiting for transfers between devices, on_device(): lax.all_to_all(computed, EXP, split_axis=0, concat_axis=0, tiled=True)  31 us
    all_to_all x1, waiting for transfers between devices, on_device(): lax.all_to_all(spread, 'chip', split_axis=1, concat_axis=1, tiled=True)  23.2 us
    all_to_all x1, blocking collectives, on_device(): lax.all_to_all(jnp.broadcast_to(prefix_key_values[:, None], (2, req_count...  16.6 us
    pallas_call x1, Pallas kernels, attend(): pl.pallas_call(attention_kernel, grid=(KEY_VALUE_HEADS,), in_specs=[pl.Bl...  14.3 us
    all_to_all x1, blocking collectives, on_device(): lax.all_to_all(paired, 'core', split_axis=1, concat_axis=1, tiled=True)  12.4 us
    dot_general x1, matrix products, on_device(): jnp.dot(active, down_experts[0], preferred_element_type=jnp.float32)  9.06 us
    all_to_all x1, starting transfers between devices, on_device(): lax.all_to_all(spread, 'chip', split_axis=1, concat_axis=1, tiled=True)  6.94 us
  transfers between devices with their start and end apart: 3, of which 2 were waited for; matrix products, arithmetic and copies ran while one was open for 4% of the time, Pallas kernels for 8%

profile of v3, /device:TPU:1, one launch (start us, length us, event | category | flops | bytes accessed | tf_op | source)
XLA Modules:
  0.0 187.7 jit_solution(17402459914120013315)
XLA Ops:
  6.5 0.0 copy-start
  6.5 0.0 all-gather.2.cloned.1.call-start
  6.5 0.7 all-gather.2.cloned.1.call-update
  7.3 0.7 broadcast_in_dim.18
  8.0 16.6 %all_to_all.25 = bf16[2,8,16,256]{3,2,0,1:T(8,128)(2,1)S(1)} all-to-all(bf16[2,8,16,256]{3,2,0,1:T(8,128)(2,1)S(1)} %broadcast_in_dim.18), channel_id=1, replica_groups=mesh['req'=8,'chip'=16,'core'=2] {'req'}, dimensions={1} | all-to-all | bytes 262144 | tf_op jit(solution)/shard_map/all_to_all | solution.py:100
  24.6 1.6 broadcast_in_dim.39
  26.2 0.0 copy-start.9
  26.2 6.9 %all-to-all-start.1 = ((bf16[2,16,128,256]{3,2,0,1:T(8,128)(2,1)}), bf16[2,16,128,256]{3,2,0,1:T(8,128)(2,1)}, u32[]{:S(2)}, u32[]{:S(2)}) async-start(bf16[2,16,128,256]{3,2,0,1:T(8,128)(2,1)} %broadcast_in_dim.39), calls=%async_computation.1 | async-start | bytes 4194304 | tf_op jit(solution)/shard_map/all_to_all | solution.py:108
  33.1 0.0 copy-done.9
  33.1 0.1 copy.55
  33.3 0.1 eq.38
  33.4 0.1 eq.42
  33.5 0.0 copy-done.3
  33.5 0.1 copy.54.rid_col_ref
  33.6 1.2 reduce-window.6
  34.8 0.2 slice_reduce_fusion
  35.0 0.1 fusion.14
  35.2 0.1 reduce_sum.30
  35.3 0.1 copy.58
  35.3 0.3 fusion.8
  35.6 23.2 %all-to-all-done.1 = bf16[2,16,128,256]{3,2,0,1:T(8,128)(2,1)} async-done(((bf16[2,16,128,256]{3,2,0,1:T(8,128)(2,1)}), bf16[2,16,128,256]{3,2,0,1:T(8,128)(2,1)}, u32[]{:S(2)}, u32[]{:S(2)}) %all-to-all-start.1) | async-done | bytes 2097184 | tf_op jit(solution)/shard_map/all_to_all | solution.py:108
  58.8 1.7 copy.52
  60.6 0.3 broadcast_in_dim.41
  60.9 12.4 %all_to_all.26 = bf16[2,2,2048,256]{3,2,0,1:T(8,128)(2,1)S(1)} all-to-all(bf16[2,2,2048,256]{3,2,0,1:T(8,128)(2,1)S(1)} %broadcast_in_dim.41), channel_id=1, replica_groups=mesh['req'=8,'chip'=16,'core'=2] {'core'}, dimensions={1} | all-to-all | bytes 8388608 | tf_op jit(solution)/shard_map/all_to_all | solution.py:112
  73.3 0.3 copy.53
  73.6 0.7 copy-done.1
  74.3 0.0 copy-done.2
  74.3 14.3 %shard_map.118 = bf16[128,1536]{1,0:T(8,128)(2,1)S(1)} custom-call(s32[128,1]{1,0:T(8,128)S(1)} %copy.54.rid_col_ref, s32[1,128]{1,0:T(1,128)S(1)} %copy-done.3, bf16[128,1536]{1,0:T(8,128)(2,1)S(1)} %copy-done.1, bf16[2,4096,256]{2,1,0:T(8,128)(2,1)S(1)} %bitcast.43, bf16[2,128,256]{2,1,0:T(8,128)(2,1)S(1)} %copy-done.2), custom_call_target="tpu_custom_call" | custom-call | tf_op jit(solution)/shard_map/pallas_call | solution.py:64
  88.6 0.0 copy-start.8
  88.6 0.0 all-gather.2.cloned.1.call-done
  88.6 0.0 copy-done.7
  88.6 3.2 %multiply_reduce_fusion = (f32[128]{0:T(128)S(1)}, f32[128,1536]{1,0:T(8,128)S(1)}) fusion(bf16[128,1536]{1,0:T(8,128)(2,1)S(1)} %shard_map.118, bf16[1536,1536]{1,0:T(8,128)(2,1)} %all-gather.2.cloned.1.call-done, bf16[128,1536]{1,0:T(8,128)(2,1)S(1)} %copy-done.7), kind=kOutput, calls=%fused_computation.15 | convolution fusion | flops 604766080 | bytes 6291968 | tf_op jit(solution)/shard_map/dot_general | solution.py:117
  91.9 0.0 copy-done.8
  91.9 0.9 convolution_convert_fusion.1
  92.8 0.0 copy-start.11
  92.8 34.7 %all_to_all.27 = bf16[32,24,1536]{2,1,0:T(8,128)(2,1)S(1)} all-to-all(bf16[32,24,1536]{2,1,0:T(8,128)(2,1)S(1)} %bitcast.45), channel_id=1, replica_groups=mesh['req'=8,'chip'=16,'core'=2] {'chip','core'}, dimensions={0} | all-to-all | bytes 4718592 | tf_op jit(solution)/shard_map/all_to_all | solution.py:142
  127.5 0.0 copy-done.4
  127.5 1.4 copy-done.6
  128.9 0.0 copy-done.11
  128.9 3.4 %fusion.2 = f32[768,768]{1,0:T(8,128)} fusion(bf16[768,1536]{1,0:T(8,128)(2,1)S(1)} %bitcast.48, bf16[1,1536,768]{2,1,0:T(8,128)(2,1)S(1)} %copy-done.11), kind=kOutput, calls=%fused_computation.6 | convolution fusion | flops 1811939328 | bytes 7077888 | tf_op jit(solution)/shard_map/dot_general | solution.py:146
  132.3 0.0 copy-done
  132.3 9.1 %convolution_convert_fusion = bf16[768,1536]{1,0:T(8,128)(2,1)} fusion(bf16[1,768,1536]{2,1,0:T(8,128)(2,1)S(1)} %copy-done, f32[768,768]{1,0:T(8,128)} %fusion.2, bf16[768,1536]{1,0:T(8,128)(2,1)} %bitcast.49, bf16[1,1536,768]{2,1,0:T(8,128)(2,1)} %param.21), kind=kOutput, calls=%fused_computation | convolution fusion | flops 3626827776 | bytes 11796480 | tf_op jit(solution)/shard_map/dot_general | solution.py:148
  141.4 4.7 %all-to-all-start.4 = ((bf16[32,24,1536]{2,1,0:T(8,128)(2,1)}), bf16[32,24,1536]{2,1,0:T(8,128)(2,1)}, u32[]{:S(2)}, u32[]{:S(2)}) async-start(bf16[32,24,1536]{2,1,0:T(8,128)(2,1)} %bitcast.47), calls=%async_computation.4 | async-start | bytes 4718592 | tf_op jit(solution)/shard_map/all_to_all | solution.py:152
  146.1 0.0 copy-done.10
  146.1 0.2 select_reduce_fusion
  146.4 31.0 %all-to-all-done.4 = bf16[32,24,1536]{2,1,0:T(8,128)(2,1)} async-done(((bf16[32,24,1536]{2,1,0:T(8,128)(2,1)}), bf16[32,24,1536]{2,1,0:T(8,128)(2,1)}, u32[]{:S(2)}, u32[]{:S(2)}) %all-to-all-start.4) | async-done | bytes 2359328 | tf_op jit(solution)/shard_map/all_to_all | solution.py:152
  177.3 0.0 copy-done.5
  177.3 3.5 %fusion = bf16[128,1536]{1,0:T(8,128)(2,1)} fusion(f32[128,1536]{1,0:T(8,128)S(1)} %copy-done.5, f32[128,768]{1,0:T(8,128)S(1)} %select_reduce_fusion, bf16[768,1536]{1,0:T(8,128)(2,1)} %bitcast.11), kind=kOutput, calls=%fused_computation.4 | convolution fusion | flops 1812332544 | bytes 3932160 | tf_op jit(solution)/shard_map/dot_general | solution.py:154
  (14 shorter events, 0.1 us)
Async XLA Ops:
  6.5 125.8 %copy-start = (bf16[1,768,1536]{2,1,0:T(8,128)(2,1)S(1)}, bf16[1,768,1536]{2,1,0:T(8,128)(2,1)}, u32[]{:S(2)}) copy-start(bf16[1,768,1536]{2,1,0:T(8,128)(2,1)} %param.23) | copy-start | bytes 7077892
  6.5 82.1 %all-gather.2.cloned.1.call-start = ((), (), s32[]{:S(2)}) async-start(), calls=%async_computation.5 | async-start | bytes 5308416 | tf_op jit(solution)/shard_map/all_gather | solution.py:119
  26.2 7.0 %copy-start.9 = (s32[128,4]{0,1:T(4,128)S(1)}, s32[128,4]{0,1:T(4,128)}, u32[]{:S(2)}) copy-start(s32[128,4]{0,1:T(4,128)} %param.19) | copy-start | bytes 6148
  26.2 7.3 %copy-start.3 = (s32[1,128]{1,0:T(1,128)S(1)}, s32[1,128]{1,0:T(1,128)}, u32[]{:S(2)}) copy-start(s32[1,128]{1,0:T(1,128)} %rid_row_ref.1) | copy-start | bytes 1540
  26.2 32.7 %all-to-all-start.1 = ((bf16[2,16,128,256]{3,2,0,1:T(8,128)(2,1)}), bf16[2,16,128,256]{3,2,0,1:T(8,128)(2,1)}, u32[]{:S(2)}, u32[]{:S(2)}) async-start(bf16[2,16,128,256]{3,2,0,1:T(8,128)(2,1)} %broadcast_in_dim.39), calls=%async_computation.1 | async-start | bytes 4194304 | tf_op jit(solution)/shard_map/all_to_all | solution.py:108
  73.3 1.0 copy-start.1
  73.3 1.0 copy-start.2
  74.3 14.3 %copy-start.7 = (bf16[128,1536]{1,0:T(8,128)(2,1)S(1)}, bf16[128,1536]{1,0:T(8,128)(2,1)}, u32[]{:S(2)}) copy-start(bf16[128,1536]{1,0:T(8,128)(2,1)} %param.12) | copy-start | bytes 1179652
  88.6 3.3 %copy-start.8 = (f32[1536]{0:T(1024)S(1)}, f32[1536]{0:T(1024)}, u32[]{:S(2)}) copy-start(f32[1536]{0:T(1024)} %param.18) | copy-start | bytes 18436
  91.9 35.6 %copy-start.4 = (f32[128,1536]{1,0:T(8,128)}, f32[128,1536]{1,0:T(8,128)S(1)}, u32[]{:S(2)}) copy-start(f32[128,1536]{1,0:T(8,128)S(1)} %get-tuple-element.6) | copy-start | bytes 2359300
  92.8 36.2 %copy-start.11 = (bf16[1,1536,768]{2,1,0:T(8,128)(2,1)S(1)}, bf16[1,1536,768]{2,1,0:T(8,128)(2,1)}, u32[]{:S(2)}) copy-start(bf16[1,1536,768]{2,1,0:T(8,128)(2,1)} %param.22) | copy-start | bytes 7077892
  127.5 1.4 copy-start.6
  141.4 4.7 %copy-start.10 = (f32[128,4]{0,1:T(4,128)S(1)}, f32[128,4]{0,1:T(4,128)}, u32[]{:S(2)}) copy-start(f32[128,4]{0,1:T(4,128)} %param.20) | copy-start | bytes 6148
  141.4 36.0 %copy-start.5 = (f32[128,1536]{1,0:T(8,128)S(1)}, f32[128,1536]{1,0:T(8,128)}, u32[]{:S(2)}) copy-start(f32[128,1536]{1,0:T(8,128)} %copy-done.4) | copy-start | bytes 2359300
  141.4 36.0 %all-to-all-start.4 = ((bf16[32,24,1536]{2,1,0:T(8,128)(2,1)}), bf16[32,24,1536]{2,1,0:T(8,128)(2,1)}, u32[]{:S(2)}, u32[]{:S(2)}) async-start(bf16[32,24,1536]{2,1,0:T(8,128)(2,1)} %bitcast.47), calls=%async_computation.4 | async-start | bytes 4718592 | tf_op jit(solution)/shard_map/all_to_all | solution.py:152
Sparse Core Ops, SparseCore 0:
  9.1 63.2 all-gather.1

commit v4 on v3

--- a/solution.py
+++ b/solution.py
@@ -130,26 +130,35 @@
         jnp.int32
     )
     slot_rank = jnp.sum((jnp.cumsum(matches, axis=0) - 1) * matches, axis=1)
-    slot_of_route = flat_routes * capacity + slot_rank
+    chunks = 2 if capacity % 2 == 0 else 1
+    part = capacity // chunks
+    slot_of_route = (
+        (slot_rank // part) * (expert_count * part) + flat_routes * part + slot_rank % part
+    )
     slot_ids = jnp.arange(expert_count * capacity, dtype=jnp.int32)
     hit = slot_of_route.reshape(local_count, top_count)[:, :, None] == slot_ids[None, None, :]
     dispatch = jnp.any(hit, axis=1).astype(jnp.bfloat16)
     outgoing = (
         jnp.einsum("ts,tf->sf", dispatch, normed, preferred_element_type=jnp.float32)
         .astype(jnp.bfloat16)
-        .reshape(expert_count, capacity, model_width)
+        .reshape(chunks, expert_count, part, model_width)
     )
-    slot_rows = lax.all_to_all(outgoing, EXP, split_axis=0, concat_axis=0, tiled=True)
-    senders, slot_count, features = slot_rows.shape
-    flat_rows = slot_rows.reshape(senders * slot_count, features)
-    gated = jnp.dot(flat_rows, gate_experts[0], preferred_element_type=jnp.float32)
-    lifted = jnp.dot(flat_rows, up_experts[0], preferred_element_type=jnp.float32)
-    active = (jnp.maximum(gated, 0.0) * lifted).astype(jnp.bfloat16)
-    produced = jnp.dot(active, down_experts[0], preferred_element_type=jnp.float32).astype(
-        jnp.bfloat16
-    )
-    computed = produced.reshape(senders, slot_count, features)
-    returned = lax.all_to_all(computed, EXP, split_axis=0, concat_axis=0, tiled=True)
+    returned_parts = []
+    for chunk in range(chunks):
+        slot_rows = lax.all_to_all(outgoing[chunk], EXP, split_axis=0, concat_axis=0, tiled=True)
+        senders, slot_count, features = slot_rows.shape
+        flat_rows = slot_rows.reshape(senders * slot_count, features)
+        gated = jnp.dot(flat_rows, gate_experts[0], preferred_element_type=jnp.float32)
+        lifted = jnp.dot(flat_rows, up_experts[0], preferred_element_type=jnp.float32)
+        active = (jnp.maximum(gated, 0.0) * lifted).astype(jnp.bfloat16)
+        produced = jnp.dot(active, down_experts[0], preferred_element_type=jnp.float32).astype(
+            jnp.bfloat16
+        )
+        computed = produced.reshape(senders, slot_count, features)
+        returned_parts.append(
+            lax.all_to_all(computed, EXP, split_axis=0, concat_axis=0, tiled=True)
+        )
+    returned = jnp.stack(returned_parts)
     slot_gates = jnp.sum(jnp.where(hit, route_gates[:, :, None], 0.0), axis=1)
     combined = jnp.dot(
         slot_gates,

time: 188 us -> 231 us (1.23)
  blocking collectives: 63.7 us -> 29 us
  waiting for transfers between devices: 54.9 us -> 82.6 us
  local copies, waits for them, and re-layouts: 7.7 us -> 28.3 us
  starting transfers between devices: 11.7 us -> 30.4 us
  matrix products: 20 us -> 26.1 us
  other arithmetic: 1.85 us -> 5.81 us
    all_to_all x1 -> x0, blocking collectives: 34.7 us -> none  [on_device(): lax.all_to_all(outgoing, EXP, split_axis=0, concat_axis=0, tiled=True)]
    all_to_all x0 -> x2, waiting for transfers between devices: none -> 29 us  [on_device(): lax.all_to_all(outgoing[chunk], EXP, split_axis=0, concat_axis=0, tiled=T...]
    reshape x0 -> x5, local copies, waits for them, and re-layouts: none -> 15.3 us  [the longest x2 5.93 us: on_device(): computed = produced.reshape(senders, slot_count, features)]
    all_to_all x0 -> x2, starting transfers between devices: none -> 11.1 us  [on_device(): lax.all_to_all(outgoing[chunk], EXP, split_axis=0, concat_axis=0, tiled=T...]
    all_to_all x1 -> x2, starting transfers between devices: 4.73 us -> 12.4 us  [on_device(): lax.all_to_all(computed, EXP, split_axis=0, concat_axis=0, tiled=True)]
    squeeze x0 -> x2, local copies, waits for them, and re-layouts: none -> 4.28 us  [on_device(): outgoing[chunk]]
    dot_general x1 -> x2, matrix products: 3.38 us -> 7.52 us  [on_device(): jnp.dot(flat_rows, up_experts[0], preferred_element_type=jnp.float32)]
    another operation x2 -> x3, other arithmetic: 1.2 us -> 5.15 us  [the longest x1 3.94 us: on_device(): returned = jnp.stack(returned_parts)]
  transfers between devices with their start and end apart: 3 -> 6, of which waited for: 2 -> 5; matrix products, arithmetic and copies ran while one was open for 4% -> 16% of each run, Pallas kernels for 8% -> 6%
where the time goes in v4:
time: 231 us; the launch traced here: 230 us
  waiting for transfers between devices  82.6 us (36%)
  starting transfers between devices  30.4 us (13%)
  blocking collectives  29 us (13%)
  local copies, waits for them, and re-layouts  28.3 us (12%)
  matrix products  26.1 us (11%)
  Pallas kernels  14.3 us (6%)
  between operations  13.6 us (6%)
  other arithmetic  5.81 us (3%)
    all_to_all x2, waiting for transfers between devices, on_device(): lax.all_to_all(computed, EXP, split_axis=0, concat_axis=0, tiled=True)  30.1 us
    all_to_all x2, waiting for transfers between devices, on_device(): lax.all_to_all(outgoing[chunk], EXP, split_axis=0, concat_axis=0, tiled=T...  29 us
    all_to_all x1, waiting for transfers between devices, on_device(): lax.all_to_all(spread, 'chip', split_axis=1, concat_axis=1, tiled=True)  22.8 us
    all_to_all x1, blocking collectives, on_device(): lax.all_to_all(jnp.broadcast_to(prefix_key_values[:, None], (2, req_count...  16.6 us
    pallas_call x1, Pallas kernels, attend(): pl.pallas_call(attention_kernel, grid=(KEY_VALUE_HEADS,), in_specs=[pl.Bl...  14.3 us
    all_to_all x2, starting transfers between devices, on_device(): lax.all_to_all(computed, EXP, split_axis=0, concat_axis=0, tiled=True)  12.4 us
    all_to_all x1, blocking collectives, on_device(): lax.all_to_all(paired, 'core', split_axis=1, concat_axis=1, tiled=True)  12.4 us
    all_to_all x2, starting transfers between devices, on_device(): lax.all_to_all(outgoing[chunk], EXP, split_axis=0, concat_axis=0, tiled=T...  11.1 us
  transfers between devices with their start and end apart: 6, of which 5 were waited for; matrix products, arithmetic and copies ran while one was open for 16% of the time, Pallas kernels for 6%

profile of v4, /device:TPU:1, one launch (start us, length us, event | category | flops | bytes accessed | tf_op | source)
XLA Modules:
  0.0 230.1 jit_solution(7064282484307615207)
XLA Ops:
  6.5 0.7 all-gather.2.cloned.1.call-update
  7.3 0.7 broadcast_in_dim.18
  8.0 16.6 %all_to_all.35 = bf16[2,8,16,256]{3,2,0,1:T(8,128)(2,1)S(1)} all-to-all(bf16[2,8,16,256]{3,2,0,1:T(8,128)(2,1)S(1)} %broadcast_in_dim.18), channel_id=1, replica_groups=mesh['req'=8,'chip'=16,'core'=2] {'req'}, dimensions={1} | all-to-all | bytes 262144 | tf_op jit(solution)/shard_map/all_to_all | solution.py:100
  24.6 1.6 broadcast_in_dim.39
  26.2 6.9 %all-to-all-start.1 = ((bf16[2,16,128,256]{3,2,0,1:T(8,128)(2,1)}), bf16[2,16,128,256]{3,2,0,1:T(8,128)(2,1)}, u32[]{:S(2)}, u32[]{:S(2)}) async-start(bf16[2,16,128,256]{3,2,0,1:T(8,128)(2,1)} %broadcast_in_dim.39), calls=%async_computation.1 | async-start | bytes 4194304 | tf_op jit(solution)/shard_map/all_to_all | solution.py:108
  33.2 0.1 copy.59
  33.4 0.1 eq.44
  33.5 0.1 copy.58.rid_col_ref
  33.6 1.2 reduce-window.6
  34.8 0.2 slice_reduce_fusion
  35.0 0.1 fusion.39
  35.2 0.1 div.18
  35.4 0.1 rem.22
  35.6 0.1 ne.34
  35.8 0.3 fusion.11
  36.1 22.8 %all-to-all-done.1 = bf16[2,16,128,256]{3,2,0,1:T(8,128)(2,1)} async-done(((bf16[2,16,128,256]{3,2,0,1:T(8,128)(2,1)}), bf16[2,16,128,256]{3,2,0,1:T(8,128)(2,1)}, u32[]{:S(2)}, u32[]{:S(2)}) %all-to-all-start.1) | async-done | bytes 2097184 | tf_op jit(solution)/shard_map/all_to_all | solution.py:108
  58.9 1.7 copy.56
  60.6 0.3 broadcast_in_dim.41
  60.9 12.4 %all_to_all.36 = bf16[2,2,2048,256]{3,2,0,1:T(8,128)(2,1)S(1)} all-to-all(bf16[2,2,2048,256]{3,2,0,1:T(8,128)(2,1)S(1)} %broadcast_in_dim.41), channel_id=1, replica_groups=mesh['req'=8,'chip'=16,'core'=2] {'core'}, dimensions={1} | all-to-all | bytes 8388608 | tf_op jit(solution)/shard_map/all_to_all | solution.py:112
  73.3 0.3 copy.57
  73.6 0.7 copy-done.1
  74.3 14.3 %shard_map.118 = bf16[128,1536]{1,0:T(8,128)(2,1)S(1)} custom-call(s32[128,1]{1,0:T(8,128)S(1)} %copy.58.rid_col_ref, s32[1,128]{1,0:T(1,128)S(1)} %copy-done.3, bf16[128,1536]{1,0:T(8,128)(2,1)S(1)} %copy-done.1, bf16[2,4096,256]{2,1,0:T(8,128)(2,1)S(1)} %bitcast.61, bf16[2,128,256]{2,1,0:T(8,128)(2,1)S(1)} %copy-done.2), custom_call_target="tpu_custom_call" | custom-call | tf_op jit(solution)/shard_map/pallas_call | solution.py:64
  88.7 3.2 %multiply_reduce_fusion = (f32[128]{0:T(128)S(1)}, f32[128,1536]{1,0:T(8,128)S(1)}) fusion(bf16[128,1536]{1,0:T(8,128)(2,1)S(1)} %shard_map.118, bf16[1536,1536]{1,0:T(8,128)(2,1)} %all-gather.2.cloned.1.call-done, bf16[128,1536]{1,0:T(8,128)(2,1)S(1)} %copy-done.6), kind=kOutput, calls=%fused_computation.27 | convolution fusion | flops 604766080 | bytes 6291968 | tf_op jit(solution)/shard_map/dot_general | solution.py:117
  91.9 0.9 copy-done.4
  92.8 0.8 convolution_convert_fusion
  93.6 1.2 fusion.46
  94.8 3.0 %squeeze.22 = bf16[32,12,1536]{2,1,0:T(8,128)(2,1)} reshape(bf16[384,1536]{1,0:T(8,128)(2,1)} %get-tuple-element.6) | data formatting | bytes 2359296 | tf_op jit(solution)/shard_map/squeeze | solution.py:148
  97.8 4.8 %all-to-all-start.5 = ((bf16[32,12,1536]{2,1,0:T(8,128)(2,1)}), bf16[32,12,1536]{2,1,0:T(8,128)(2,1)}, u32[]{:S(2)}, u32[]{:S(2)}) async-start(bf16[32,12,1536]{2,1,0:T(8,128)(2,1)} %squeeze.22), calls=%async_computation.5 | async-start | bytes 3145728 | tf_op jit(solution)/shard_map/all_to_all | solution.py:148
  102.6 1.3 squeeze.18
  103.9 21.1 %all-to-all-done.5 = bf16[32,12,1536]{2,1,0:T(8,128)(2,1)} async-done(((bf16[32,12,1536]{2,1,0:T(8,128)(2,1)}), bf16[32,12,1536]{2,1,0:T(8,128)(2,1)}, u32[]{:S(2)}, u32[]{:S(2)}) %all-to-all-start.5) | async-done | bytes 1179680 | tf_op jit(solution)/shard_map/all_to_all | solution.py:148
  125.0 6.2 %all-to-all-start.3 = ((bf16[32,12,1536]{2,1,0:T(8,128)(2,1)}), bf16[32,12,1536]{2,1,0:T(8,128)(2,1)}, u32[]{:S(2)}, u32[]{:S(2)}) async-start(bf16[32,12,1536]{2,1,0:T(8,128)(2,1)} %squeeze.18), calls=%async_computation.3 | async-start | bytes 3145728 | tf_op jit(solution)/shard_map/all_to_all | solution.py:148
  131.2 2.2 reshape.93
  133.5 3.8 %fusion.3 = f32[384,768]{1,0:T(8,128)} fusion(bf16[384,1536]{1,0:T(8,128)(2,1)S(1)} %reshape.93, bf16[1,1536,768]{2,1,0:T(8,128)(2,1)} %param.22), kind=kOutput, calls=%fused_computation.9 | convolution fusion | flops 905969664 | bytes 4718592 | tf_op jit(solution)/shard_map/dot_general | solution.py:152
  137.2 5.5 %convolution_convert_fusion.1 = bf16[384,1536]{1,0:T(8,128)(2,1)} fusion(bf16[1,768,1536]{2,1,0:T(8,128)(2,1)S(1)} %copy-done, f32[384,768]{1,0:T(8,128)} %fusion.3, bf16[384,1536]{1,0:T(8,128)(2,1)S(1)} %reshape.93, bf16[1,1536,768]{2,1,0:T(8,128)(2,1)} %param.21), kind=kOutput, calls=%fused_computation.2 | convolution fusion | flops 1813413888 | bytes 8257536 | tf_op jit(solution)/shard_map/dot_general | solution.py:154
  142.7 3.0 %reshape.94 = bf16[32,12,1536]{2,1,0:T(8,128)(2,1)} reshape(bf16[384,1536]{1,0:T(8,128)(2,1)} %convolution_convert_fusion.1) | data formatting | bytes 2359296 | tf_op jit(solution)/shard_map/reshape | solution.py:157
  145.7 7.9 %all-to-all-done.3 = bf16[32,12,1536]{2,1,0:T(8,128)(2,1)} async-done(((bf16[32,12,1536]{2,1,0:T(8,128)(2,1)}), bf16[32,12,1536]{2,1,0:T(8,128)(2,1)}, u32[]{:S(2)}, u32[]{:S(2)}) %all-to-all-start.3) | async-done | bytes 1179680 | tf_op jit(solution)/shard_map/all_to_all | solution.py:148
  153.6 6.2 %all-to-all-start.6 = ((bf16[32,12,1536]{2,1,0:T(8,128)(2,1)}), bf16[32,12,1536]{2,1,0:T(8,128)(2,1)}, u32[]{:S(2)}, u32[]{:S(2)}) async-start(bf16[32,12,1536]{2,1,0:T(8,128)(2,1)} %reshape.94), calls=%async_computation.6 | async-start | bytes 3145728 | tf_op jit(solution)/shard_map/all_to_all | solution.py:159
  159.8 2.2 reshape.91
  162.1 3.8 %fusion.5 = f32[384,768]{1,0:T(8,128)} fusion(bf16[384,1536]{1,0:T(8,128)(2,1)S(1)} %reshape.91, bf16[1,1536,768]{2,1,0:T(8,128)(2,1)} %param.22), kind=kOutput, calls=%fused_computation.11 | convolution fusion | flops 905969664 | bytes 4718592 | tf_op jit(solution)/shard_map/dot_general | solution.py:152
  165.8 5.5 %convolution_convert_fusion.2 = bf16[384,1536]{1,0:T(8,128)(2,1)} fusion(bf16[1,768,1536]{2,1,0:T(8,128)(2,1)S(1)} %copy-done, f32[384,768]{1,0:T(8,128)} %fusion.5, bf16[384,1536]{1,0:T(8,128)(2,1)S(1)} %reshape.91, bf16[1,1536,768]{2,1,0:T(8,128)(2,1)} %param.21), kind=kOutput, calls=%fused_computation.3 | convolution fusion | flops 1813413888 | bytes 8257536 | tf_op jit(solution)/shard_map/dot_general | solution.py:154
  171.3 3.0 %reshape.92 = bf16[32,12,1536]{2,1,0:T(8,128)(2,1)} reshape(bf16[384,1536]{1,0:T(8,128)(2,1)} %convolution_convert_fusion.2) | data formatting | bytes 2359296 | tf_op jit(solution)/shard_map/reshape | solution.py:157
  174.3 7.9 %all-to-all-done.6 = bf16[32,12,1536]{2,1,0:T(8,128)(2,1)} async-done(((bf16[32,12,1536]{2,1,0:T(8,128)(2,1)}), bf16[32,12,1536]{2,1,0:T(8,128)(2,1)}, u32[]{:S(2)}, u32[]{:S(2)}) %all-to-all-start.6) | async-done | bytes 1179680 | tf_op jit(solution)/shard_map/all_to_all | solution.py:159
  182.2 6.2 %all-to-all-start.4 = ((bf16[32,12,1536]{2,1,0:T(8,128)(2,1)}), bf16[32,12,1536]{2,1,0:T(8,128)(2,1)}, u32[]{:S(2)}, u32[]{:S(2)}) async-start(bf16[32,12,1536]{2,1,0:T(8,128)(2,1)} %reshape.92), calls=%async_computation.4 | async-start | bytes 3145728 | tf_op jit(solution)/shard_map/all_to_all | solution.py:159
  188.5 0.2 select_reduce_fusion
  188.7 22.1 %all-to-all-done.4 = bf16[32,12,1536]{2,1,0:T(8,128)(2,1)} async-done(((bf16[32,12,1536]{2,1,0:T(8,128)(2,1)}), bf16[32,12,1536]{2,1,0:T(8,128)(2,1)}, u32[]{:S(2)}, u32[]{:S(2)}) %all-to-all-start.4) | async-done | bytes 1179680 | tf_op jit(solution)/shard_map/all_to_all | solution.py:159
  210.8 3.9 %pad_maximum_fusion = bf16[2,32,12,1536]{3,2,1,0:T(8,128)(2,1)} fusion(bf16[1,32,12,1536]{3,2,1,0:T(8,128)(2,1)} %bitcast.9, bf16[1,32,12,1536]{3,2,1,0:T(8,128)(2,1)} %bitcast.8), kind=kLoop, calls=%fused_computation.1 | loop fusion | flops 1179648 | bytes 4718592 | tf_op jit(solution)/shard_map/stack | solution.py:161
  214.8 4.9 %reshape.95 = bf16[768,1536]{1,0:T(8,128)(2,1)} reshape(bf16[2,32,12,1536]{3,2,1,0:T(8,128)(2,1)} %pad_maximum_fusion) | data formatting | bytes 4718592 | tf_op jit(solution)/shard_map/reshape | solution.py:165
  219.7 3.5 %fusion = bf16[128,1536]{1,0:T(8,128)(2,1)} fusion(f32[128,1536]{1,0:T(8,128)S(1)} %copy-done.5, f32[128,768]{1,0:T(8,128)S(1)} %select_reduce_fusion, bf16[768,1536]{1,0:T(8,128)(2,1)} %reshape.95), kind=kOutput, calls=%fused_computation.6 | convolution fusion | flops 1812332544 | bytes 3932160 | tf_op jit(solution)/shard_map/dot_general | solution.py:163
  (32 shorter events, 0.5 us)
Async XLA Ops:
  6.5 130.7 %copy-start = (bf16[1,768,1536]{2,1,0:T(8,128)(2,1)S(1)}, bf16[1,768,1536]{2,1,0:T(8,128)(2,1)}, u32[]{:S(2)}) copy-start(bf16[1,768,1536]{2,1,0:T(8,128)(2,1)} %param.23) | copy-start | bytes 7077892
  6.5 82.1 %all-gather.2.cloned.1.call-start = ((), (), s32[]{:S(2)}) async-start(), calls=%async_computation.7 | async-start | bytes 5308416 | tf_op jit(solution)/shard_map/all_gather | solution.py:119
  26.2 7.0 %copy-start.8 = (s32[128,4]{0,1:T(4,128)S(1)}, s32[128,4]{0,1:T(4,128)}, u32[]{:S(2)}) copy-start(s32[128,4]{0,1:T(4,128)} %param.19) | copy-start | bytes 6148
  26.2 7.3 %copy-start.3 = (s32[1,128]{1,0:T(1,128)S(1)}, s32[1,128]{1,0:T(1,128)}, u32[]{:S(2)}) copy-start(s32[1,128]{1,0:T(1,128)} %rid_row_ref.1) | copy-start | bytes 1540
  26.2 32.7 %all-to-all-start.1 = ((bf16[2,16,128,256]{3,2,0,1:T(8,128)(2,1)}), bf16[2,16,128,256]{3,2,0,1:T(8,128)(2,1)}, u32[]{:S(2)}, u32[]{:S(2)}) async-start(bf16[2,16,128,256]{3,2,0,1:T(8,128)(2,1)} %broadcast_in_dim.39), calls=%async_computation.1 | async-start | bytes 4194304 | tf_op jit(solution)/shard_map/all_to_all | solution.py:108
  73.3 1.0 copy-start.1
  73.3 1.0 copy-start.2
  74.3 14.3 %copy-start.6 = (bf16[128,1536]{1,0:T(8,128)(2,1)S(1)}, bf16[128,1536]{1,0:T(8,128)(2,1)}, u32[]{:S(2)}) copy-start(bf16[128,1536]{1,0:T(8,128)(2,1)} %param.12) | copy-start | bytes 1179652
  88.6 4.2 %copy-start.7 = (f32[1536]{0:T(1024)S(1)}, f32[1536]{0:T(1024)}, u32[]{:S(2)}) copy-start(f32[1536]{0:T(1024)} %param.18) | copy-start | bytes 18436
  91.9 0.9 copy-start.4
  97.8 27.2 %all-to-all-start.5 = ((bf16[32,12,1536]{2,1,0:T(8,128)(2,1)}), bf16[32,12,1536]{2,1,0:T(8,128)(2,1)}, u32[]{:S(2)}, u32[]{:S(2)}) async-start(bf16[32,12,1536]{2,1,0:T(8,128)(2,1)} %squeeze.22), calls=%async_computation.5 | async-start | bytes 3145728 | tf_op jit(solution)/shard_map/all_to_all | solution.py:148
  125.0 28.6 %all-to-all-start.3 = ((bf16[32,12,1536]{2,1,0:T(8,128)(2,1)}), bf16[32,12,1536]{2,1,0:T(8,128)(2,1)}, u32[]{:S(2)}, u32[]{:S(2)}) async-start(bf16[32,12,1536]{2,1,0:T(8,128)(2,1)} %squeeze.18), calls=%async_computation.3 | async-start | bytes 3145728 | tf_op jit(solution)/shard_map/all_to_all | solution.py:148
  153.6 28.6 %all-to-all-start.6 = ((bf16[32,12,1536]{2,1,0:T(8,128)(2,1)}), bf16[32,12,1536]{2,1,0:T(8,128)(2,1)}, u32[]{:S(2)}, u32[]{:S(2)}) async-start(bf16[32,12,1536]{2,1,0:T(8,128)(2,1)} %reshape.94), calls=%async_computation.6 | async-start | bytes 3145728 | tf_op jit(solution)/shard_map/all_to_all | solution.py:159
  174.3 14.2 %copy-start.9 = (f32[128,4]{0,1:T(4,128)S(1)}, f32[128,4]{0,1:T(4,128)}, u32[]{:S(2)}) copy-start(f32[128,4]{0,1:T(4,128)} %param.20) | copy-start | bytes 6148
  182.2 28.6 %all-to-all-start.4 = ((bf16[32,12,1536]{2,1,0:T(8,128)(2,1)}), bf16[32,12,1536]{2,1,0:T(8,128)(2,1)}, u32[]{:S(2)}, u32[]{:S(2)}) async-start(bf16[32,12,1536]{2,1,0:T(8,128)(2,1)} %reshape.92), calls=%async_computation.4 | async-start | bytes 3145728 | tf_op jit(solution)/shard_map/all_to_all | solution.py:159
  214.8 4.9 %copy-start.5 = (f32[128,1536]{1,0:T(8,128)S(1)}, f32[128,1536]{1,0:T(8,128)}, u32[]{:S(2)}) copy-start(f32[128,1536]{1,0:T(8,128)} %copy-done.4) | copy-start | bytes 2359300
Sparse Core Ops, SparseCore 0:
  9.1 63.2 all-gather.1

commit v5 on v3

--- a/solution.py
+++ b/solution.py
@@ -76,6 +76,44 @@
         compiler_params=pltpu.CompilerParams(vmem_limit_bytes=48 * 1024 * 1024),
     )(request_ids.reshape(local_count, 1), request_ids.reshape(1, local_count), queries,
       prefix_key_values, suffix_key_values)
+
+
+def expert_kernel(rows_ref, gate_ref, up_ref, down_ref, out_ref, acc_ref):
+    step = pl.program_id(0)
+
+    @pl.when(step == 0)
+    def _():
+        acc_ref[...] = jnp.zeros_like(acc_ref)
+
+    rows = rows_ref[...]
+    gated = jnp.dot(rows, gate_ref[...], preferred_element_type=jnp.float32)
+    lifted = jnp.dot(rows, up_ref[...], preferred_element_type=jnp.float32)
+    active = (jnp.maximum(gated, 0.0) * lifted).astype(jnp.bfloat16)
+    acc_ref[...] += jnp.dot(active, down_ref[...], preferred_element_type=jnp.float32)
+
+    @pl.when(step == pl.num_programs(0) - 1)
+    def _():
+        out_ref[...] = acc_ref[...].astype(out_ref.dtype)
+
+
+def expert_ffn(rows, gate_experts, up_experts, down_experts):
+    count, width = rows.shape
+    hidden = gate_experts.shape[2]
+    block = 256 if hidden % 256 == 0 else hidden
+    return pl.pallas_call(
+        expert_kernel,
+        grid=(hidden // block,),
+        in_specs=[
+            pl.BlockSpec((count, width), lambda f: (0, 0)),
+            pl.BlockSpec((None, width, block), lambda f: (0, 0, f)),
+            pl.BlockSpec((None, width, block), lambda f: (0, 0, f)),
+            pl.BlockSpec((None, block, width), lambda f: (0, f, 0)),
+        ],
+        out_specs=pl.BlockSpec((count, width), lambda f: (0, 0)),
+        out_shape=jax.ShapeDtypeStruct((count, width), jnp.bfloat16),
+        scratch_shapes=[pltpu.VMEM((count, width), jnp.float32)],
+        compiler_params=pltpu.CompilerParams(vmem_limit_bytes=48 * 1024 * 1024),
+    )(rows, gate_experts, up_experts, down_experts)
 
 
 def on_device(
@@ -142,12 +180,7 @@
     slot_rows = lax.all_to_all(outgoing, EXP, split_axis=0, concat_axis=0, tiled=True)
     senders, slot_count, features = slot_rows.shape
     flat_rows = slot_rows.reshape(senders * slot_count, features)
-    gated = jnp.dot(flat_rows, gate_experts[0], preferred_element_type=jnp.float32)
-    lifted = jnp.dot(flat_rows, up_experts[0], preferred_element_type=jnp.float32)
-    active = (jnp.maximum(gated, 0.0) * lifted).astype(jnp.bfloat16)
-    produced = jnp.dot(active, down_experts[0], preferred_element_type=jnp.float32).astype(
-        jnp.bfloat16
-    )
+    produced = expert_ffn(flat_rows, gate_experts, up_experts, down_experts)
     computed = produced.reshape(senders, slot_count, features)
     returned = lax.all_to_all(computed, EXP, split_axis=0, concat_axis=0, tiled=True)
     slot_gates = jnp.sum(jnp.where(hit, route_gates[:, :, None], 0.0), axis=1)

time: 188 us -> 180 us (0.957)
  matrix products: 20 us -> 5.9 us
  Pallas kernels: 14.3 us -> 23.9 us
  local copies, waits for them, and re-layouts: 7.7 us -> 4.7 us
    dot_general x2 -> x0, matrix products: 12.4 us -> none  [the longest x1 9.06 us: on_device(): jnp.dot(active, down_experts[0], preferred_element_type=jnp.float32)]
    pallas_call x0 -> x1, Pallas kernels: none -> 9.62 us  [expert_ffn(): pl.pallas_call(expert_kernel, grid=(hidden // block,), in_specs=[pl.Block...]
  transfers between devices with their start and end apart: 3 -> 3, of which waited for: 2 -> 2; matrix products, arithmetic and copies ran while one was open for 4% -> 3% of each run, Pallas kernels for 8% -> 8%
where the time goes in v5:
time: 180 us; the launch traced here: 179 us
  blocking collectives  63.5 us (35%)
  waiting for transfers between devices  54.9 us (30%)
  Pallas kernels  23.9 us (13%)
  between operations  13.5 us (8%)
  starting transfers between devices  10.9 us (6%)
  matrix products  5.9 us (3%)
  local copies, waits for them, and re-layouts  4.7 us (3%)
  other arithmetic  1.85 us (1%)
    all_to_all x1, blocking collectives, on_device(): lax.all_to_all(outgoing, EXP, split_axis=0, concat_axis=0, tiled=True)  34.5 us
    all_to_all x1, waiting for transfers between devices, on_device(): lax.all_to_all(computed, EXP, split_axis=0, concat_axis=0, tiled=True)  31 us
    all_to_all x1, waiting for transfers between devices, on_device(): lax.all_to_all(spread, 'chip', split_axis=1, concat_axis=1, tiled=True)  23.2 us
    all_to_all x1, blocking collectives, on_device(): lax.all_to_all(jnp.broadcast_to(prefix_key_values[:, None], (2, req_count...  16.6 us
    pallas_call x1, Pallas kernels, attend(): pl.pallas_call(attention_kernel, grid=(KEY_VALUE_HEADS,), in_specs=[pl.Bl...  14.3 us
    all_to_all x1, blocking collectives, on_device(): lax.all_to_all(paired, 'core', split_axis=1, concat_axis=1, tiled=True)  12.4 us
    pallas_call x1, Pallas kernels, expert_ffn(): pl.pallas_call(expert_kernel, grid=(hidden // block,), in_specs=[pl.Block...  9.62 us
    all_to_all x1, starting transfers between devices, on_device(): lax.all_to_all(spread, 'chip', split_axis=1, concat_axis=1, tiled=True)  6.89 us
  transfers between devices with their start and end apart: 3, of which 2 were waited for; matrix products, arithmetic and copies ran while one was open for 3% of the time, Pallas kernels for 8%

profile of v5, /device:TPU:1, one launch (start us, length us, event | category | flops | bytes accessed | tf_op | source)
XLA Modules:
  0.0 179.2 jit_solution(14156115137425518447)
XLA Ops:
  6.5 0.0 all-gather.2.cloned.1.call-start
  6.5 0.7 all-gather.2.cloned.1.call-update
  7.3 0.7 broadcast_in_dim.18
  8.0 16.6 %all_to_all.25 = bf16[2,8,16,256]{3,2,0,1:T(8,128)(2,1)S(1)} all-to-all(bf16[2,8,16,256]{3,2,0,1:T(8,128)(2,1)S(1)} %broadcast_in_dim.18), channel_id=1, replica_groups=mesh['req'=8,'chip'=16,'core'=2] {'req'}, dimensions={1} | all-to-all | bytes 262144 | tf_op jit(solution)/shard_map/all_to_all | solution.py:138
  24.6 1.6 broadcast_in_dim.39
  26.2 0.0 copy-start.5
  26.2 0.0 copy-start.2
  26.2 6.9 %all-to-all-start.1 = ((bf16[2,16,128,256]{3,2,0,1:T(8,128)(2,1)}), bf16[2,16,128,256]{3,2,0,1:T(8,128)(2,1)S(1)}, u32[]{:S(2)}, u32[]{:S(2)}) async-start(bf16[2,16,128,256]{3,2,0,1:T(8,128)(2,1)} %broadcast_in_dim.39), calls=%async_computation.1 | async-start | bytes 4194304 | tf_op jit(solution)/shard_map/all_to_all | solution.py:146
  33.1 0.0 copy-done.5
  33.1 0.1 copy.55
  33.2 0.1 eq.38
  33.3 0.1 eq.42
  33.4 0.0 copy-done.2
  33.4 0.1 copy.54.rid_col_ref
  33.5 1.2 reduce-window.6
  34.7 0.2 slice_reduce_fusion
  35.0 0.1 fusion.5
  35.1 0.1 reduce_sum.30
  35.2 0.1 copy.58
  35.3 0.3 fusion.1
  35.6 23.2 %all-to-all-done.1 = bf16[2,16,128,256]{3,2,0,1:T(8,128)(2,1)S(1)} async-done(((bf16[2,16,128,256]{3,2,0,1:T(8,128)(2,1)}), bf16[2,16,128,256]{3,2,0,1:T(8,128)(2,1)S(1)}, u32[]{:S(2)}, u32[]{:S(2)}) %all-to-all-start.1) | async-done | bytes 2097184 | tf_op jit(solution)/shard_map/all_to_all | solution.py:146
  58.7 0.2 copy.52
  58.9 0.3 broadcast_in_dim.41
  59.2 12.4 %all_to_all.26 = bf16[2,2,2048,256]{3,2,0,1:T(8,128)(2,1)S(1)} all-to-all(bf16[2,2,2048,256]{3,2,0,1:T(8,128)(2,1)S(1)} %broadcast_in_dim.41), channel_id=1, replica_groups=mesh['req'=8,'chip'=16,'core'=2] {'core'}, dimensions={1} | all-to-all | bytes 8388608 | tf_op jit(solution)/shard_map/all_to_all | solution.py:150
  71.6 0.0 copy-start
  71.6 0.0 copy-start.1
  71.6 0.3 copy.53
  71.9 0.7 copy-done
  72.6 0.0 copy-done.1
  72.6 0.0 copy-start.3
  72.6 14.3 %shard_map.118 = bf16[128,1536]{1,0:T(8,128)(2,1)S(1)} custom-call(s32[128,1]{1,0:T(8,128)S(1)} %copy.54.rid_col_ref, s32[1,128]{1,0:T(1,128)S(1)} %copy-done.2, bf16[128,1536]{1,0:T(8,128)(2,1)S(1)} %copy-done, bf16[2,4096,256]{2,1,0:T(8,128)(2,1)S(1)} %bitcast.28, bf16[2,128,256]{2,1,0:T(8,128)(2,1)S(1)} %copy-done.1), custom_call_target="tpu_custom_call" | custom-call | tf_op jit(solution)/shard_map/pallas_call | solution.py:64
  86.9 0.0 copy-start.4
  87.0 0.0 all-gather.2.cloned.1.call-done
  87.0 0.0 copy-done.3
  87.0 3.2 %multiply_reduce_fusion = (f32[128]{0:T(128)S(1)}, f32[128,1536]{1,0:T(8,128)S(1)}) fusion(bf16[128,1536]{1,0:T(8,128)(2,1)S(1)} %shard_map.118, bf16[1536,1536]{1,0:T(8,128)(2,1)} %all-gather.2.cloned.1.call-done, bf16[128,1536]{1,0:T(8,128)(2,1)S(1)} %copy-done.3), kind=kOutput, calls=%fused_computation.8 | convolution fusion | flops 604766080 | bytes 6291968 | tf_op jit(solution)/shard_map/dot_general | solution.py:155
  90.2 0.0 copy-done.4
  90.2 0.9 convolution_convert_fusion
  91.1 34.5 %all_to_all.27 = bf16[32,24,1536]{2,1,0:T(8,128)(2,1)S(1)} all-to-all(bf16[32,24,1536]{2,1,0:T(8,128)(2,1)S(1)} %bitcast.32), channel_id=1, replica_groups=mesh['req'=8,'chip'=16,'core'=2] {'chip','core'}, dimensions={0} | all-to-all | bytes 4718592 | tf_op jit(solution)/shard_map/all_to_all | solution.py:180
  125.6 9.6 %shard_map.119 = bf16[768,1536]{1,0:T(8,128)(2,1)} custom-call(bf16[768,1536]{1,0:T(8,128)(2,1)S(1)} %bitcast.29, bf16[1,1536,768]{2,1,0:T(8,128)(2,1)} %gate_ref.1, bf16[1,1536,768]{2,1,0:T(8,128)(2,1)} %up_ref.1, bf16[1,768,1536]{2,1,0:T(8,128)(2,1)} %down_ref.1), custom_call_target="tpu_custom_call" | custom-call | tf_op jit(solution)/shard_map/pallas_call | solution.py:103
  135.2 0.0 copy-start.6
  135.2 4.0 %all-to-all-start.4 = ((bf16[32,24,1536]{2,1,0:T(8,128)(2,1)}), bf16[32,24,1536]{2,1,0:T(8,128)(2,1)S(1)}, u32[]{:S(2)}, u32[]{:S(2)}) async-start(bf16[32,24,1536]{2,1,0:T(8,128)(2,1)} %bitcast.7), calls=%async_computation.4 | async-start | bytes 4718592 | tf_op jit(solution)/shard_map/all_to_all | solution.py:185
  139.2 0.0 copy-done.6
  139.2 0.2 select_reduce_fusion
  139.5 31.0 %all-to-all-done.4 = bf16[32,24,1536]{2,1,0:T(8,128)(2,1)S(1)} async-done(((bf16[32,24,1536]{2,1,0:T(8,128)(2,1)}), bf16[32,24,1536]{2,1,0:T(8,128)(2,1)S(1)}, u32[]{:S(2)}, u32[]{:S(2)}) %all-to-all-start.4) | async-done | bytes 2359328 | tf_op jit(solution)/shard_map/all_to_all | solution.py:185
  170.5 1.8 %fusion = bf16[128,1536]{1,0:T(8,128)(2,1)} fusion(f32[128,1536]{1,0:T(8,128)S(1)} %get-tuple-element.6, f32[128,768]{1,0:T(8,128)S(1)} %select_reduce_fusion, bf16[768,1536]{1,0:T(8,128)(2,1)S(1)} %bitcast.31), kind=kOutput, calls=%fused_computation.3 | convolution fusion | flops 1812332544 | bytes 3932160 | tf_op jit(solution)/shard_map/dot_general | solution.py:187
  (6 shorter events, 0.1 us)
Async XLA Ops:
  6.5 80.4 %all-gather.2.cloned.1.call-start = ((), (), s32[]{:S(2)}) async-start(), calls=%async_computation.5 | async-start | bytes 5308416 | tf_op jit(solution)/shard_map/all_gather | solution.py:157
  26.2 6.9 %copy-start.5 = (s32[128,4]{0,1:T(4,128)S(1)}, s32[128,4]{0,1:T(4,128)}, u32[]{:S(2)}) copy-start(s32[128,4]{0,1:T(4,128)} %param.19) | copy-start | bytes 6148
  26.2 7.2 %copy-start.2 = (s32[1,128]{1,0:T(1,128)S(1)}, s32[1,128]{1,0:T(1,128)}, u32[]{:S(2)}) copy-start(s32[1,128]{1,0:T(1,128)} %rid_row_ref.1) | copy-start | bytes 1540
  26.2 32.6 %all-to-all-start.1 = ((bf16[2,16,128,256]{3,2,0,1:T(8,128)(2,1)}), bf16[2,16,128,256]{3,2,0,1:T(8,128)(2,1)S(1)}, u32[]{:S(2)}, u32[]{:S(2)}) async-start(bf16[2,16,128,256]{3,2,0,1:T(8,128)(2,1)} %broadcast_in_dim.39), calls=%async_computation.1 | async-start | bytes 4194304 | tf_op jit(solution)/shard_map/all_to_all | solution.py:146
  71.6 1.0 copy-start
  71.6 1.0 copy-start.1
  72.6 14.3 %copy-start.3 = (bf16[128,1536]{1,0:T(8,128)(2,1)S(1)}, bf16[128,1536]{1,0:T(8,128)(2,1)}, u32[]{:S(2)}) copy-start(bf16[128,1536]{1,0:T(8,128)(2,1)} %param.12) | copy-start | bytes 1179652
  86.9 3.3 %copy-start.4 = (f32[1536]{0:T(1024)S(1)}, f32[1536]{0:T(1024)}, u32[]{:S(2)}) copy-start(f32[1536]{0:T(1024)} %param.18) | copy-start | bytes 18436
  135.2 4.0 %copy-start.6 = (f32[128,4]{0,1:T(4,128)S(1)}, f32[128,4]{0,1:T(4,128)}, u32[]{:S(2)}) copy-start(f32[128,4]{0,1:T(4,128)} %param.20) | copy-start | bytes 6148
  135.2 35.2 %all-to-all-start.4 = ((bf16[32,24,1536]{2,1,0:T(8,128)(2,1)}), bf16[32,24,1536]{2,1,0:T(8,128)(2,1)S(1)}, u32[]{:S(2)}, u32[]{:S(2)}) async-start(bf16[32,24,1536]{2,1,0:T(8,128)(2,1)} %bitcast.7), calls=%async_computation.4 | async-start | bytes 4718592 | tf_op jit(solution)/shard_map/all_to_all | solution.py:185
Sparse Core Ops, SparseCore 0:
  9.1 63.2 all-gather.1

commit v6 on v5

--- a/solution.py
+++ b/solution.py
@@ -17,28 +17,25 @@
 EXP = ("chip", "core")
 
 
-def attention_kernel(rid_col_ref, rid_row_ref, q_ref, pkv_ref, skv_ref, out_ref):
+def head_scores(q_ref, keys, head):
+    columns = slice(head * HEAD_SIZE, (head + 1) * HEAD_SIZE)
+    contract = (((1,), (1,)), ((), ()))
+    return lax.dot_general(
+        q_ref[:, columns], keys, contract, preferred_element_type=jnp.float32
+    ) * (1.0 / math.sqrt(HEAD_SIZE))
+
+
+def local_kernel(rid_col_ref, rid_row_ref, q_ref, pkv_ref, skv_ref, acc_ref, peak_ref, total_ref):
     local_count = q_ref.shape[0]
-    scale = 1.0 / math.sqrt(HEAD_SIZE)
     position = lax.broadcasted_iota(jnp.int32, (local_count, local_count), 0)
     key_position = lax.broadcasted_iota(jnp.int32, (local_count, local_count), 1)
     allowed = (rid_col_ref[...] == rid_row_ref[...]) & (position >= key_position)
-    prefix_keys = pkv_ref[0]
-    prefix_values = pkv_ref[1]
-    suffix_keys = skv_ref[0]
-    suffix_values = skv_ref[1]
-    contract = (((1,), (1,)), ((), ()))
-    for head in range(QUERY_HEADS // KEY_VALUE_HEADS):
+    groups = QUERY_HEADS // KEY_VALUE_HEADS
+    for head in range(QUERY_HEADS):
+        kv_columns = slice((head // groups) * HEAD_SIZE, (head // groups + 1) * HEAD_SIZE)
         columns = slice(head * HEAD_SIZE, (head + 1) * HEAD_SIZE)
-        query_rows = q_ref[:, columns]
-        prefix_scores = (
-            lax.dot_general(query_rows, prefix_keys, contract, preferred_element_type=jnp.float32)
-            * scale
-        )
-        suffix_scores = (
-            lax.dot_general(query_rows, suffix_keys, contract, preferred_element_type=jnp.float32)
-            * scale
-        )
+        prefix_scores = head_scores(q_ref, pkv_ref[0, :, kv_columns], head)
+        suffix_scores = head_scores(q_ref, skv_ref[0, :, kv_columns], head)
         suffix_scores = jnp.where(allowed, suffix_scores, MASKED_SCORE)
         peak = jnp.maximum(
             jnp.max(prefix_scores, axis=1, keepdims=True),
@@ -46,36 +43,69 @@
         )
         prefix_weights = jnp.exp(prefix_scores - peak)
         suffix_weights = jnp.where(allowed, jnp.exp(suffix_scores - peak), 0.0)
-        total = jnp.sum(prefix_weights, axis=1, keepdims=True) + jnp.sum(
+        total_ref[:, head : head + 1] = jnp.sum(prefix_weights, axis=1, keepdims=True) + jnp.sum(
             suffix_weights, axis=1, keepdims=True
         )
-        summed = jnp.dot(
-            prefix_weights.astype(jnp.bfloat16), prefix_values, preferred_element_type=jnp.float32
+        peak_ref[:, head : head + 1] = peak
+        acc_ref[:, columns] = jnp.dot(
+            prefix_weights.astype(jnp.bfloat16),
+            pkv_ref[1, :, kv_columns],
+            preferred_element_type=jnp.float32,
         ) + jnp.dot(
-            suffix_weights.astype(jnp.bfloat16), suffix_values, preferred_element_type=jnp.float32
-        )
+            suffix_weights.astype(jnp.bfloat16),
+            skv_ref[1, :, kv_columns],
+            preferred_element_type=jnp.float32,
+        )
+
+
+def merge_kernel(q_ref, pkv_ref, acc_ref, peak_ref, total_ref, out_ref):
+    groups = QUERY_HEADS // KEY_VALUE_HEADS
+    for head in range(QUERY_HEADS):
+        kv_columns = slice((head // groups) * HEAD_SIZE, (head // groups + 1) * HEAD_SIZE)
+        columns = slice(head * HEAD_SIZE, (head + 1) * HEAD_SIZE)
+        scores = head_scores(q_ref, pkv_ref[0, :, kv_columns], head)
+        own_peak = jnp.max(scores, axis=1, keepdims=True)
+        weights = jnp.exp(scores - own_peak)
+        own_total = jnp.sum(weights, axis=1, keepdims=True)
+        own_acc = jnp.dot(
+            weights.astype(jnp.bfloat16), pkv_ref[1, :, kv_columns], preferred_element_type=jnp.float32
+        )
+        first_peak = peak_ref[:, head : head + 1]
+        peak = jnp.maximum(first_peak, own_peak)
+        first_scale = jnp.exp(first_peak - peak)
+        own_scale = jnp.exp(own_peak - peak)
+        total = total_ref[:, head : head + 1] * first_scale + own_total * own_scale
+        summed = acc_ref[:, columns] * first_scale + own_acc * own_scale
         out_ref[:, columns] = (summed / total).astype(out_ref.dtype)
 
 
-def attend(queries, prefix_key_values, suffix_key_values, request_ids):
+def whole(shape):
+    return pl.BlockSpec(shape, lambda: (0,) * len(shape))
+
+
+def attend_local(queries, prefix_key_values, suffix_key_values, request_ids):
     local_count, model_width = queries.shape
-    prefix_count = prefix_key_values.shape[1]
-    group_width = model_width // KEY_VALUE_HEADS
+    column, row = request_ids.reshape(local_count, 1), request_ids.reshape(1, local_count)
+    inputs = (column, row, queries, prefix_key_values, suffix_key_values)
+    stats = jax.ShapeDtypeStruct((local_count, QUERY_HEADS), jnp.float32)
     return pl.pallas_call(
-        attention_kernel,
-        grid=(KEY_VALUE_HEADS,),
-        in_specs=[
-            pl.BlockSpec((local_count, 1), lambda g: (0, 0)),
-            pl.BlockSpec((1, local_count), lambda g: (0, 0)),
-            pl.BlockSpec((local_count, group_width), lambda g: (0, g)),
-            pl.BlockSpec((2, prefix_count, HEAD_SIZE), lambda g: (0, 0, g)),
-            pl.BlockSpec((2, local_count, HEAD_SIZE), lambda g: (0, 0, g)),
-        ],
-        out_specs=pl.BlockSpec((local_count, group_width), lambda g: (0, g)),
-        out_shape=jax.ShapeDtypeStruct((local_count, model_width), jnp.bfloat16),
+        local_kernel,
+        in_specs=[whole(x.shape) for x in inputs],
+        out_specs=[whole((local_count, model_width)), whole(stats.shape), whole(stats.shape)],
+        out_shape=[jax.ShapeDtypeStruct((local_count, model_width), jnp.float32), stats, stats],
         compiler_params=pltpu.CompilerParams(vmem_limit_bytes=48 * 1024 * 1024),
-    )(request_ids.reshape(local_count, 1), request_ids.reshape(1, local_count), queries,
-      prefix_key_values, suffix_key_values)
+    )(*inputs)
+
+
+def attend_merge(queries, prefix_key_values, acc, peak, total):
+    inputs = (queries, prefix_key_values, acc, peak, total)
+    return pl.pallas_call(
+        merge_kernel,
+        in_specs=[whole(x.shape) for x in inputs],
+        out_specs=whole(queries.shape),
+        out_shape=jax.ShapeDtypeStruct(queries.shape, jnp.bfloat16),
+        compiler_params=pltpu.CompilerParams(vmem_limit_bytes=48 * 1024 * 1024),
+    )(*inputs)
 
 
 def expert_kernel(rows_ref, gate_ref, up_ref, down_ref, out_ref, acc_ref):
@@ -133,7 +163,6 @@
     local_count = queries.shape[0]
     model_width = queries.shape[1]
     chip_count = lax.axis_size("chip")
-    core_count = lax.axis_size("core")
     req_count = lax.axis_size("req")
     by_req = lax.all_to_all(
         jnp.broadcast_to(prefix_key_values[:, None], (2, req_count) + prefix_key_values.shape[1:]),
@@ -146,11 +175,9 @@
     by_chip = lax.all_to_all(spread, "chip", split_axis=1, concat_axis=1, tiled=True).reshape(
         2, chip_count * by_req.shape[1], by_req.shape[2]
     )
-    paired = jnp.broadcast_to(by_chip[:, None], (2, core_count) + by_chip.shape[1:])
-    all_prefix = lax.all_to_all(paired, "core", split_axis=1, concat_axis=1, tiled=True).reshape(
-        2, core_count * by_chip.shape[1], by_chip.shape[2]
-    )
-    attended = attend(queries, all_prefix, suffix_key_values, request_ids)
+    partner_half = lax.ppermute(by_chip, "core", [(0, 1), (1, 0)])
+    acc, peak, total = attend_local(queries, by_chip, suffix_key_values, request_ids)
+    attended = attend_merge(queries, partner_half, acc, peak, total)
     section = attended
     projected = jnp.dot(
         section,

time: 180 us -> 172 us (0.956)
  waiting for transfers between devices: 54.9 us -> 31.7 us
  blocking collectives: 63.5 us -> 84.3 us
  starting transfers between devices: 10.9 us -> 7.36 us
  local copies, waits for them, and re-layouts: 4.7 us -> 1.97 us
    all_to_all x1 -> x0, waiting for transfers between devices: 23.2 us -> none  [on_device(): lax.all_to_all(spread, 'chip', split_axis=1, concat_axis=1, tiled=True)]
    all_to_all x1, blocking collectives: 12.4 us -> 33 us  [on_device(): lax.all_to_all(spread, 'chip', split_axis=1, concat_axis=1, tiled=True)]
    all_to_all x1 -> x0, starting transfers between devices: 6.89 us -> none  [on_device(): lax.all_to_all(spread, 'chip', split_axis=1, concat_axis=1, tiled=True)]
    ppermute x0 -> x1, starting transfers between devices: none -> 3.36 us  [on_device(): partner_half = lax.ppermute(by_chip, 'core', [(0, 1), (1, 0)])]
    pallas_call x1 -> x2, Pallas kernels: 14.3 us -> 15.5 us  [the longest x1 8.57 us: attend_merge(): pl.pallas_call(merge_kernel, in_specs=[whole(x.shape) for x in inputs], o...]
  transfers between devices with their start and end apart: 3 -> 3, of which waited for: 2 -> 1; matrix products, arithmetic and copies ran while one was open for 3% -> 2% of each run, Pallas kernels for 8% -> 9%
where the time goes in v6:
time: 172 us
  blocking collectives  84.3 us (49%)
  waiting for transfers between devices  31.7 us (18%)
  Pallas kernels  25.2 us (15%)
  between operations  13.6 us (8%)
  starting transfers between devices  7.36 us (4%)
  matrix products  5.92 us (3%)
  local copies, waits for them, and re-layouts  1.97 us (1%)
  other arithmetic  1.85 us (1%)
    all_to_all x1, blocking collectives, on_device(): lax.all_to_all(outgoing, EXP, split_axis=0, concat_axis=0, tiled=True)  34.8 us
    all_to_all x1, blocking collectives, on_device(): lax.all_to_all(spread, 'chip', split_axis=1, concat_axis=1, tiled=True)  33 us
    all_to_all x1, waiting for transfers between devices, on_device(): lax.all_to_all(computed, EXP, split_axis=0, concat_axis=0, tiled=True)  31 us
    all_to_all x1, blocking collectives, on_device(): lax.all_to_all(jnp.broadcast_to(prefix_key_values[:, None], (2, req_count...  16.6 us
    pallas_call x1, Pallas kernels, expert_ffn(): pl.pallas_call(expert_kernel, grid=(hidden // block,), in_specs=[pl.Block...  9.61 us
    pallas_call x1, Pallas kernels, attend_merge(): pl.pallas_call(merge_kernel, in_specs=[whole(x.shape) for x in inputs], o...  8.57 us
    pallas_call x1, Pallas kernels, attend_local(): pl.pallas_call(local_kernel, in_specs=[whole(x.shape) for x in inputs], o...  6.98 us
    all_to_all x1, starting transfers between devices, on_device(): lax.all_to_all(computed, EXP, split_axis=0, concat_axis=0, tiled=True)  3.99 us
  transfers between devices with their start and end apart: 3, of which 1 were waited for; matrix products, arithmetic and copies ran while one was open for 2% of the time, Pallas kernels for 9%

profile of v6, /device:TPU:1, one launch (start us, length us, event | category | flops | bytes accessed | tf_op | source)
XLA Modules:
  0.0 171.9 jit_solution(3151761654851140080)
XLA Ops:
  6.5 0.0 all-gather.2.cloned.1.call-start
  6.5 0.7 all-gather.2.cloned.1.call-update
  7.3 0.7 broadcast_in_dim.14
  8.0 16.6 %all_to_all.20 = bf16[2,8,16,256]{3,2,0,1:T(8,128)(2,1)S(1)} all-to-all(bf16[2,8,16,256]{3,2,0,1:T(8,128)(2,1)S(1)} %broadcast_in_dim.14), channel_id=1, replica_groups=mesh['req'=8,'chip'=16,'core'=2] {'req'}, dimensions={1} | all-to-all | bytes 262144 | tf_op jit(solution)/shard_map/all_to_all | solution.py:167
  24.6 0.2 broadcast_in_dim.32
  24.8 33.0 %all_to_all.21 = bf16[2,16,128,256]{3,2,0,1:T(8,128)(2,1)S(1)} all-to-all(bf16[2,16,128,256]{3,2,0,1:T(8,128)(2,1)S(1)} %broadcast_in_dim.32), channel_id=1, replica_groups=mesh['req'=8,'chip'=16,'core'=2] {'chip'}, dimensions={1} | all-to-all | bytes 4194304 | tf_op jit(solution)/shard_map/all_to_all | solution.py:175
  57.8 0.0 copy-start.5
  57.8 0.0 copy-start.2
  57.8 0.0 copy-start
  57.8 0.0 copy-start.1
  57.8 0.1 copy.50
  58.0 3.4 %collective-permute-start = (bf16[2,2048,256]{2,1,0:T(8,128)(2,1)S(1)}, bf16[2,2048,256]{2,1,0:T(8,128)(2,1)}, u32[]{:S(2)}, u32[]{:S(2)}) collective-permute-start(bf16[2,2048,256]{2,1,0:T(8,128)(2,1)S(1)} %bitcast.28), channel_id=1, source_target_pairs={{0,1},{1,0},{2,3},{3,2},{4,5},{5,4},{6,7},{7,6},{8,9},{9,8},{10,11... | collective-permute-start | bytes 6291464 | tf_op jit(solution)/shard_map/ppermute | solution.py:178
  61.3 0.0 copy-done.5
  61.3 0.1 copy.52
  61.4 0.1 eq.42
  61.5 0.1 eq.38
  61.7 0.0 copy-done.2
  61.7 0.1 copy.51.rid_col_ref
  61.8 1.2 reduce-window.6
  63.0 0.2 slice_reduce_fusion
  63.2 0.1 fusion.5
  63.3 0.1 reduce_sum.30
  63.4 0.1 copy.55
  63.5 0.3 fusion.1
  63.8 0.0 copy-done
  63.8 0.0 copy-done.1
  63.8 7.0 %shard_map.118 = (f32[128,1536]{1,0:T(8,128)S(1)}, f32[128,12]{1,0:T(8,128)S(1)}, f32[128,12]{1,0:T(8,128)S(1)}) custom-call(s32[128,1]{1,0:T(8,128)S(1)} %copy.51.rid_col_ref, s32[1,128]{1,0:T(1,128)S(1)} %copy-done.2, bf16[128,1536]{1,0:T(8,128)(2,1)S(1)} %copy-done, bf16[2,2048,256]{2,1,0:T(8,128)(2,1)S(1)} %bitcast.29, bf16[2,128,256]{2,1,0:T(8,128)(2,1)S(1)} %copy-done.1), custom_call_target="tpu_custom_call" | custom-call | tf_op jit(solution)/shard_map/pallas_call | solution.py:91
  70.8 0.0 copy-start.3
  70.8 0.0 collective-permute-done.pkv_ref
  70.8 8.6 %shard_map.119 = bf16[128,1536]{1,0:T(8,128)(2,1)S(1)} custom-call(bf16[128,1536]{1,0:T(8,128)(2,1)S(1)} %copy-done, bf16[2,2048,256]{2,1,0:T(8,128)(2,1)} %collective-permute-done.pkv_ref, f32[128,1536]{1,0:T(8,128)S(1)} %get-tuple-element.8.acc_ref, f32[128,12]{1,0:T(8,128)S(1)} %get-tuple-element.9.peak_ref, f32[128,12]{1,0:T(8,128)S(1)} %get-tuple-element.10.total_ref), custom_call_target="tpu_custom_call" | custom-call | tf_op jit(solution)/shard_map/pallas_call | solution.py:102
  79.4 0.0 copy-start.4
  79.4 0.0 all-gather.2.cloned.1.call-done
  79.5 0.0 copy-done.3
  79.5 3.2 %multiply_reduce_fusion = (f32[128]{0:T(128)S(1)}, f32[128,1536]{1,0:T(8,128)S(1)}) fusion(bf16[128,1536]{1,0:T(8,128)(2,1)S(1)} %shard_map.119, bf16[1536,1536]{1,0:T(8,128)(2,1)} %all-gather.2.cloned.1.call-done, bf16[128,1536]{1,0:T(8,128)(2,1)S(1)} %copy-done.3), kind=kOutput, calls=%fused_computation.8 | convolution fusion | flops 604766080 | bytes 6291968 | tf_op jit(solution)/shard_map/dot_general | solution.py:182
  82.7 0.0 copy-done.4
  82.7 0.9 convolution_convert_fusion
  83.6 34.8 %all_to_all.22 = bf16[32,24,1536]{2,1,0:T(8,128)(2,1)S(1)} all-to-all(bf16[32,24,1536]{2,1,0:T(8,128)(2,1)S(1)} %bitcast.32), channel_id=1, replica_groups=mesh['req'=8,'chip'=16,'core'=2] {'chip','core'}, dimensions={0} | all-to-all | bytes 4718592 | tf_op jit(solution)/shard_map/all_to_all | solution.py:207
  118.3 9.6 %shard_map.120 = bf16[768,1536]{1,0:T(8,128)(2,1)} custom-call(bf16[768,1536]{1,0:T(8,128)(2,1)S(1)} %bitcast.27, bf16[1,1536,768]{2,1,0:T(8,128)(2,1)} %gate_ref.1, bf16[1,1536,768]{2,1,0:T(8,128)(2,1)} %up_ref.1, bf16[1,768,1536]{2,1,0:T(8,128)(2,1)} %down_ref.1), custom_call_target="tpu_custom_call" | custom-call | tf_op jit(solution)/shard_map/pallas_call | solution.py:133
  127.9 0.0 copy-start.6
  127.9 4.0 %all-to-all-start.3 = ((bf16[32,24,1536]{2,1,0:T(8,128)(2,1)}), bf16[32,24,1536]{2,1,0:T(8,128)(2,1)S(1)}, u32[]{:S(2)}, u32[]{:S(2)}) async-start(bf16[32,24,1536]{2,1,0:T(8,128)(2,1)} %bitcast.6), calls=%async_computation.3 | async-start | bytes 4718592 | tf_op jit(solution)/shard_map/all_to_all | solution.py:212
  131.9 0.0 copy-done.6
  132.0 0.2 select_reduce_fusion
  132.2 31.0 %all-to-all-done.3 = bf16[32,24,1536]{2,1,0:T(8,128)(2,1)S(1)} async-done(((bf16[32,24,1536]{2,1,0:T(8,128)(2,1)}), bf16[32,24,1536]{2,1,0:T(8,128)(2,1)S(1)}, u32[]{:S(2)}, u32[]{:S(2)}) %all-to-all-start.3) | async-done | bytes 2359328 | tf_op jit(solution)/shard_map/all_to_all | solution.py:212
  163.2 1.8 %fusion = bf16[128,1536]{1,0:T(8,128)(2,1)} fusion(f32[128,1536]{1,0:T(8,128)S(1)} %get-tuple-element.12, f32[128,768]{1,0:T(8,128)S(1)} %select_reduce_fusion, bf16[768,1536]{1,0:T(8,128)(2,1)S(1)} %bitcast.31), kind=kOutput, calls=%fused_computation.3 | convolution fusion | flops 1812332544 | bytes 3932160 | tf_op jit(solution)/shard_map/dot_general | solution.py:214
  (6 shorter events, 0.1 us)
Async XLA Ops:
  6.5 72.9 %all-gather.2.cloned.1.call-start = ((), (), s32[]{:S(2)}) async-start(), calls=%async_computation.4 | async-start | bytes 5308416 | tf_op jit(solution)/shard_map/all_gather | solution.py:184
  57.8 3.5 %copy-start.5 = (s32[128,4]{0,1:T(4,128)S(1)}, s32[128,4]{0,1:T(4,128)}, u32[]{:S(2)}) copy-start(s32[128,4]{0,1:T(4,128)} %param.19) | copy-start | bytes 6148
  57.8 3.9 %copy-start.2 = (s32[1,128]{1,0:T(1,128)S(1)}, s32[1,128]{1,0:T(1,128)}, u32[]{:S(2)}) copy-start(s32[1,128]{1,0:T(1,128)} %rid_row_ref.1) | copy-start | bytes 1540
  57.8 6.0 %copy-start = (bf16[128,1536]{1,0:T(8,128)(2,1)S(1)}, bf16[128,1536]{1,0:T(8,128)(2,1)}, u32[]{:S(2)}) copy-start(bf16[128,1536]{1,0:T(8,128)(2,1)} %q_ref.3) | copy-start | bytes 1179652
  57.8 6.0 %copy-start.1 = (bf16[2,128,256]{2,1,0:T(8,128)(2,1)S(1)}, bf16[2,128,256]{2,1,0:T(8,128)(2,1)}, u32[]{:S(2)}) copy-start(bf16[2,128,256]{2,1,0:T(8,128)(2,1)} %skv_ref.1) | copy-start | bytes 393220
  58.0 12.9 %collective-permute-start = (bf16[2,2048,256]{2,1,0:T(8,128)(2,1)S(1)}, bf16[2,2048,256]{2,1,0:T(8,128)(2,1)}, u32[]{:S(2)}, u32[]{:S(2)}) collective-permute-start(bf16[2,2048,256]{2,1,0:T(8,128)(2,1)S(1)} %bitcast.28), channel_id=1, source_target_pairs={{0,1},{1,0},{2,3},{3,2},{4,5},{5,4},{6,7},{7,6},{8,9},{9,8},{10,11... | collective-permute-start | bytes 6291464 | tf_op jit(solution)/shard_map/ppermute | solution.py:178
  70.8 8.6 %copy-start.3 = (bf16[128,1536]{1,0:T(8,128)(2,1)S(1)}, bf16[128,1536]{1,0:T(8,128)(2,1)}, u32[]{:S(2)}) copy-start(bf16[128,1536]{1,0:T(8,128)(2,1)} %param.12) | copy-start | bytes 1179652
  79.4 3.3 %copy-start.4 = (f32[1536]{0:T(1024)S(1)}, f32[1536]{0:T(1024)}, u32[]{:S(2)}) copy-start(f32[1536]{0:T(1024)} %param.18) | copy-start | bytes 18436
  127.9 4.0 %copy-start.6 = (f32[128,4]{0,1:T(4,128)S(1)}, f32[128,4]{0,1:T(4,128)}, u32[]{:S(2)}) copy-start(f32[128,4]{0,1:T(4,128)} %param.20) | copy-start | bytes 6148
  127.9 35.2 %all-to-all-start.3 = ((bf16[32,24,1536]{2,1,0:T(8,128)(2,1)}), bf16[32,24,1536]{2,1,0:T(8,128)(2,1)S(1)}, u32[]{:S(2)}, u32[]{:S(2)}) async-start(bf16[32,24,1536]{2,1,0:T(8,128)(2,1)} %bitcast.6), calls=%async_computation.3 | async-start | bytes 4718592 | tf_op jit(solution)/shard_map/all_to_all | solution.py:212
Sparse Core Ops, SparseCore 0:
  9.1 63.2 all-gather.1

commit v7 on v6

--- a/solution.py
+++ b/solution.py
@@ -194,7 +194,13 @@
     matches = (flat_routes[:, None] == jnp.arange(expert_count, dtype=jnp.int32)[None, :]).astype(
         jnp.int32
     )
-    slot_rank = jnp.sum((jnp.cumsum(matches, axis=0) - 1) * matches, axis=1)
+    route_count = flat_routes.shape[0]
+    earlier = (
+        lax.broadcasted_iota(jnp.int32, (route_count, route_count), 0)
+        > lax.broadcasted_iota(jnp.int32, (route_count, route_count), 1)
+    ).astype(jnp.bfloat16)
+    before = jnp.dot(earlier, matches.astype(jnp.bfloat16), preferred_element_type=jnp.float32)
+    slot_rank = jnp.sum(before.astype(jnp.int32) * matches, axis=1)
     slot_of_route = flat_routes * capacity + slot_rank
     slot_ids = jnp.arange(expert_count * capacity, dtype=jnp.int32)
     hit = slot_of_route.reshape(local_count, top_count)[:, :, None] == slot_ids[None, None, :]

time: 172 us -> 171 us (level)
  transfers between devices with their start and end apart: 3 -> 3, of which waited for: 1 -> 1; matrix products, arithmetic and copies ran while one was open for 2% -> 1% of each run, Pallas kernels for 9% -> 9%
where the time goes in v7:
time: 171 us; the launch traced here: 170 us
  blocking collectives  84.3 us (49%)
  waiting for transfers between devices  31.7 us (19%)
  Pallas kernels  25.2 us (15%)
  between operations  13.6 us (8%)
  starting transfers between devices  7.36 us (4%)
  matrix products  6.2 us (4%)
    all_to_all x1, blocking collectives, on_device(): lax.all_to_all(outgoing, EXP, split_axis=0, concat_axis=0, tiled=True)  34.7 us
    all_to_all x1, blocking collectives, on_device(): lax.all_to_all(spread, 'chip', split_axis=1, concat_axis=1, tiled=True)  33 us
    all_to_all x1, waiting for transfers between devices, on_device(): lax.all_to_all(computed, EXP, split_axis=0, concat_axis=0, tiled=True)  31 us
    all_to_all x1, blocking collectives, on_device(): lax.all_to_all(jnp.broadcast_to(prefix_key_values[:, None], (2, req_count...  16.6 us
    pallas_call x1, Pallas kernels, expert_ffn(): pl.pallas_call(expert_kernel, grid=(hidden // block,), in_specs=[pl.Block...  9.62 us
    pallas_call x1, Pallas kernels, attend_merge(): pl.pallas_call(merge_kernel, in_specs=[whole(x.shape) for x in inputs], o...  8.56 us
    pallas_call x1, Pallas kernels, attend_local(): pl.pallas_call(local_kernel, in_specs=[whole(x.shape) for x in inputs], o...  6.98 us
    all_to_all x1, starting transfers between devices, on_device(): lax.all_to_all(computed, EXP, split_axis=0, concat_axis=0, tiled=True)  3.99 us
  transfers between devices with their start and end apart: 3, of which 1 were waited for; matrix products, arithmetic and copies ran while one was open for 1% of the time, Pallas kernels for 9%

profile of v7, /device:TPU:1, one launch (start us, length us, event | category | flops | bytes accessed | tf_op | source)
XLA Modules:
  0.0 170.5 jit_solution(890113840415897584)
XLA Ops:
  6.5 0.0 all-gather.2.cloned.1.call-start
  6.5 0.7 all-gather.2.cloned.1.call-update
  7.3 0.7 broadcast_in_dim.14
  8.0 16.6 %all_to_all.20 = bf16[2,8,16,256]{3,2,0,1:T(8,128)(2,1)S(1)} all-to-all(bf16[2,8,16,256]{3,2,0,1:T(8,128)(2,1)S(1)} %broadcast_in_dim.14), channel_id=1, replica_groups=mesh['req'=8,'chip'=16,'core'=2] {'req'}, dimensions={1} | all-to-all | bytes 262144 | tf_op jit(solution)/shard_map/all_to_all | solution.py:167
  24.6 0.2 broadcast_in_dim.32
  24.8 33.0 %all_to_all.21 = bf16[2,16,128,256]{3,2,0,1:T(8,128)(2,1)S(1)} all-to-all(bf16[2,16,128,256]{3,2,0,1:T(8,128)(2,1)S(1)} %broadcast_in_dim.32), channel_id=1, replica_groups=mesh['req'=8,'chip'=16,'core'=2] {'chip'}, dimensions={1} | all-to-all | bytes 4194304 | tf_op jit(solution)/shard_map/all_to_all | solution.py:175
  57.8 0.0 copy-start.2
  57.8 0.0 copy-start.5
  57.8 0.0 copy-start
  57.8 0.0 copy-start.1
  57.8 0.1 copy.42
  58.0 3.4 %collective-permute-start = (bf16[2,2048,256]{2,1,0:T(8,128)(2,1)S(1)}, bf16[2,2048,256]{2,1,0:T(8,128)(2,1)}, u32[]{:S(2)}, u32[]{:S(2)}) collective-permute-start(bf16[2,2048,256]{2,1,0:T(8,128)(2,1)S(1)} %bitcast.13), channel_id=1, source_target_pairs={{0,1},{1,0},{2,3},{3,2},{4,5},{5,4},{6,7},{7,6},{8,9},{9,8},{10,11... | collective-permute-start | bytes 6291464 | tf_op jit(solution)/shard_map/ppermute | solution.py:178
  61.3 0.0 copy-done.2
  61.3 0.1 copy.43.rid_col_ref
  61.4 0.0 copy-done.5
  61.4 0.1 copy.44
  61.6 0.1 eq.28
  61.7 0.3 fusion.3
  61.9 0.1 reduce_sum.30
  62.1 0.1 copy.45
  62.1 0.3 fusion.1
  62.4 0.0 copy-done
  62.4 0.0 copy-done.1
  62.4 7.0 %shard_map.118 = (f32[128,1536]{1,0:T(8,128)S(1)}, f32[128,12]{1,0:T(8,128)S(1)}, f32[128,12]{1,0:T(8,128)S(1)}) custom-call(s32[128,1]{1,0:T(8,128)S(1)} %copy.43.rid_col_ref, s32[1,128]{1,0:T(1,128)S(1)} %copy-done.2, bf16[128,1536]{1,0:T(8,128)(2,1)S(1)} %copy-done, bf16[2,2048,256]{2,1,0:T(8,128)(2,1)S(1)} %bitcast.14, bf16[2,128,256]{2,1,0:T(8,128)(2,1)S(1)} %copy-done.1), custom_call_target="tpu_custom_call" | custom-call | tf_op jit(solution)/shard_map/pallas_call | solution.py:91
  69.4 0.0 copy-start.3
  69.4 0.0 collective-permute-done.pkv_ref
  69.5 8.6 %shard_map.119 = bf16[128,1536]{1,0:T(8,128)(2,1)S(1)} custom-call(bf16[128,1536]{1,0:T(8,128)(2,1)S(1)} %copy-done, bf16[2,2048,256]{2,1,0:T(8,128)(2,1)} %collective-permute-done.pkv_ref, f32[128,1536]{1,0:T(8,128)S(1)} %get-tuple-element.8.acc_ref, f32[128,12]{1,0:T(8,128)S(1)} %get-tuple-element.9.peak_ref, f32[128,12]{1,0:T(8,128)S(1)} %get-tuple-element.10.total_ref), custom_call_target="tpu_custom_call" | custom-call | tf_op jit(solution)/shard_map/pallas_call | solution.py:102
  78.0 0.0 copy-start.4
  78.0 0.0 all-gather.2.cloned.1.call-done
  78.1 0.0 copy-done.3
  78.1 3.2 %multiply_reduce_fusion = (f32[128]{0:T(128)S(1)}, f32[128,1536]{1,0:T(8,128)S(1)}) fusion(bf16[128,1536]{1,0:T(8,128)(2,1)S(1)} %shard_map.119, bf16[1536,1536]{1,0:T(8,128)(2,1)} %all-gather.2.cloned.1.call-done, bf16[128,1536]{1,0:T(8,128)(2,1)S(1)} %copy-done.3), kind=kOutput, calls=%fused_computation.12 | convolution fusion | flops 604766080 | bytes 6291968 | tf_op jit(solution)/shard_map/dot_general | solution.py:182
  81.3 0.0 copy-done.4
  81.3 0.9 convolution_convert_fusion
  82.2 34.7 %all_to_all.22 = bf16[32,24,1536]{2,1,0:T(8,128)(2,1)S(1)} all-to-all(bf16[32,24,1536]{2,1,0:T(8,128)(2,1)S(1)} %bitcast.17), channel_id=1, replica_groups=mesh['req'=8,'chip'=16,'core'=2] {'chip','core'}, dimensions={0} | all-to-all | bytes 4718592 | tf_op jit(solution)/shard_map/all_to_all | solution.py:213
  116.9 9.6 %shard_map.120 = bf16[768,1536]{1,0:T(8,128)(2,1)} custom-call(bf16[768,1536]{1,0:T(8,128)(2,1)S(1)} %bitcast.12, bf16[1,1536,768]{2,1,0:T(8,128)(2,1)} %gate_ref.1, bf16[1,1536,768]{2,1,0:T(8,128)(2,1)} %up_ref.1, bf16[1,768,1536]{2,1,0:T(8,128)(2,1)} %down_ref.1), custom_call_target="tpu_custom_call" | custom-call | tf_op jit(solution)/shard_map/pallas_call | solution.py:133
  126.5 0.0 copy-start.6
  126.5 4.0 %all-to-all-start.3 = ((bf16[32,24,1536]{2,1,0:T(8,128)(2,1)}), bf16[32,24,1536]{2,1,0:T(8,128)(2,1)S(1)}, u32[]{:S(2)}, u32[]{:S(2)}) async-start(bf16[32,24,1536]{2,1,0:T(8,128)(2,1)} %bitcast.5), calls=%async_computation.3 | async-start | bytes 4718592 | tf_op jit(solution)/shard_map/all_to_all | solution.py:218
  130.5 0.0 copy-done.6
  130.5 0.2 select_reduce_fusion
  130.8 31.0 %all-to-all-done.3 = bf16[32,24,1536]{2,1,0:T(8,128)(2,1)S(1)} async-done(((bf16[32,24,1536]{2,1,0:T(8,128)(2,1)}), bf16[32,24,1536]{2,1,0:T(8,128)(2,1)S(1)}, u32[]{:S(2)}, u32[]{:S(2)}) %all-to-all-start.3) | async-done | bytes 2359328 | tf_op jit(solution)/shard_map/all_to_all | solution.py:218
  161.8 1.8 %fusion = bf16[128,1536]{1,0:T(8,128)(2,1)} fusion(f32[128,1536]{1,0:T(8,128)S(1)} %get-tuple-element.12, f32[128,768]{1,0:T(8,128)S(1)} %select_reduce_fusion, bf16[768,1536]{1,0:T(8,128)(2,1)S(1)} %bitcast.16), kind=kOutput, calls=%fused_computation.3 | convolution fusion | flops 1812332544 | bytes 3932160 | tf_op jit(solution)/shard_map/dot_general | solution.py:220
  (3 shorter events, 0.0 us)
Async XLA Ops:
  6.5 71.5 %all-gather.2.cloned.1.call-start = ((), (), s32[]{:S(2)}) async-start(), calls=%async_computation.4 | async-start | bytes 5308416 | tf_op jit(solution)/shard_map/all_gather | solution.py:184
  57.8 3.5 %copy-start.2 = (s32[1,128]{1,0:T(1,128)S(1)}, s32[1,128]{1,0:T(1,128)}, u32[]{:S(2)}) copy-start(s32[1,128]{1,0:T(1,128)} %rid_row_ref.1) | copy-start | bytes 1540
  57.8 3.6 %copy-start.5 = (s32[128,4]{0,1:T(4,128)S(1)}, s32[128,4]{0,1:T(4,128)}, u32[]{:S(2)}) copy-start(s32[128,4]{0,1:T(4,128)} %param.19) | copy-start | bytes 6148
  57.8 4.6 %copy-start = (bf16[128,1536]{1,0:T(8,128)(2,1)S(1)}, bf16[128,1536]{1,0:T(8,128)(2,1)}, u32[]{:S(2)}) copy-start(bf16[128,1536]{1,0:T(8,128)(2,1)} %q_ref.3) | copy-start | bytes 1179652
  57.8 4.6 %copy-start.1 = (bf16[2,128,256]{2,1,0:T(8,128)(2,1)S(1)}, bf16[2,128,256]{2,1,0:T(8,128)(2,1)}, u32[]{:S(2)}) copy-start(bf16[2,128,256]{2,1,0:T(8,128)(2,1)} %skv_ref.1) | copy-start | bytes 393220
  58.0 11.5 %collective-permute-start = (bf16[2,2048,256]{2,1,0:T(8,128)(2,1)S(1)}, bf16[2,2048,256]{2,1,0:T(8,128)(2,1)}, u32[]{:S(2)}, u32[]{:S(2)}) collective-permute-start(bf16[2,2048,256]{2,1,0:T(8,128)(2,1)S(1)} %bitcast.13), channel_id=1, source_target_pairs={{0,1},{1,0},{2,3},{3,2},{4,5},{5,4},{6,7},{7,6},{8,9},{9,8},{10,11... | collective-permute-start | bytes 6291464 | tf_op jit(solution)/shard_map/ppermute | solution.py:178
  69.4 8.6 %copy-start.3 = (bf16[128,1536]{1,0:T(8,128)(2,1)S(1)}, bf16[128,1536]{1,0:T(8,128)(2,1)}, u32[]{:S(2)}) copy-start(bf16[128,1536]{1,0:T(8,128)(2,1)} %param.12) | copy-start | bytes 1179652
  78.0 3.3 %copy-start.4 = (f32[1536]{0:T(1024)S(1)}, f32[1536]{0:T(1024)}, u32[]{:S(2)}) copy-start(f32[1536]{0:T(1024)} %param.18) | copy-start | bytes 18436
  126.5 4.0 %copy-start.6 = (f32[128,4]{0,1:T(4,128)S(1)}, f32[128,4]{0,1:T(4,128)}, u32[]{:S(2)}) copy-start(f32[128,4]{0,1:T(4,128)} %param.20) | copy-start | bytes 6148
  126.5 35.2 %all-to-all-start.3 = ((bf16[32,24,1536]{2,1,0:T(8,128)(2,1)}), bf16[32,24,1536]{2,1,0:T(8,128)(2,1)S(1)}, u32[]{:S(2)}, u32[]{:S(2)}) async-start(bf16[32,24,1536]{2,1,0:T(8,128)(2,1)} %bitcast.5), calls=%async_computation.3 | async-start | bytes 4718592 | tf_op jit(solution)/shard_map/all_to_all | solution.py:218
Sparse Core Ops, SparseCore 0:
  9.1 63.2 all-gather.1

commit v8 on v7

--- a/solution.py
+++ b/solution.py
@@ -30,12 +30,10 @@
     position = lax.broadcasted_iota(jnp.int32, (local_count, local_count), 0)
     key_position = lax.broadcasted_iota(jnp.int32, (local_count, local_count), 1)
     allowed = (rid_col_ref[...] == rid_row_ref[...]) & (position >= key_position)
-    groups = QUERY_HEADS // KEY_VALUE_HEADS
-    for head in range(QUERY_HEADS):
-        kv_columns = slice((head // groups) * HEAD_SIZE, (head // groups + 1) * HEAD_SIZE)
+    for head in range(QUERY_HEADS // KEY_VALUE_HEADS):
         columns = slice(head * HEAD_SIZE, (head + 1) * HEAD_SIZE)
-        prefix_scores = head_scores(q_ref, pkv_ref[0, :, kv_columns], head)
-        suffix_scores = head_scores(q_ref, skv_ref[0, :, kv_columns], head)
+        prefix_scores = head_scores(q_ref, pkv_ref[0], head)
+        suffix_scores = head_scores(q_ref, skv_ref[0], head)
         suffix_scores = jnp.where(allowed, suffix_scores, MASKED_SCORE)
         peak = jnp.maximum(
             jnp.max(prefix_scores, axis=1, keepdims=True),
@@ -48,27 +46,21 @@
         )
         peak_ref[:, head : head + 1] = peak
         acc_ref[:, columns] = jnp.dot(
-            prefix_weights.astype(jnp.bfloat16),
-            pkv_ref[1, :, kv_columns],
-            preferred_element_type=jnp.float32,
+            prefix_weights.astype(jnp.bfloat16), pkv_ref[1], preferred_element_type=jnp.float32
         ) + jnp.dot(
-            suffix_weights.astype(jnp.bfloat16),
-            skv_ref[1, :, kv_columns],
-            preferred_element_type=jnp.float32,
+            suffix_weights.astype(jnp.bfloat16), skv_ref[1], preferred_element_type=jnp.float32
         )
 
 
 def merge_kernel(q_ref, pkv_ref, acc_ref, peak_ref, total_ref, out_ref):
-    groups = QUERY_HEADS // KEY_VALUE_HEADS
-    for head in range(QUERY_HEADS):
-        kv_columns = slice((head // groups) * HEAD_SIZE, (head // groups + 1) * HEAD_SIZE)
+    for head in range(QUERY_HEADS // KEY_VALUE_HEADS):
         columns = slice(head * HEAD_SIZE, (head + 1) * HEAD_SIZE)
-        scores = head_scores(q_ref, pkv_ref[0, :, kv_columns], head)
+        scores = head_scores(q_ref, pkv_ref[0], head)
         own_peak = jnp.max(scores, axis=1, keepdims=True)
         weights = jnp.exp(scores - own_peak)
         own_total = jnp.sum(weights, axis=1, keepdims=True)
         own_acc = jnp.dot(
-            weights.astype(jnp.bfloat16), pkv_ref[1, :, kv_columns], preferred_element_type=jnp.float32
+            weights.astype(jnp.bfloat16), pkv_ref[1], preferred_element_type=jnp.float32
         )
         first_peak = peak_ref[:, head : head + 1]
         peak = jnp.maximum(first_peak, own_peak)
@@ -79,33 +71,53 @@
         out_ref[:, columns] = (summed / total).astype(out_ref.dtype)
 
 
-def whole(shape):
-    return pl.BlockSpec(shape, lambda: (0,) * len(shape))
+def group_specs(local_count, model_width, prefix_count):
+    group_width = model_width // KEY_VALUE_HEADS
+    groups = QUERY_HEADS // KEY_VALUE_HEADS
+    rows = pl.BlockSpec((local_count, group_width), lambda g: (0, g))
+    keys = pl.BlockSpec((2, prefix_count, HEAD_SIZE), lambda g: (0, 0, g))
+    stats = pl.BlockSpec((None, local_count, groups), lambda g: (g, 0, 0))
+    return rows, keys, stats
 
 
 def attend_local(queries, prefix_key_values, suffix_key_values, request_ids):
     local_count, model_width = queries.shape
-    column, row = request_ids.reshape(local_count, 1), request_ids.reshape(1, local_count)
-    inputs = (column, row, queries, prefix_key_values, suffix_key_values)
-    stats = jax.ShapeDtypeStruct((local_count, QUERY_HEADS), jnp.float32)
+    rows, keys, stats = group_specs(local_count, model_width, prefix_key_values.shape[1])
+    stat_shape = jax.ShapeDtypeStruct(
+        (KEY_VALUE_HEADS, local_count, QUERY_HEADS // KEY_VALUE_HEADS), jnp.float32
+    )
     return pl.pallas_call(
         local_kernel,
-        in_specs=[whole(x.shape) for x in inputs],
-        out_specs=[whole((local_count, model_width)), whole(stats.shape), whole(stats.shape)],
-        out_shape=[jax.ShapeDtypeStruct((local_count, model_width), jnp.float32), stats, stats],
+        grid=(KEY_VALUE_HEADS,),
+        in_specs=[
+            pl.BlockSpec((local_count, 1), lambda g: (0, 0)),
+            pl.BlockSpec((1, local_count), lambda g: (0, 0)),
+            rows,
+            keys,
+            pl.BlockSpec((2, local_count, HEAD_SIZE), lambda g: (0, 0, g)),
+        ],
+        out_specs=[rows, stats, stats],
+        out_shape=[
+            jax.ShapeDtypeStruct((local_count, model_width), jnp.float32),
+            stat_shape,
+            stat_shape,
+        ],
         compiler_params=pltpu.CompilerParams(vmem_limit_bytes=48 * 1024 * 1024),
-    )(*inputs)
+    )(request_ids.reshape(local_count, 1), request_ids.reshape(1, local_count), queries,
+      prefix_key_values, suffix_key_values)
 
 
 def attend_merge(queries, prefix_key_values, acc, peak, total):
-    inputs = (queries, prefix_key_values, acc, peak, total)
+    local_count, model_width = queries.shape
+    rows, keys, stats = group_specs(local_count, model_width, prefix_key_values.shape[1])
     return pl.pallas_call(
         merge_kernel,
-        in_specs=[whole(x.shape) for x in inputs],
-        out_specs=whole(queries.shape),
+        grid=(KEY_VALUE_HEADS,),
+        in_specs=[rows, keys, rows, stats, stats],
+        out_specs=rows,
         out_shape=jax.ShapeDtypeStruct(queries.shape, jnp.bfloat16),
         compiler_params=pltpu.CompilerParams(vmem_limit_bytes=48 * 1024 * 1024),
-    )(*inputs)
+    )(queries, prefix_key_values, acc, peak, total)
 
 
 def expert_kernel(rows_ref, gate_ref, up_ref, down_ref, out_ref, acc_ref):

time: 171 us -> 171 us (level)
  no operation moved by 1% of the time
where the time goes in v8:
time: 171 us
  blocking collectives  84.3 us (49%)
  waiting for transfers between devices  31.7 us (19%)
  Pallas kernels  25.4 us (15%)
  between operations  13.6 us (8%)
  starting transfers between devices  7.36 us (4%)
  matrix products  6.2 us (4%)
    all_to_all x1, blocking collectives, on_device(): lax.all_to_all(outgoing, EXP, split_axis=0, concat_axis=0, tiled=True)  34.7 us
    all_to_all x1, blocking collectives, on_device(): lax.all_to_all(spread, 'chip', split_axis=1, concat_axis=1, tiled=True)  33 us
    all_to_all x1, waiting for transfers between devices, on_device(): lax.all_to_all(computed, EXP, split_axis=0, concat_axis=0, tiled=True)  31 us
    all_to_all x1, blocking collectives, on_device(): lax.all_to_all(jnp.broadcast_to(prefix_key_values[:, None], (2, req_count...  16.6 us
    pallas_call x1, Pallas kernels, expert_ffn(): pl.pallas_call(expert_kernel, grid=(hidden // block,), in_specs=[pl.Block...  9.62 us
    pallas_call x1, Pallas kernels, attend_merge(): pl.pallas_call(merge_kernel, grid=(KEY_VALUE_HEADS,), in_specs=[rows, key...  8.16 us
    pallas_call x1, Pallas kernels, attend_local(): pl.pallas_call(local_kernel, grid=(KEY_VALUE_HEADS,), in_specs=[pl.BlockS...  7.6 us
    all_to_all x1, starting transfers between devices, on_device(): lax.all_to_all(computed, EXP, split_axis=0, concat_axis=0, tiled=True)  3.99 us
  transfers between devices with their start and end apart: 3, of which 1 were waited for; matrix products, arithmetic and copies ran while one was open for 1% of the time, Pallas kernels for 9%

profile of v8, /device:TPU:1, one launch (start us, length us, event | category | flops | bytes accessed | tf_op | source)
XLA Modules:
  0.0 170.7 jit_solution(5939059752450863999)
XLA Ops:
  6.5 0.0 all-gather.2.cloned.1.call-start
  6.5 0.7 all-gather.2.cloned.1.call-update
  7.3 0.7 broadcast_in_dim.14
  8.0 16.6 %all_to_all.20 = bf16[2,8,16,256]{3,2,0,1:T(8,128)(2,1)S(1)} all-to-all(bf16[2,8,16,256]{3,2,0,1:T(8,128)(2,1)S(1)} %broadcast_in_dim.14), channel_id=1, replica_groups=mesh['req'=8,'chip'=16,'core'=2] {'req'}, dimensions={1} | all-to-all | bytes 262144 | tf_op jit(solution)/shard_map/all_to_all | solution.py:179
  24.6 0.2 broadcast_in_dim.32
  24.8 33.0 %all_to_all.21 = bf16[2,16,128,256]{3,2,0,1:T(8,128)(2,1)S(1)} all-to-all(bf16[2,16,128,256]{3,2,0,1:T(8,128)(2,1)S(1)} %broadcast_in_dim.32), channel_id=1, replica_groups=mesh['req'=8,'chip'=16,'core'=2] {'chip'}, dimensions={1} | all-to-all | bytes 4194304 | tf_op jit(solution)/shard_map/all_to_all | solution.py:187
  57.8 0.0 copy-start.2
  57.8 0.0 copy-start.5
  57.8 0.0 copy-start
  57.8 0.0 copy-start.1
  57.8 0.1 copy.42
  58.0 3.4 %collective-permute-start = (bf16[2,2048,256]{2,1,0:T(8,128)(2,1)S(1)}, bf16[2,2048,256]{2,1,0:T(8,128)(2,1)}, u32[]{:S(2)}, u32[]{:S(2)}) collective-permute-start(bf16[2,2048,256]{2,1,0:T(8,128)(2,1)S(1)} %bitcast.13), channel_id=1, source_target_pairs={{0,1},{1,0},{2,3},{3,2},{4,5},{5,4},{6,7},{7,6},{8,9},{9,8},{10,11... | collective-permute-start | bytes 6291464 | tf_op jit(solution)/shard_map/ppermute | solution.py:190
  61.3 0.0 copy-done.2
  61.3 0.1 copy.43.rid_col_ref
  61.4 0.0 copy-done.5
  61.4 0.1 copy.44
  61.6 0.1 eq.28
  61.7 0.3 fusion.3
  61.9 0.1 reduce_sum.30
  62.1 0.1 copy.45
  62.1 0.3 fusion.1
  62.4 0.0 copy-done
  62.4 0.0 copy-done.1
  62.4 7.6 %shard_map.118 = (f32[128,1536]{1,0:T(8,128)S(1)}, f32[2,128,6]{2,1,0:T(8,128)S(1)}, f32[2,128,6]{2,1,0:T(8,128)S(1)}) custom-call(s32[128,1]{1,0:T(8,128)S(1)} %copy.43.rid_col_ref, s32[1,128]{1,0:T(1,128)S(1)} %copy-done.2, bf16[128,1536]{1,0:T(8,128)(2,1)S(1)} %copy-done, bf16[2,2048,256]{2,1,0:T(8,128)(2,1)S(1)} %bitcast.14, ...), custom_call_target="tpu_custom_call" | custom-call | tf_op jit(solution)/shard_map/pallas_call | solution.py:89
  70.1 0.0 copy-start.3
  70.1 0.0 collective-permute-done.pkv_ref
  70.1 8.2 %shard_map.119 = bf16[128,1536]{1,0:T(8,128)(2,1)S(1)} custom-call(bf16[128,1536]{1,0:T(8,128)(2,1)S(1)} %copy-done, bf16[2,2048,256]{2,1,0:T(8,128)(2,1)} %collective-permute-done.pkv_ref, f32[128,1536]{1,0:T(8,128)S(1)} %get-tuple-element.8.acc_ref, f32[2,128,6]{2,1,0:T(8,128)S(1)} %get-tuple-element.9.peak_ref, f32[2,128,6]{2,1,0:T(8,128)S(1)} %get-tuple-element.10.total_ref), custom_call_target="tpu_custom_call" | custom-call | tf_op jit(solution)/shard_map/pallas_call | solution.py:113
  78.3 0.0 copy-start.4
  78.3 0.0 all-gather.2.cloned.1.call-done
  78.3 0.0 copy-done.3
  78.3 3.2 %multiply_reduce_fusion = (f32[128]{0:T(128)S(1)}, f32[128,1536]{1,0:T(8,128)S(1)}) fusion(bf16[128,1536]{1,0:T(8,128)(2,1)S(1)} %shard_map.119, bf16[1536,1536]{1,0:T(8,128)(2,1)} %all-gather.2.cloned.1.call-done, bf16[128,1536]{1,0:T(8,128)(2,1)S(1)} %copy-done.3), kind=kOutput, calls=%fused_computation.12 | convolution fusion | flops 604766080 | bytes 6291968 | tf_op jit(solution)/shard_map/dot_general | solution.py:194
  81.5 0.0 copy-done.4
  81.5 0.9 convolution_convert_fusion
  82.4 34.7 %all_to_all.22 = bf16[32,24,1536]{2,1,0:T(8,128)(2,1)S(1)} all-to-all(bf16[32,24,1536]{2,1,0:T(8,128)(2,1)S(1)} %bitcast.17), channel_id=1, replica_groups=mesh['req'=8,'chip'=16,'core'=2] {'chip','core'}, dimensions={0} | all-to-all | bytes 4718592 | tf_op jit(solution)/shard_map/all_to_all | solution.py:225
  117.1 9.6 %shard_map.120 = bf16[768,1536]{1,0:T(8,128)(2,1)} custom-call(bf16[768,1536]{1,0:T(8,128)(2,1)S(1)} %bitcast.12, bf16[1,1536,768]{2,1,0:T(8,128)(2,1)} %gate_ref.1, bf16[1,1536,768]{2,1,0:T(8,128)(2,1)} %up_ref.1, bf16[1,768,1536]{2,1,0:T(8,128)(2,1)} %down_ref.1), custom_call_target="tpu_custom_call" | custom-call | tf_op jit(solution)/shard_map/pallas_call | solution.py:145
  126.7 0.0 copy-start.6
  126.7 4.0 %all-to-all-start.3 = ((bf16[32,24,1536]{2,1,0:T(8,128)(2,1)}), bf16[32,24,1536]{2,1,0:T(8,128)(2,1)S(1)}, u32[]{:S(2)}, u32[]{:S(2)}) async-start(bf16[32,24,1536]{2,1,0:T(8,128)(2,1)} %bitcast.5), calls=%async_computation.3 | async-start | bytes 4718592 | tf_op jit(solution)/shard_map/all_to_all | solution.py:230
  130.7 0.0 copy-done.6
  130.7 0.2 select_reduce_fusion
  131.0 31.0 %all-to-all-done.3 = bf16[32,24,1536]{2,1,0:T(8,128)(2,1)S(1)} async-done(((bf16[32,24,1536]{2,1,0:T(8,128)(2,1)}), bf16[32,24,1536]{2,1,0:T(8,128)(2,1)S(1)}, u32[]{:S(2)}, u32[]{:S(2)}) %all-to-all-start.3) | async-done | bytes 2359328 | tf_op jit(solution)/shard_map/all_to_all | solution.py:230
  162.0 1.8 %fusion = bf16[128,1536]{1,0:T(8,128)(2,1)} fusion(f32[128,1536]{1,0:T(8,128)S(1)} %get-tuple-element.12, f32[128,768]{1,0:T(8,128)S(1)} %select_reduce_fusion, bf16[768,1536]{1,0:T(8,128)(2,1)S(1)} %bitcast.16), kind=kOutput, calls=%fused_computation.3 | convolution fusion | flops 1812332544 | bytes 3932160 | tf_op jit(solution)/shard_map/dot_general | solution.py:232
  (3 shorter events, 0.0 us)
Async XLA Ops:
  6.5 71.8 %all-gather.2.cloned.1.call-start = ((), (), s32[]{:S(2)}) async-start(), calls=%async_computation.4 | async-start | bytes 5308416 | tf_op jit(solution)/shard_map/all_gather | solution.py:196
  57.8 3.5 %copy-start.2 = (s32[1,128]{1,0:T(1,128)S(1)}, s32[1,128]{1,0:T(1,128)}, u32[]{:S(2)}) copy-start(s32[1,128]{1,0:T(1,128)} %rid_row_ref.1) | copy-start | bytes 1540
  57.8 3.6 %copy-start.5 = (s32[128,4]{0,1:T(4,128)S(1)}, s32[128,4]{0,1:T(4,128)}, u32[]{:S(2)}) copy-start(s32[128,4]{0,1:T(4,128)} %param.19) | copy-start | bytes 6148
  57.8 4.6 %copy-start = (bf16[128,1536]{1,0:T(8,128)(2,1)S(1)}, bf16[128,1536]{1,0:T(8,128)(2,1)}, u32[]{:S(2)}) copy-start(bf16[128,1536]{1,0:T(8,128)(2,1)} %q_ref.3) | copy-start | bytes 1179652
  57.8 4.6 %copy-start.1 = (bf16[2,128,256]{2,1,0:T(8,128)(2,1)S(1)}, bf16[2,128,256]{2,1,0:T(8,128)(2,1)}, u32[]{:S(2)}) copy-start(bf16[2,128,256]{2,1,0:T(8,128)(2,1)} %skv_ref.1) | copy-start | bytes 393220
  58.0 12.1 %collective-permute-start = (bf16[2,2048,256]{2,1,0:T(8,128)(2,1)S(1)}, bf16[2,2048,256]{2,1,0:T(8,128)(2,1)}, u32[]{:S(2)}, u32[]{:S(2)}) collective-permute-start(bf16[2,2048,256]{2,1,0:T(8,128)(2,1)S(1)} %bitcast.13), channel_id=1, source_target_pairs={{0,1},{1,0},{2,3},{3,2},{4,5},{5,4},{6,7},{7,6},{8,9},{9,8},{10,11... | collective-permute-start | bytes 6291464 | tf_op jit(solution)/shard_map/ppermute | solution.py:190
  70.1 8.2 %copy-start.3 = (bf16[128,1536]{1,0:T(8,128)(2,1)S(1)}, bf16[128,1536]{1,0:T(8,128)(2,1)}, u32[]{:S(2)}) copy-start(bf16[128,1536]{1,0:T(8,128)(2,1)} %param.12) | copy-start | bytes 1179652
  78.3 3.3 %copy-start.4 = (f32[1536]{0:T(1024)S(1)}, f32[1536]{0:T(1024)}, u32[]{:S(2)}) copy-start(f32[1536]{0:T(1024)} %param.18) | copy-start | bytes 18436
  126.7 4.0 %copy-start.6 = (f32[128,4]{0,1:T(4,128)S(1)}, f32[128,4]{0,1:T(4,128)}, u32[]{:S(2)}) copy-start(f32[128,4]{0,1:T(4,128)} %param.20) | copy-start | bytes 6148
  126.7 35.2 %all-to-all-start.3 = ((bf16[32,24,1536]{2,1,0:T(8,128)(2,1)}), bf16[32,24,1536]{2,1,0:T(8,128)(2,1)S(1)}, u32[]{:S(2)}, u32[]{:S(2)}) async-start(bf16[32,24,1536]{2,1,0:T(8,128)(2,1)} %bitcast.5), calls=%async_computation.3 | async-start | bytes 4718592 | tf_op jit(solution)/shard_map/all_to_all | solution.py:230
Sparse Core Ops, SparseCore 0:
  9.1 63.2 all-gather.1

commit v9 on v7

--- a/solution.py
+++ b/solution.py
@@ -217,12 +217,13 @@
     computed = produced.reshape(senders, slot_count, features)
     returned = lax.all_to_all(computed, EXP, split_axis=0, concat_axis=0, tiled=True)
     slot_gates = jnp.sum(jnp.where(hit, route_gates[:, :, None], 0.0), axis=1)
-    combined = jnp.dot(
-        slot_gates,
-        returned.reshape(expert_count * capacity, model_width).astype(jnp.float32),
-        precision=lax.Precision.HIGHEST,
-        preferred_element_type=jnp.float32,
-    )
+    returned_rows = returned.reshape(expert_count * capacity, model_width)
+    combined = jnp.zeros((local_count, model_width), jnp.float32)
+    remainder = slot_gates
+    for _ in range(3):
+        piece = remainder.astype(jnp.bfloat16)
+        combined = combined + jnp.dot(piece, returned_rows, preferred_element_type=jnp.float32)
+        remainder = remainder - piece.astype(jnp.float32)
     return (stream + combined).astype(jnp.bfloat16)
 
 

time: 171 us -> 171 us (level)
  no operation moved by 1% of the time
where the time goes in v9:
time: 171 us
  blocking collectives  84.3 us (49%)
  waiting for transfers between devices  31.7 us (19%)
  Pallas kernels  25.2 us (15%)
  between operations  13.6 us (8%)
  starting transfers between devices  7.36 us (4%)
  matrix products  6.59 us (4%)
    all_to_all x1, blocking collectives, on_device(): lax.all_to_all(outgoing, EXP, split_axis=0, concat_axis=0, tiled=True)  34.7 us
    all_to_all x1, blocking collectives, on_device(): lax.all_to_all(spread, 'chip', split_axis=1, concat_axis=1, tiled=True)  33 us
    all_to_all x1, waiting for transfers between devices, on_device(): lax.all_to_all(computed, EXP, split_axis=0, concat_axis=0, tiled=True)  31 us
    all_to_all x1, blocking collectives, on_device(): lax.all_to_all(jnp.broadcast_to(prefix_key_values[:, None], (2, req_count...  16.6 us
    pallas_call x1, Pallas kernels, expert_ffn(): pl.pallas_call(expert_kernel, grid=(hidden // block,), in_specs=[pl.Block...  9.62 us
    pallas_call x1, Pallas kernels, attend_merge(): pl.pallas_call(merge_kernel, in_specs=[whole(x.shape) for x in inputs], o...  8.56 us
    pallas_call x1, Pallas kernels, attend_local(): pl.pallas_call(local_kernel, in_specs=[whole(x.shape) for x in inputs], o...  6.98 us
    all_to_all x1, starting transfers between devices, on_device(): lax.all_to_all(computed, EXP, split_axis=0, concat_axis=0, tiled=True)  3.99 us
  transfers between devices with their start and end apart: 3, of which 1 were waited for; matrix products, arithmetic and copies ran while one was open for 1% of the time, Pallas kernels for 9%

profile of v9, /device:TPU:1, one launch (start us, length us, event | category | flops | bytes accessed | tf_op | source)
XLA Modules:
  0.0 170.9 jit_solution(12058767502498320037)
XLA Ops:
  6.5 0.0 all-gather.2.cloned.1.call-start
  6.5 0.7 all-gather.2.cloned.1.call-update
  7.3 0.7 broadcast_in_dim.14
  8.0 16.6 %all_to_all.20 = bf16[2,8,16,256]{3,2,0,1:T(8,128)(2,1)S(1)} all-to-all(bf16[2,8,16,256]{3,2,0,1:T(8,128)(2,1)S(1)} %broadcast_in_dim.14), channel_id=1, replica_groups=mesh['req'=8,'chip'=16,'core'=2] {'req'}, dimensions={1} | all-to-all | bytes 262144 | tf_op jit(solution)/shard_map/all_to_all | solution.py:167
  24.6 0.2 broadcast_in_dim.32
  24.8 33.0 %all_to_all.21 = bf16[2,16,128,256]{3,2,0,1:T(8,128)(2,1)S(1)} all-to-all(bf16[2,16,128,256]{3,2,0,1:T(8,128)(2,1)S(1)} %broadcast_in_dim.32), channel_id=1, replica_groups=mesh['req'=8,'chip'=16,'core'=2] {'chip'}, dimensions={1} | all-to-all | bytes 4194304 | tf_op jit(solution)/shard_map/all_to_all | solution.py:175
  57.8 0.0 copy-start.2
  57.8 0.0 copy-start.5
  57.8 0.0 copy-start
  57.8 0.0 copy-start.1
  57.8 0.1 copy.42
  58.0 3.4 %collective-permute-start = (bf16[2,2048,256]{2,1,0:T(8,128)(2,1)S(1)}, bf16[2,2048,256]{2,1,0:T(8,128)(2,1)}, u32[]{:S(2)}, u32[]{:S(2)}) collective-permute-start(bf16[2,2048,256]{2,1,0:T(8,128)(2,1)S(1)} %bitcast.14), channel_id=1, source_target_pairs={{0,1},{1,0},{2,3},{3,2},{4,5},{5,4},{6,7},{7,6},{8,9},{9,8},{10,11... | collective-permute-start | bytes 6291464 | tf_op jit(solution)/shard_map/ppermute | solution.py:178
  61.3 0.0 copy-done.2
  61.3 0.1 copy.43.rid_col_ref
  61.4 0.0 copy-done.5
  61.4 0.1 copy.44
  61.6 0.1 eq.28
  61.7 0.3 fusion.4
  61.9 0.1 reduce_sum.30
  62.1 0.1 copy.45
  62.1 0.3 fusion.2
  62.4 0.0 copy-done
  62.4 0.0 copy-done.1
  62.4 7.0 %shard_map.118 = (f32[128,1536]{1,0:T(8,128)S(1)}, f32[128,12]{1,0:T(8,128)S(1)}, f32[128,12]{1,0:T(8,128)S(1)}) custom-call(s32[128,1]{1,0:T(8,128)S(1)} %copy.43.rid_col_ref, s32[1,128]{1,0:T(1,128)S(1)} %copy-done.2, bf16[128,1536]{1,0:T(8,128)(2,1)S(1)} %copy-done, bf16[2,2048,256]{2,1,0:T(8,128)(2,1)S(1)} %bitcast.15, bf16[2,128,256]{2,1,0:T(8,128)(2,1)S(1)} %copy-done.1), custom_call_target="tpu_custom_call" | custom-call | tf_op jit(solution)/shard_map/pallas_call | solution.py:91
  69.4 0.0 copy-start.3
  69.4 0.0 collective-permute-done.pkv_ref
  69.5 8.6 %shard_map.119 = bf16[128,1536]{1,0:T(8,128)(2,1)S(1)} custom-call(bf16[128,1536]{1,0:T(8,128)(2,1)S(1)} %copy-done, bf16[2,2048,256]{2,1,0:T(8,128)(2,1)} %collective-permute-done.pkv_ref, f32[128,1536]{1,0:T(8,128)S(1)} %get-tuple-element.8.acc_ref, f32[128,12]{1,0:T(8,128)S(1)} %get-tuple-element.9.peak_ref, f32[128,12]{1,0:T(8,128)S(1)} %get-tuple-element.10.total_ref), custom_call_target="tpu_custom_call" | custom-call | tf_op jit(solution)/shard_map/pallas_call | solution.py:102
  78.0 0.0 copy-start.4
  78.0 0.0 all-gather.2.cloned.1.call-done
  78.1 0.0 copy-done.3
  78.1 3.2 %multiply_reduce_fusion = (f32[128]{0:T(128)S(1)}, f32[128,1536]{1,0:T(8,128)S(1)}) fusion(bf16[128,1536]{1,0:T(8,128)(2,1)S(1)} %shard_map.119, bf16[1536,1536]{1,0:T(8,128)(2,1)} %all-gather.2.cloned.1.call-done, bf16[128,1536]{1,0:T(8,128)(2,1)S(1)} %copy-done.3), kind=kOutput, calls=%fused_computation.14 | convolution fusion | flops 604766080 | bytes 6291968 | tf_op jit(solution)/shard_map/dot_general | solution.py:182
  81.3 0.0 copy-done.4
  81.3 0.9 convolution_convert_fusion
  82.2 34.7 %all_to_all.22 = bf16[32,24,1536]{2,1,0:T(8,128)(2,1)S(1)} all-to-all(bf16[32,24,1536]{2,1,0:T(8,128)(2,1)S(1)} %bitcast.20), channel_id=1, replica_groups=mesh['req'=8,'chip'=16,'core'=2] {'chip','core'}, dimensions={0} | all-to-all | bytes 4718592 | tf_op jit(solution)/shard_map/all_to_all | solution.py:213
  116.9 9.6 %shard_map.120 = bf16[768,1536]{1,0:T(8,128)(2,1)} custom-call(bf16[768,1536]{1,0:T(8,128)(2,1)S(1)} %bitcast.13, bf16[1,1536,768]{2,1,0:T(8,128)(2,1)} %gate_ref.1, bf16[1,1536,768]{2,1,0:T(8,128)(2,1)} %up_ref.1, bf16[1,768,1536]{2,1,0:T(8,128)(2,1)} %down_ref.1), custom_call_target="tpu_custom_call" | custom-call | tf_op jit(solution)/shard_map/pallas_call | solution.py:133
  126.5 0.0 copy-start.6
  126.5 4.0 %all-to-all-start.3 = ((bf16[32,24,1536]{2,1,0:T(8,128)(2,1)}), bf16[32,24,1536]{2,1,0:T(8,128)(2,1)S(1)}, u32[]{:S(2)}, u32[]{:S(2)}) async-start(bf16[32,24,1536]{2,1,0:T(8,128)(2,1)} %bitcast.5), calls=%async_computation.3 | async-start | bytes 4718592 | tf_op jit(solution)/shard_map/all_to_all | solution.py:218
  130.5 0.0 copy-done.6
  130.5 0.2 select_reduce_fusion
  130.8 31.0 %all-to-all-done.3 = bf16[32,24,1536]{2,1,0:T(8,128)(2,1)S(1)} async-done(((bf16[32,24,1536]{2,1,0:T(8,128)(2,1)}), bf16[32,24,1536]{2,1,0:T(8,128)(2,1)S(1)}, u32[]{:S(2)}, u32[]{:S(2)}) %all-to-all-start.3) | async-done | bytes 2359328 | tf_op jit(solution)/shard_map/all_to_all | solution.py:218
  161.8 0.5 fusion.8
  162.3 0.5 convolution_add_fusion.1
  162.8 1.3 fusion.1
  (3 shorter events, 0.0 us)
Async XLA Ops:
  6.5 71.5 %all-gather.2.cloned.1.call-start = ((), (), s32[]{:S(2)}) async-start(), calls=%async_computation.4 | async-start | bytes 5308416 | tf_op jit(solution)/shard_map/all_gather | solution.py:184
  57.8 3.5 %copy-start.2 = (s32[1,128]{1,0:T(1,128)S(1)}, s32[1,128]{1,0:T(1,128)}, u32[]{:S(2)}) copy-start(s32[1,128]{1,0:T(1,128)} %rid_row_ref.1) | copy-start | bytes 1540
  57.8 3.6 %copy-start.5 = (s32[128,4]{0,1:T(4,128)S(1)}, s32[128,4]{0,1:T(4,128)}, u32[]{:S(2)}) copy-start(s32[128,4]{0,1:T(4,128)} %param.19) | copy-start | bytes 6148
  57.8 4.6 %copy-start = (bf16[128,1536]{1,0:T(8,128)(2,1)S(1)}, bf16[128,1536]{1,0:T(8,128)(2,1)}, u32[]{:S(2)}) copy-start(bf16[128,1536]{1,0:T(8,128)(2,1)} %q_ref.3) | copy-start | bytes 1179652
  57.8 4.6 %copy-start.1 = (bf16[2,128,256]{2,1,0:T(8,128)(2,1)S(1)}, bf16[2,128,256]{2,1,0:T(8,128)(2,1)}, u32[]{:S(2)}) copy-start(bf16[2,128,256]{2,1,0:T(8,128)(2,1)} %skv_ref.1) | copy-start | bytes 393220
  58.0 11.5 %collective-permute-start = (bf16[2,2048,256]{2,1,0:T(8,128)(2,1)S(1)}, bf16[2,2048,256]{2,1,0:T(8,128)(2,1)}, u32[]{:S(2)}, u32[]{:S(2)}) collective-permute-start(bf16[2,2048,256]{2,1,0:T(8,128)(2,1)S(1)} %bitcast.14), channel_id=1, source_target_pairs={{0,1},{1,0},{2,3},{3,2},{4,5},{5,4},{6,7},{7,6},{8,9},{9,8},{10,11... | collective-permute-start | bytes 6291464 | tf_op jit(solution)/shard_map/ppermute | solution.py:178
  69.4 8.6 %copy-start.3 = (bf16[128,1536]{1,0:T(8,128)(2,1)S(1)}, bf16[128,1536]{1,0:T(8,128)(2,1)}, u32[]{:S(2)}) copy-start(bf16[128,1536]{1,0:T(8,128)(2,1)} %param.12) | copy-start | bytes 1179652
  78.0 3.3 %copy-start.4 = (f32[1536]{0:T(1024)S(1)}, f32[1536]{0:T(1024)}, u32[]{:S(2)}) copy-start(f32[1536]{0:T(1024)} %param.18) | copy-start | bytes 18436
  126.5 4.0 %copy-start.6 = (f32[128,4]{0,1:T(4,128)S(1)}, f32[128,4]{0,1:T(4,128)}, u32[]{:S(2)}) copy-start(f32[128,4]{0,1:T(4,128)} %param.20) | copy-start | bytes 6148
  126.5 35.2 %all-to-all-start.3 = ((bf16[32,24,1536]{2,1,0:T(8,128)(2,1)}), bf16[32,24,1536]{2,1,0:T(8,128)(2,1)S(1)}, u32[]{:S(2)}, u32[]{:S(2)}) async-start(bf16[32,24,1536]{2,1,0:T(8,128)(2,1)} %bitcast.5), calls=%async_computation.3 | async-start | bytes 4718592 | tf_op jit(solution)/shard_map/all_to_all | solution.py:218
Sparse Core Ops, SparseCore 0:
  9.1 63.2 all-gather.1

commit v10 on v7

--- a/solution.py
+++ b/solution.py
@@ -129,7 +129,7 @@
 def expert_ffn(rows, gate_experts, up_experts, down_experts):
     count, width = rows.shape
     hidden = gate_experts.shape[2]
-    block = 256 if hidden % 256 == 0 else hidden
+    block = 128 if hidden % 128 == 0 else hidden
     return pl.pallas_call(
         expert_kernel,
         grid=(hidden // block,),

time: 171 us -> 177 us (1.035)
  Pallas kernels: 25.2 us -> 30.9 us
    pallas_call x1, Pallas kernels: 9.62 us -> 15.3 us  [expert_ffn(): pl.pallas_call(expert_kernel, grid=(hidden // block,), in_specs=[pl.Block...]
where the time goes in v10:
time: 177 us; the launch traced here: 176 us
  blocking collectives  84.3 us (48%)
  waiting for transfers between devices  31.7 us (18%)
  Pallas kernels  30.9 us (17%)
  between operations  13.6 us (8%)
  starting transfers between devices  7.36 us (4%)
  matrix products  6.2 us (4%)
    all_to_all x1, blocking collectives, on_device(): lax.all_to_all(outgoing, EXP, split_axis=0, concat_axis=0, tiled=True)  34.7 us
    all_to_all x1, blocking collectives, on_device(): lax.all_to_all(spread, 'chip', split_axis=1, concat_axis=1, tiled=True)  33 us
    all_to_all x1, waiting for transfers between devices, on_device(): lax.all_to_all(computed, EXP, split_axis=0, concat_axis=0, tiled=True)  31 us
    all_to_all x1, blocking collectives, on_device(): lax.all_to_all(jnp.broadcast_to(prefix_key_values[:, None], (2, req_count...  16.6 us
    pallas_call x1, Pallas kernels, expert_ffn(): pl.pallas_call(expert_kernel, grid=(hidden // block,), in_specs=[pl.Block...  15.3 us
    pallas_call x1, Pallas kernels, attend_merge(): pl.pallas_call(merge_kernel, in_specs=[whole(x.shape) for x in inputs], o...  8.56 us
    pallas_call x1, Pallas kernels, attend_local(): pl.pallas_call(local_kernel, in_specs=[whole(x.shape) for x in inputs], o...  6.98 us
    all_to_all x1, starting transfers between devices, on_device(): lax.all_to_all(computed, EXP, split_axis=0, concat_axis=0, tiled=True)  3.99 us
  transfers between devices with their start and end apart: 3, of which 1 were waited for; matrix products, arithmetic and copies ran while one was open for 1% of the time, Pallas kernels for 9%

profile of v10, /device:TPU:1, one launch (start us, length us, event | category | flops | bytes accessed | tf_op | source)
XLA Modules:
  0.0 176.2 jit_solution(2187961043848532240)
XLA Ops:
  6.5 0.0 all-gather.2.cloned.1.call-start
  6.5 0.7 all-gather.2.cloned.1.call-update
  7.3 0.7 broadcast_in_dim.14
  8.0 16.6 %all_to_all.20 = bf16[2,8,16,256]{3,2,0,1:T(8,128)(2,1)S(1)} all-to-all(bf16[2,8,16,256]{3,2,0,1:T(8,128)(2,1)S(1)} %broadcast_in_dim.14), channel_id=1, replica_groups=mesh['req'=8,'chip'=16,'core'=2] {'req'}, dimensions={1} | all-to-all | bytes 262144 | tf_op jit(solution)/shard_map/all_to_all | solution.py:167
  24.6 0.2 broadcast_in_dim.32
  24.8 33.0 %all_to_all.21 = bf16[2,16,128,256]{3,2,0,1:T(8,128)(2,1)S(1)} all-to-all(bf16[2,16,128,256]{3,2,0,1:T(8,128)(2,1)S(1)} %broadcast_in_dim.32), channel_id=1, replica_groups=mesh['req'=8,'chip'=16,'core'=2] {'chip'}, dimensions={1} | all-to-all | bytes 4194304 | tf_op jit(solution)/shard_map/all_to_all | solution.py:175
  57.8 0.0 copy-start.2
  57.8 0.0 copy-start.5
  57.8 0.0 copy-start
  57.8 0.0 copy-start.1
  57.8 0.1 copy.42
  58.0 3.4 %collective-permute-start = (bf16[2,2048,256]{2,1,0:T(8,128)(2,1)S(1)}, bf16[2,2048,256]{2,1,0:T(8,128)(2,1)}, u32[]{:S(2)}, u32[]{:S(2)}) collective-permute-start(bf16[2,2048,256]{2,1,0:T(8,128)(2,1)S(1)} %bitcast.13), channel_id=1, source_target_pairs={{0,1},{1,0},{2,3},{3,2},{4,5},{5,4},{6,7},{7,6},{8,9},{9,8},{10,11... | collective-permute-start | bytes 6291464 | tf_op jit(solution)/shard_map/ppermute | solution.py:178
  61.3 0.0 copy-done.2
  61.3 0.1 copy.43.rid_col_ref
  61.4 0.0 copy-done.5
  61.4 0.1 copy.44
  61.6 0.1 eq.28
  61.7 0.3 fusion.3
  61.9 0.1 reduce_sum.30
  62.1 0.1 copy.45
  62.1 0.3 fusion.1
  62.4 0.0 copy-done
  62.4 0.0 copy-done.1
  62.4 7.0 %shard_map.118 = (f32[128,1536]{1,0:T(8,128)S(1)}, f32[128,12]{1,0:T(8,128)S(1)}, f32[128,12]{1,0:T(8,128)S(1)}) custom-call(s32[128,1]{1,0:T(8,128)S(1)} %copy.43.rid_col_ref, s32[1,128]{1,0:T(1,128)S(1)} %copy-done.2, bf16[128,1536]{1,0:T(8,128)(2,1)S(1)} %copy-done, bf16[2,2048,256]{2,1,0:T(8,128)(2,1)S(1)} %bitcast.14, bf16[2,128,256]{2,1,0:T(8,128)(2,1)S(1)} %copy-done.1), custom_call_target="tpu_custom_call" | custom-call | tf_op jit(solution)/shard_map/pallas_call | solution.py:91
  69.4 0.0 copy-start.3
  69.4 0.0 collective-permute-done.pkv_ref
  69.5 8.6 %shard_map.119 = bf16[128,1536]{1,0:T(8,128)(2,1)S(1)} custom-call(bf16[128,1536]{1,0:T(8,128)(2,1)S(1)} %copy-done, bf16[2,2048,256]{2,1,0:T(8,128)(2,1)} %collective-permute-done.pkv_ref, f32[128,1536]{1,0:T(8,128)S(1)} %get-tuple-element.8.acc_ref, f32[128,12]{1,0:T(8,128)S(1)} %get-tuple-element.9.peak_ref, f32[128,12]{1,0:T(8,128)S(1)} %get-tuple-element.10.total_ref), custom_call_target="tpu_custom_call" | custom-call | tf_op jit(solution)/shard_map/pallas_call | solution.py:102
  78.0 0.0 copy-start.4
  78.0 0.0 all-gather.2.cloned.1.call-done
  78.1 0.0 copy-done.3
  78.1 3.2 %multiply_reduce_fusion = (f32[128]{0:T(128)S(1)}, f32[128,1536]{1,0:T(8,128)S(1)}) fusion(bf16[128,1536]{1,0:T(8,128)(2,1)S(1)} %shard_map.119, bf16[1536,1536]{1,0:T(8,128)(2,1)} %all-gather.2.cloned.1.call-done, bf16[128,1536]{1,0:T(8,128)(2,1)S(1)} %copy-done.3), kind=kOutput, calls=%fused_computation.12 | convolution fusion | flops 604766080 | bytes 6291968 | tf_op jit(solution)/shard_map/dot_general | solution.py:182
  81.3 0.0 copy-done.4
  81.3 0.9 convolution_convert_fusion
  82.2 34.7 %all_to_all.22 = bf16[32,24,1536]{2,1,0:T(8,128)(2,1)S(1)} all-to-all(bf16[32,24,1536]{2,1,0:T(8,128)(2,1)S(1)} %bitcast.17), channel_id=1, replica_groups=mesh['req'=8,'chip'=16,'core'=2] {'chip','core'}, dimensions={0} | all-to-all | bytes 4718592 | tf_op jit(solution)/shard_map/all_to_all | solution.py:213
  116.9 15.3 %shard_map.120 = bf16[768,1536]{1,0:T(8,128)(2,1)} custom-call(bf16[768,1536]{1,0:T(8,128)(2,1)S(1)} %bitcast.12, bf16[1,1536,768]{2,1,0:T(8,128)(2,1)} %gate_ref.1, bf16[1,1536,768]{2,1,0:T(8,128)(2,1)} %up_ref.1, bf16[1,768,1536]{2,1,0:T(8,128)(2,1)} %down_ref.1), custom_call_target="tpu_custom_call" | custom-call | tf_op jit(solution)/shard_map/pallas_call | solution.py:133
  132.2 0.0 copy-start.6
  132.2 4.0 %all-to-all-start.3 = ((bf16[32,24,1536]{2,1,0:T(8,128)(2,1)}), bf16[32,24,1536]{2,1,0:T(8,128)(2,1)S(1)}, u32[]{:S(2)}, u32[]{:S(2)}) async-start(bf16[32,24,1536]{2,1,0:T(8,128)(2,1)} %bitcast.5), calls=%async_computation.3 | async-start | bytes 4718592 | tf_op jit(solution)/shard_map/all_to_all | solution.py:218
  136.2 0.0 copy-done.6
  136.2 0.2 select_reduce_fusion
  136.5 31.0 %all-to-all-done.3 = bf16[32,24,1536]{2,1,0:T(8,128)(2,1)S(1)} async-done(((bf16[32,24,1536]{2,1,0:T(8,128)(2,1)}), bf16[32,24,1536]{2,1,0:T(8,128)(2,1)S(1)}, u32[]{:S(2)}, u32[]{:S(2)}) %all-to-all-start.3) | async-done | bytes 2359328 | tf_op jit(solution)/shard_map/all_to_all | solution.py:218
  167.5 1.8 %fusion = bf16[128,1536]{1,0:T(8,128)(2,1)} fusion(f32[128,1536]{1,0:T(8,128)S(1)} %get-tuple-element.12, f32[128,768]{1,0:T(8,128)S(1)} %select_reduce_fusion, bf16[768,1536]{1,0:T(8,128)(2,1)S(1)} %bitcast.16), kind=kOutput, calls=%fused_computation.3 | convolution fusion | flops 1812332544 | bytes 3932160 | tf_op jit(solution)/shard_map/dot_general | solution.py:220
  (3 shorter events, 0.0 us)
Async XLA Ops:
  6.5 71.5 %all-gather.2.cloned.1.call-start = ((), (), s32[]{:S(2)}) async-start(), calls=%async_computation.4 | async-start | bytes 5308416 | tf_op jit(solution)/shard_map/all_gather | solution.py:184
  57.8 3.5 %copy-start.2 = (s32[1,128]{1,0:T(1,128)S(1)}, s32[1,128]{1,0:T(1,128)}, u32[]{:S(2)}) copy-start(s32[1,128]{1,0:T(1,128)} %rid_row_ref.1) | copy-start | bytes 1540
  57.8 3.6 %copy-start.5 = (s32[128,4]{0,1:T(4,128)S(1)}, s32[128,4]{0,1:T(4,128)}, u32[]{:S(2)}) copy-start(s32[128,4]{0,1:T(4,128)} %param.19) | copy-start | bytes 6148
  57.8 4.6 %copy-start = (bf16[128,1536]{1,0:T(8,128)(2,1)S(1)}, bf16[128,1536]{1,0:T(8,128)(2,1)}, u32[]{:S(2)}) copy-start(bf16[128,1536]{1,0:T(8,128)(2,1)} %q_ref.3) | copy-start | bytes 1179652
  57.8 4.6 %copy-start.1 = (bf16[2,128,256]{2,1,0:T(8,128)(2,1)S(1)}, bf16[2,128,256]{2,1,0:T(8,128)(2,1)}, u32[]{:S(2)}) copy-start(bf16[2,128,256]{2,1,0:T(8,128)(2,1)} %skv_ref.1) | copy-start | bytes 393220
  58.0 11.5 %collective-permute-start = (bf16[2,2048,256]{2,1,0:T(8,128)(2,1)S(1)}, bf16[2,2048,256]{2,1,0:T(8,128)(2,1)}, u32[]{:S(2)}, u32[]{:S(2)}) collective-permute-start(bf16[2,2048,256]{2,1,0:T(8,128)(2,1)S(1)} %bitcast.13), channel_id=1, source_target_pairs={{0,1},{1,0},{2,3},{3,2},{4,5},{5,4},{6,7},{7,6},{8,9},{9,8},{10,11... | collective-permute-start | bytes 6291464 | tf_op jit(solution)/shard_map/ppermute | solution.py:178
  69.4 8.6 %copy-start.3 = (bf16[128,1536]{1,0:T(8,128)(2,1)S(1)}, bf16[128,1536]{1,0:T(8,128)(2,1)}, u32[]{:S(2)}) copy-start(bf16[128,1536]{1,0:T(8,128)(2,1)} %param.12) | copy-start | bytes 1179652
  78.0 3.3 %copy-start.4 = (f32[1536]{0:T(1024)S(1)}, f32[1536]{0:T(1024)}, u32[]{:S(2)}) copy-start(f32[1536]{0:T(1024)} %param.18) | copy-start | bytes 18436
  132.2 4.0 %copy-start.6 = (f32[128,4]{0,1:T(4,128)S(1)}, f32[128,4]{0,1:T(4,128)}, u32[]{:S(2)}) copy-start(f32[128,4]{0,1:T(4,128)} %param.20) | copy-start | bytes 6148
  132.2 35.2 %all-to-all-start.3 = ((bf16[32,24,1536]{2,1,0:T(8,128)(2,1)}), bf16[32,24,1536]{2,1,0:T(8,128)(2,1)S(1)}, u32[]{:S(2)}, u32[]{:S(2)}) async-start(bf16[32,24,1536]{2,1,0:T(8,128)(2,1)} %bitcast.5), calls=%async_computation.3 | async-start | bytes 4718592 | tf_op jit(solution)/shard_map/all_to_all | solution.py:218
Sparse Core Ops, SparseCore 0:
  9.1 63.2 all-gather.1

commit v11 on v7

--- a/solution.py
+++ b/solution.py
@@ -110,20 +110,29 @@
 
 def expert_kernel(rows_ref, gate_ref, up_ref, down_ref, out_ref, acc_ref):
     step = pl.program_id(0)
-
-    @pl.when(step == 0)
-    def _():
-        acc_ref[...] = jnp.zeros_like(acc_ref)
-
+    first = step == 0
+    last = step == pl.num_programs(0) - 1
     rows = rows_ref[...]
     gated = jnp.dot(rows, gate_ref[...], preferred_element_type=jnp.float32)
     lifted = jnp.dot(rows, up_ref[...], preferred_element_type=jnp.float32)
     active = (jnp.maximum(gated, 0.0) * lifted).astype(jnp.bfloat16)
-    acc_ref[...] += jnp.dot(active, down_ref[...], preferred_element_type=jnp.float32)
-
-    @pl.when(step == pl.num_programs(0) - 1)
-    def _():
-        out_ref[...] = acc_ref[...].astype(out_ref.dtype)
+    part = jnp.dot(active, down_ref[...], preferred_element_type=jnp.float32)
+
+    @pl.when(first & jnp.logical_not(last))
+    def _():
+        acc_ref[...] = part
+
+    @pl.when(jnp.logical_not(first) & jnp.logical_not(last))
+    def _():
+        acc_ref[...] += part
+
+    @pl.when(last & jnp.logical_not(first))
+    def _():
+        out_ref[...] = (acc_ref[...] + part).astype(out_ref.dtype)
+
+    @pl.when(first & last)
+    def _():
+        out_ref[...] = part.astype(out_ref.dtype)
 
 
 def expert_ffn(rows, gate_experts, up_experts, down_experts):

time: 171 us -> 171 us (level)
  no operation moved by 1% of the time
where the time goes in v11:
time: 171 us
  blocking collectives  84.3 us (49%)
  waiting for transfers between devices  31.7 us (19%)
  Pallas kernels  25.8 us (15%)
  between operations  13.6 us (8%)
  starting transfers between devices  7.36 us (4%)
  matrix products  6.2 us (4%)
    all_to_all x1, blocking collectives, on_device(): lax.all_to_all(outgoing, EXP, split_axis=0, concat_axis=0, tiled=True)  34.7 us
    all_to_all x1, blocking collectives, on_device(): lax.all_to_all(spread, 'chip', split_axis=1, concat_axis=1, tiled=True)  33 us
    all_to_all x1, waiting for transfers between devices, on_device(): lax.all_to_all(computed, EXP, split_axis=0, concat_axis=0, tiled=True)  31 us
    all_to_all x1, blocking collectives, on_device(): lax.all_to_all(jnp.broadcast_to(prefix_key_values[:, None], (2, req_count...  16.6 us
    pallas_call x1, Pallas kernels, expert_ffn(): pl.pallas_call(expert_kernel, grid=(hidden // block,), in_specs=[pl.Block...  10.2 us
    pallas_call x1, Pallas kernels, attend_merge(): pl.pallas_call(merge_kernel, in_specs=[whole(x.shape) for x in inputs], o...  8.56 us
    pallas_call x1, Pallas kernels, attend_local(): pl.pallas_call(local_kernel, in_specs=[whole(x.shape) for x in inputs], o...  6.98 us
    all_to_all x1, starting transfers between devices, on_device(): lax.all_to_all(computed, EXP, split_axis=0, concat_axis=0, tiled=True)  3.99 us
  transfers between devices with their start and end apart: 3, of which 1 were waited for; matrix products, arithmetic and copies ran while one was open for 1% of the time, Pallas kernels for 9%

profile of v11, /device:TPU:1, one launch (start us, length us, event | category | flops | bytes accessed | tf_op | source)
XLA Modules:
  0.0 171.1 jit_solution(8110408895442245502)
XLA Ops:
  6.5 0.0 all-gather.2.cloned.1.call-start
  6.5 0.7 all-gather.2.cloned.1.call-update
  7.3 0.7 broadcast_in_dim.14
  8.0 16.6 %all_to_all.20 = bf16[2,8,16,256]{3,2,0,1:T(8,128)(2,1)S(1)} all-to-all(bf16[2,8,16,256]{3,2,0,1:T(8,128)(2,1)S(1)} %broadcast_in_dim.14), channel_id=1, replica_groups=mesh['req'=8,'chip'=16,'core'=2] {'req'}, dimensions={1} | all-to-all | bytes 262144 | tf_op jit(solution)/shard_map/all_to_all | solution.py:176
  24.6 0.2 broadcast_in_dim.32
  24.8 33.0 %all_to_all.21 = bf16[2,16,128,256]{3,2,0,1:T(8,128)(2,1)S(1)} all-to-all(bf16[2,16,128,256]{3,2,0,1:T(8,128)(2,1)S(1)} %broadcast_in_dim.32), channel_id=1, replica_groups=mesh['req'=8,'chip'=16,'core'=2] {'chip'}, dimensions={1} | all-to-all | bytes 4194304 | tf_op jit(solution)/shard_map/all_to_all | solution.py:184
  57.8 0.0 copy-start.2
  57.8 0.0 copy-start.5
  57.8 0.0 copy-start
  57.8 0.0 copy-start.1
  57.8 0.1 copy.42
  58.0 3.4 %collective-permute-start = (bf16[2,2048,256]{2,1,0:T(8,128)(2,1)S(1)}, bf16[2,2048,256]{2,1,0:T(8,128)(2,1)}, u32[]{:S(2)}, u32[]{:S(2)}) collective-permute-start(bf16[2,2048,256]{2,1,0:T(8,128)(2,1)S(1)} %bitcast.13), channel_id=1, source_target_pairs={{0,1},{1,0},{2,3},{3,2},{4,5},{5,4},{6,7},{7,6},{8,9},{9,8},{10,11... | collective-permute-start | bytes 6291464 | tf_op jit(solution)/shard_map/ppermute | solution.py:187
  61.3 0.0 copy-done.2
  61.3 0.1 copy.43.rid_col_ref
  61.4 0.0 copy-done.5
  61.4 0.1 copy.44
  61.6 0.1 eq.28
  61.7 0.3 fusion.3
  61.9 0.1 reduce_sum.30
  62.1 0.1 copy.45
  62.1 0.3 fusion.1
  62.4 0.0 copy-done
  62.4 0.0 copy-done.1
  62.4 7.0 %shard_map.118 = (f32[128,1536]{1,0:T(8,128)S(1)}, f32[128,12]{1,0:T(8,128)S(1)}, f32[128,12]{1,0:T(8,128)S(1)}) custom-call(s32[128,1]{1,0:T(8,128)S(1)} %copy.43.rid_col_ref, s32[1,128]{1,0:T(1,128)S(1)} %copy-done.2, bf16[128,1536]{1,0:T(8,128)(2,1)S(1)} %copy-done, bf16[2,2048,256]{2,1,0:T(8,128)(2,1)S(1)} %bitcast.14, bf16[2,128,256]{2,1,0:T(8,128)(2,1)S(1)} %copy-done.1), custom_call_target="tpu_custom_call" | custom-call | tf_op jit(solution)/shard_map/pallas_call | solution.py:91
  69.4 0.0 copy-start.3
  69.4 0.0 collective-permute-done.pkv_ref
  69.5 8.6 %shard_map.119 = bf16[128,1536]{1,0:T(8,128)(2,1)S(1)} custom-call(bf16[128,1536]{1,0:T(8,128)(2,1)S(1)} %copy-done, bf16[2,2048,256]{2,1,0:T(8,128)(2,1)} %collective-permute-done.pkv_ref, f32[128,1536]{1,0:T(8,128)S(1)} %get-tuple-element.8.acc_ref, f32[128,12]{1,0:T(8,128)S(1)} %get-tuple-element.9.peak_ref, f32[128,12]{1,0:T(8,128)S(1)} %get-tuple-element.10.total_ref), custom_call_target="tpu_custom_call" | custom-call | tf_op jit(solution)/shard_map/pallas_call | solution.py:102
  78.0 0.0 copy-start.4
  78.0 0.0 all-gather.2.cloned.1.call-done
  78.1 0.0 copy-done.3
  78.1 3.2 %multiply_reduce_fusion = (f32[128]{0:T(128)S(1)}, f32[128,1536]{1,0:T(8,128)S(1)}) fusion(bf16[128,1536]{1,0:T(8,128)(2,1)S(1)} %shard_map.119, bf16[1536,1536]{1,0:T(8,128)(2,1)} %all-gather.2.cloned.1.call-done, bf16[128,1536]{1,0:T(8,128)(2,1)S(1)} %copy-done.3), kind=kOutput, calls=%fused_computation.12 | convolution fusion | flops 604766080 | bytes 6291968 | tf_op jit(solution)/shard_map/dot_general | solution.py:191
  81.3 0.0 copy-done.4
  81.3 0.9 convolution_convert_fusion
  82.2 34.7 %all_to_all.22 = bf16[32,24,1536]{2,1,0:T(8,128)(2,1)S(1)} all-to-all(bf16[32,24,1536]{2,1,0:T(8,128)(2,1)S(1)} %bitcast.17), channel_id=1, replica_groups=mesh['req'=8,'chip'=16,'core'=2] {'chip','core'}, dimensions={0} | all-to-all | bytes 4718592 | tf_op jit(solution)/shard_map/all_to_all | solution.py:222
  116.9 10.2 %shard_map.120 = bf16[768,1536]{1,0:T(8,128)(2,1)} custom-call(bf16[768,1536]{1,0:T(8,128)(2,1)S(1)} %bitcast.12, bf16[1,1536,768]{2,1,0:T(8,128)(2,1)} %gate_ref.1, bf16[1,1536,768]{2,1,0:T(8,128)(2,1)} %up_ref.1, bf16[1,768,1536]{2,1,0:T(8,128)(2,1)} %down_ref.1), custom_call_target="tpu_custom_call" | custom-call | tf_op jit(solution)/shard_map/pallas_call | solution.py:142
  127.1 0.0 copy-start.6
  127.1 4.0 %all-to-all-start.3 = ((bf16[32,24,1536]{2,1,0:T(8,128)(2,1)}), bf16[32,24,1536]{2,1,0:T(8,128)(2,1)S(1)}, u32[]{:S(2)}, u32[]{:S(2)}) async-start(bf16[32,24,1536]{2,1,0:T(8,128)(2,1)} %bitcast.5), calls=%async_computation.3 | async-start | bytes 4718592 | tf_op jit(solution)/shard_map/all_to_all | solution.py:227
  131.1 0.0 copy-done.6
  131.1 0.2 select_reduce_fusion
  131.4 31.0 %all-to-all-done.3 = bf16[32,24,1536]{2,1,0:T(8,128)(2,1)S(1)} async-done(((bf16[32,24,1536]{2,1,0:T(8,128)(2,1)}), bf16[32,24,1536]{2,1,0:T(8,128)(2,1)S(1)}, u32[]{:S(2)}, u32[]{:S(2)}) %all-to-all-start.3) | async-done | bytes 2359328 | tf_op jit(solution)/shard_map/all_to_all | solution.py:227
  162.4 1.8 %fusion = bf16[128,1536]{1,0:T(8,128)(2,1)} fusion(f32[128,1536]{1,0:T(8,128)S(1)} %get-tuple-element.12, f32[128,768]{1,0:T(8,128)S(1)} %select_reduce_fusion, bf16[768,1536]{1,0:T(8,128)(2,1)S(1)} %bitcast.16), kind=kOutput, calls=%fused_computation.3 | convolution fusion | flops 1812332544 | bytes 3932160 | tf_op jit(solution)/shard_map/dot_general | solution.py:229
  (3 shorter events, 0.0 us)
Async XLA Ops:
  6.5 71.5 %all-gather.2.cloned.1.call-start = ((), (), s32[]{:S(2)}) async-start(), calls=%async_computation.4 | async-start | bytes 5308416 | tf_op jit(solution)/shard_map/all_gather | solution.py:193
  57.8 3.5 %copy-start.2 = (s32[1,128]{1,0:T(1,128)S(1)}, s32[1,128]{1,0:T(1,128)}, u32[]{:S(2)}) copy-start(s32[1,128]{1,0:T(1,128)} %rid_row_ref.1) | copy-start | bytes 1540
  57.8 3.6 %copy-start.5 = (s32[128,4]{0,1:T(4,128)S(1)}, s32[128,4]{0,1:T(4,128)}, u32[]{:S(2)}) copy-start(s32[128,4]{0,1:T(4,128)} %param.19) | copy-start | bytes 6148
  57.8 4.6 %copy-start = (bf16[128,1536]{1,0:T(8,128)(2,1)S(1)}, bf16[128,1536]{1,0:T(8,128)(2,1)}, u32[]{:S(2)}) copy-start(bf16[128,1536]{1,0:T(8,128)(2,1)} %q_ref.3) | copy-start | bytes 1179652
  57.8 4.6 %copy-start.1 = (bf16[2,128,256]{2,1,0:T(8,128)(2,1)S(1)}, bf16[2,128,256]{2,1,0:T(8,128)(2,1)}, u32[]{:S(2)}) copy-start(bf16[2,128,256]{2,1,0:T(8,128)(2,1)} %skv_ref.1) | copy-start | bytes 393220
  58.0 11.5 %collective-permute-start = (bf16[2,2048,256]{2,1,0:T(8,128)(2,1)S(1)}, bf16[2,2048,256]{2,1,0:T(8,128)(2,1)}, u32[]{:S(2)}, u32[]{:S(2)}) collective-permute-start(bf16[2,2048,256]{2,1,0:T(8,128)(2,1)S(1)} %bitcast.13), channel_id=1, source_target_pairs={{0,1},{1,0},{2,3},{3,2},{4,5},{5,4},{6,7},{7,6},{8,9},{9,8},{10,11... | collective-permute-start | bytes 6291464 | tf_op jit(solution)/shard_map/ppermute | solution.py:187
  69.4 8.6 %copy-start.3 = (bf16[128,1536]{1,0:T(8,128)(2,1)S(1)}, bf16[128,1536]{1,0:T(8,128)(2,1)}, u32[]{:S(2)}) copy-start(bf16[128,1536]{1,0:T(8,128)(2,1)} %param.12) | copy-start | bytes 1179652
  78.0 3.3 %copy-start.4 = (f32[1536]{0:T(1024)S(1)}, f32[1536]{0:T(1024)}, u32[]{:S(2)}) copy-start(f32[1536]{0:T(1024)} %param.18) | copy-start | bytes 18436
  127.1 4.0 %copy-start.6 = (f32[128,4]{0,1:T(4,128)S(1)}, f32[128,4]{0,1:T(4,128)}, u32[]{:S(2)}) copy-start(f32[128,4]{0,1:T(4,128)} %param.20) | copy-start | bytes 6148
  127.1 35.2 %all-to-all-start.3 = ((bf16[32,24,1536]{2,1,0:T(8,128)(2,1)}), bf16[32,24,1536]{2,1,0:T(8,128)(2,1)S(1)}, u32[]{:S(2)}, u32[]{:S(2)}) async-start(bf16[32,24,1536]{2,1,0:T(8,128)(2,1)} %bitcast.5), calls=%async_computation.3 | async-start | bytes 4718592 | tf_op jit(solution)/shard_map/all_to_all | solution.py:227
Sparse Core Ops, SparseCore 0:
  9.1 63.2 all-gather.1

commit v12 on v7

--- a/solution.py
+++ b/solution.py
@@ -76,7 +76,7 @@
         own_scale = jnp.exp(own_peak - peak)
         total = total_ref[:, head : head + 1] * first_scale + own_total * own_scale
         summed = acc_ref[:, columns] * first_scale + own_acc * own_scale
-        out_ref[:, columns] = (summed / total).astype(out_ref.dtype)
+        out_ref[:, columns] = (summed * (1.0 / total)).astype(out_ref.dtype)
 
 
 def whole(shape):

time: 171 us -> 171 us (level)
  no operation moved by 1% of the time
where the time goes in v12:
time: 171 us
  blocking collectives  84.3 us (49%)
  waiting for transfers between devices  31.7 us (19%)
  Pallas kernels  25.3 us (15%)
  between operations  13.5 us (8%)
  starting transfers between devices  7.36 us (4%)
  matrix products  6.21 us (4%)
    all_to_all x1, blocking collectives, on_device(): lax.all_to_all(outgoing, EXP, split_axis=0, concat_axis=0, tiled=True)  34.7 us
    all_to_all x1, blocking collectives, on_device(): lax.all_to_all(spread, 'chip', split_axis=1, concat_axis=1, tiled=True)  33 us
    all_to_all x1, waiting for transfers between devices, on_device(): lax.all_to_all(computed, EXP, split_axis=0, concat_axis=0, tiled=True)  31 us
    all_to_all x1, blocking collectives, on_device(): lax.all_to_all(jnp.broadcast_to(prefix_key_values[:, None], (2, req_count...  16.6 us
    pallas_call x1, Pallas kernels, expert_ffn(): pl.pallas_call(expert_kernel, grid=(hidden // block,), in_specs=[pl.Block...  9.62 us
    pallas_call x1, Pallas kernels, attend_merge(): pl.pallas_call(merge_kernel, in_specs=[whole(x.shape) for x in inputs], o...  8.67 us
    pallas_call x1, Pallas kernels, attend_local(): pl.pallas_call(local_kernel, in_specs=[whole(x.shape) for x in inputs], o...  6.98 us
    all_to_all x1, starting transfers between devices, on_device(): lax.all_to_all(computed, EXP, split_axis=0, concat_axis=0, tiled=True)  3.99 us
  transfers between devices with their start and end apart: 3, of which 1 were waited for; matrix products, arithmetic and copies ran while one was open for 1% of the time, Pallas kernels for 9%

profile of v12, /device:TPU:1, one launch (start us, length us, event | category | flops | bytes accessed | tf_op | source)
XLA Modules:
  0.0 170.6 jit_solution(12631571495891871627)
XLA Ops:
  6.5 0.0 all-gather.2.cloned.1.call-start
  6.5 0.7 all-gather.2.cloned.1.call-update
  7.3 0.7 broadcast_in_dim.14
  8.0 16.6 %all_to_all.20 = bf16[2,8,16,256]{3,2,0,1:T(8,128)(2,1)S(1)} all-to-all(bf16[2,8,16,256]{3,2,0,1:T(8,128)(2,1)S(1)} %broadcast_in_dim.14), channel_id=1, replica_groups=mesh['req'=8,'chip'=16,'core'=2] {'req'}, dimensions={1} | all-to-all | bytes 262144 | tf_op jit(solution)/shard_map/all_to_all | solution.py:167
  24.6 0.2 broadcast_in_dim.32
  24.8 33.0 %all_to_all.21 = bf16[2,16,128,256]{3,2,0,1:T(8,128)(2,1)S(1)} all-to-all(bf16[2,16,128,256]{3,2,0,1:T(8,128)(2,1)S(1)} %broadcast_in_dim.32), channel_id=1, replica_groups=mesh['req'=8,'chip'=16,'core'=2] {'chip'}, dimensions={1} | all-to-all | bytes 4194304 | tf_op jit(solution)/shard_map/all_to_all | solution.py:175
  57.8 0.0 copy-start.2
  57.8 0.0 copy-start.5
  57.8 0.0 copy-start
  57.8 0.0 copy-start.1
  57.8 0.1 copy.42
  58.0 3.4 %collective-permute-start = (bf16[2,2048,256]{2,1,0:T(8,128)(2,1)S(1)}, bf16[2,2048,256]{2,1,0:T(8,128)(2,1)}, u32[]{:S(2)}, u32[]{:S(2)}) collective-permute-start(bf16[2,2048,256]{2,1,0:T(8,128)(2,1)S(1)} %bitcast.13), channel_id=1, source_target_pairs={{0,1},{1,0},{2,3},{3,2},{4,5},{5,4},{6,7},{7,6},{8,9},{9,8},{10,11... | collective-permute-start | bytes 6291464 | tf_op jit(solution)/shard_map/ppermute | solution.py:178
  61.3 0.0 copy-done.2
  61.3 0.1 copy.43.rid_col_ref
  61.4 0.0 copy-done.5
  61.4 0.1 copy.44
  61.6 0.1 eq.28
  61.7 0.3 fusion.3
  61.9 0.1 reduce_sum.30
  62.1 0.1 copy.45
  62.1 0.3 fusion.1
  62.4 0.0 copy-done
  62.4 0.0 copy-done.1
  62.4 7.0 %shard_map.118 = (f32[128,1536]{1,0:T(8,128)S(1)}, f32[128,12]{1,0:T(8,128)S(1)}, f32[128,12]{1,0:T(8,128)S(1)}) custom-call(s32[128,1]{1,0:T(8,128)S(1)} %copy.43.rid_col_ref, s32[1,128]{1,0:T(1,128)S(1)} %copy-done.2, bf16[128,1536]{1,0:T(8,128)(2,1)S(1)} %copy-done, bf16[2,2048,256]{2,1,0:T(8,128)(2,1)S(1)} %bitcast.14, bf16[2,128,256]{2,1,0:T(8,128)(2,1)S(1)} %copy-done.1), custom_call_target="tpu_custom_call" | custom-call | tf_op jit(solution)/shard_map/pallas_call | solution.py:91
  69.4 0.0 copy-start.3
  69.4 0.0 collective-permute-done.pkv_ref
  69.5 8.7 %shard_map.119 = bf16[128,1536]{1,0:T(8,128)(2,1)S(1)} custom-call(bf16[128,1536]{1,0:T(8,128)(2,1)S(1)} %copy-done, bf16[2,2048,256]{2,1,0:T(8,128)(2,1)} %collective-permute-done.pkv_ref, f32[128,1536]{1,0:T(8,128)S(1)} %get-tuple-element.8.acc_ref, f32[128,12]{1,0:T(8,128)S(1)} %get-tuple-element.9.peak_ref, f32[128,12]{1,0:T(8,128)S(1)} %get-tuple-element.10.total_ref), custom_call_target="tpu_custom_call" | custom-call | tf_op jit(solution)/shard_map/pallas_call | solution.py:102
  78.1 0.0 copy-start.4
  78.1 0.0 all-gather.2.cloned.1.call-done
  78.2 0.0 copy-done.3
  78.2 3.2 %multiply_reduce_fusion = (f32[128]{0:T(128)S(1)}, f32[128,1536]{1,0:T(8,128)S(1)}) fusion(bf16[128,1536]{1,0:T(8,128)(2,1)S(1)} %shard_map.119, bf16[1536,1536]{1,0:T(8,128)(2,1)} %all-gather.2.cloned.1.call-done, bf16[128,1536]{1,0:T(8,128)(2,1)S(1)} %copy-done.3), kind=kOutput, calls=%fused_computation.12 | convolution fusion | flops 604766080 | bytes 6291968 | tf_op jit(solution)/shard_map/dot_general | solution.py:182
  81.4 0.0 copy-done.4
  81.4 0.9 convolution_convert_fusion
  82.3 34.7 %all_to_all.22 = bf16[32,24,1536]{2,1,0:T(8,128)(2,1)S(1)} all-to-all(bf16[32,24,1536]{2,1,0:T(8,128)(2,1)S(1)} %bitcast.17), channel_id=1, replica_groups=mesh['req'=8,'chip'=16,'core'=2] {'chip','core'}, dimensions={0} | all-to-all | bytes 4718592 | tf_op jit(solution)/shard_map/all_to_all | solution.py:213
  117.0 9.6 %shard_map.120 = bf16[768,1536]{1,0:T(8,128)(2,1)} custom-call(bf16[768,1536]{1,0:T(8,128)(2,1)S(1)} %bitcast.12, bf16[1,1536,768]{2,1,0:T(8,128)(2,1)} %gate_ref.1, bf16[1,1536,768]{2,1,0:T(8,128)(2,1)} %up_ref.1, bf16[1,768,1536]{2,1,0:T(8,128)(2,1)} %down_ref.1), custom_call_target="tpu_custom_call" | custom-call | tf_op jit(solution)/shard_map/pallas_call | solution.py:133
  126.6 0.0 copy-start.6
  126.6 4.0 %all-to-all-start.3 = ((bf16[32,24,1536]{2,1,0:T(8,128)(2,1)}), bf16[32,24,1536]{2,1,0:T(8,128)(2,1)S(1)}, u32[]{:S(2)}, u32[]{:S(2)}) async-start(bf16[32,24,1536]{2,1,0:T(8,128)(2,1)} %bitcast.5), calls=%async_computation.3 | async-start | bytes 4718592 | tf_op jit(solution)/shard_map/all_to_all | solution.py:218
  130.6 0.0 copy-done.6
  130.6 0.2 select_reduce_fusion
  130.9 31.0 %all-to-all-done.3 = bf16[32,24,1536]{2,1,0:T(8,128)(2,1)S(1)} async-done(((bf16[32,24,1536]{2,1,0:T(8,128)(2,1)}), bf16[32,24,1536]{2,1,0:T(8,128)(2,1)S(1)}, u32[]{:S(2)}, u32[]{:S(2)}) %all-to-all-start.3) | async-done | bytes 2359328 | tf_op jit(solution)/shard_map/all_to_all | solution.py:218
  161.9 1.8 %fusion = bf16[128,1536]{1,0:T(8,128)(2,1)} fusion(f32[128,1536]{1,0:T(8,128)S(1)} %get-tuple-element.12, f32[128,768]{1,0:T(8,128)S(1)} %select_reduce_fusion, bf16[768,1536]{1,0:T(8,128)(2,1)S(1)} %bitcast.16), kind=kOutput, calls=%fused_computation.3 | convolution fusion | flops 1812332544 | bytes 3932160 | tf_op jit(solution)/shard_map/dot_general | solution.py:220
  (3 shorter events, 0.0 us)
Async XLA Ops:
  6.5 71.6 %all-gather.2.cloned.1.call-start = ((), (), s32[]{:S(2)}) async-start(), calls=%async_computation.4 | async-start | bytes 5308416 | tf_op jit(solution)/shard_map/all_gather | solution.py:184
  57.8 3.5 %copy-start.2 = (s32[1,128]{1,0:T(1,128)S(1)}, s32[1,128]{1,0:T(1,128)}, u32[]{:S(2)}) copy-start(s32[1,128]{1,0:T(1,128)} %rid_row_ref.1) | copy-start | bytes 1540
  57.8 3.6 %copy-start.5 = (s32[128,4]{0,1:T(4,128)S(1)}, s32[128,4]{0,1:T(4,128)}, u32[]{:S(2)}) copy-start(s32[128,4]{0,1:T(4,128)} %param.19) | copy-start | bytes 6148
  57.8 4.6 %copy-start = (bf16[128,1536]{1,0:T(8,128)(2,1)S(1)}, bf16[128,1536]{1,0:T(8,128)(2,1)}, u32[]{:S(2)}) copy-start(bf16[128,1536]{1,0:T(8,128)(2,1)} %q_ref.3) | copy-start | bytes 1179652
  57.8 4.6 %copy-start.1 = (bf16[2,128,256]{2,1,0:T(8,128)(2,1)S(1)}, bf16[2,128,256]{2,1,0:T(8,128)(2,1)}, u32[]{:S(2)}) copy-start(bf16[2,128,256]{2,1,0:T(8,128)(2,1)} %skv_ref.1) | copy-start | bytes 393220
  58.0 11.5 %collective-permute-start = (bf16[2,2048,256]{2,1,0:T(8,128)(2,1)S(1)}, bf16[2,2048,256]{2,1,0:T(8,128)(2,1)}, u32[]{:S(2)}, u32[]{:S(2)}) collective-permute-start(bf16[2,2048,256]{2,1,0:T(8,128)(2,1)S(1)} %bitcast.13), channel_id=1, source_target_pairs={{0,1},{1,0},{2,3},{3,2},{4,5},{5,4},{6,7},{7,6},{8,9},{9,8},{10,11... | collective-permute-start | bytes 6291464 | tf_op jit(solution)/shard_map/ppermute | solution.py:178
  69.4 8.7 %copy-start.3 = (bf16[128,1536]{1,0:T(8,128)(2,1)S(1)}, bf16[128,1536]{1,0:T(8,128)(2,1)}, u32[]{:S(2)}) copy-start(bf16[128,1536]{1,0:T(8,128)(2,1)} %param.12) | copy-start | bytes 1179652
  78.1 3.3 %copy-start.4 = (f32[1536]{0:T(1024)S(1)}, f32[1536]{0:T(1024)}, u32[]{:S(2)}) copy-start(f32[1536]{0:T(1024)} %param.18) | copy-start | bytes 18436
  126.6 4.0 %copy-start.6 = (f32[128,4]{0,1:T(4,128)S(1)}, f32[128,4]{0,1:T(4,128)}, u32[]{:S(2)}) copy-start(f32[128,4]{0,1:T(4,128)} %param.20) | copy-start | bytes 6148
  126.6 35.2 %all-to-all-start.3 = ((bf16[32,24,1536]{2,1,0:T(8,128)(2,1)}), bf16[32,24,1536]{2,1,0:T(8,128)(2,1)S(1)}, u32[]{:S(2)}, u32[]{:S(2)}) async-start(bf16[32,24,1536]{2,1,0:T(8,128)(2,1)} %bitcast.5), calls=%async_computation.3 | async-start | bytes 4718592 | tf_op jit(solution)/shard_map/all_to_all | solution.py:218
Sparse Core Ops, SparseCore 0:
  9.1 63.2 all-gather.1

commit v13 on v10

--- a/solution.py
+++ b/solution.py
@@ -129,7 +129,7 @@
 def expert_ffn(rows, gate_experts, up_experts, down_experts):
     count, width = rows.shape
     hidden = gate_experts.shape[2]
-    block = 128 if hidden % 128 == 0 else hidden
+    block = 384 if hidden % 384 == 0 else hidden
     return pl.pallas_call(
         expert_kernel,
         grid=(hidden // block,),

time: 177 us -> 173 us (0.977)
  Pallas kernels: 30.9 us -> 27.1 us
    pallas_call x1, Pallas kernels: 15.3 us -> 11.6 us  [expert_ffn(): pl.pallas_call(expert_kernel, grid=(hidden // block,), in_specs=[pl.Block...]
where the time goes in v13:
time: 173 us; the launch traced here: 172 us
  blocking collectives  84.3 us (49%)
  waiting for transfers between devices  31.7 us (18%)
  Pallas kernels  27.1 us (16%)
  between operations  13.6 us (8%)
  starting transfers between devices  7.36 us (4%)
  matrix products  6.2 us (4%)
    all_to_all x1, blocking collectives, on_device(): lax.all_to_all(outgoing, EXP, split_axis=0, concat_axis=0, tiled=True)  34.7 us
    all_to_all x1, blocking collectives, on_device(): lax.all_to_all(spread, 'chip', split_axis=1, concat_axis=1, tiled=True)  33 us
    all_to_all x1, waiting for transfers between devices, on_device(): lax.all_to_all(computed, EXP, split_axis=0, concat_axis=0, tiled=True)  31 us
    all_to_all x1, blocking collectives, on_device(): lax.all_to_all(jnp.broadcast_to(prefix_key_values[:, None], (2, req_count...  16.6 us
    pallas_call x1, Pallas kernels, expert_ffn(): pl.pallas_call(expert_kernel, grid=(hidden // block,), in_specs=[pl.Block...  11.6 us
    pallas_call x1, Pallas kernels, attend_merge(): pl.pallas_call(merge_kernel, in_specs=[whole(x.shape) for x in inputs], o...  8.56 us
    pallas_call x1, Pallas kernels, attend_local(): pl.pallas_call(local_kernel, in_specs=[whole(x.shape) for x in inputs], o...  6.98 us
    all_to_all x1, starting transfers between devices, on_device(): lax.all_to_all(computed, EXP, split_axis=0, concat_axis=0, tiled=True)  3.99 us
  transfers between devices with their start and end apart: 3, of which 1 were waited for; matrix products, arithmetic and copies ran while one was open for 1% of the time, Pallas kernels for 9%

profile of v13, /device:TPU:1, one launch (start us, length us, event | category | flops | bytes accessed | tf_op | source)
XLA Modules:
  0.0 172.4 jit_solution(12267851856178959353)
XLA Ops:
  6.5 0.0 all-gather.2.cloned.1.call-start
  6.5 0.7 all-gather.2.cloned.1.call-update
  7.3 0.7 broadcast_in_dim.14
  8.0 16.6 %all_to_all.20 = bf16[2,8,16,256]{3,2,0,1:T(8,128)(2,1)S(1)} all-to-all(bf16[2,8,16,256]{3,2,0,1:T(8,128)(2,1)S(1)} %broadcast_in_dim.14), channel_id=1, replica_groups=mesh['req'=8,'chip'=16,'core'=2] {'req'}, dimensions={1} | all-to-all | bytes 262144 | tf_op jit(solution)/shard_map/all_to_all | solution.py:167
  24.6 0.2 broadcast_in_dim.32
  24.8 33.0 %all_to_all.21 = bf16[2,16,128,256]{3,2,0,1:T(8,128)(2,1)S(1)} all-to-all(bf16[2,16,128,256]{3,2,0,1:T(8,128)(2,1)S(1)} %broadcast_in_dim.32), channel_id=1, replica_groups=mesh['req'=8,'chip'=16,'core'=2] {'chip'}, dimensions={1} | all-to-all | bytes 4194304 | tf_op jit(solution)/shard_map/all_to_all | solution.py:175
  57.8 0.0 copy-start.2
  57.8 0.0 copy-start.5
  57.8 0.0 copy-start
  57.8 0.0 copy-start.1
  57.8 0.1 copy.42
  58.0 3.4 %collective-permute-start = (bf16[2,2048,256]{2,1,0:T(8,128)(2,1)S(1)}, bf16[2,2048,256]{2,1,0:T(8,128)(2,1)}, u32[]{:S(2)}, u32[]{:S(2)}) collective-permute-start(bf16[2,2048,256]{2,1,0:T(8,128)(2,1)S(1)} %bitcast.13), channel_id=1, source_target_pairs={{0,1},{1,0},{2,3},{3,2},{4,5},{5,4},{6,7},{7,6},{8,9},{9,8},{10,11... | collective-permute-start | bytes 6291464 | tf_op jit(solution)/shard_map/ppermute | solution.py:178
  61.3 0.0 copy-done.2
  61.3 0.1 copy.43.rid_col_ref
  61.4 0.0 copy-done.5
  61.4 0.1 copy.44
  61.6 0.1 eq.28
  61.7 0.3 fusion.3
  61.9 0.1 reduce_sum.30
  62.1 0.1 copy.45
  62.1 0.3 fusion.1
  62.4 0.0 copy-done
  62.4 0.0 copy-done.1
  62.4 7.0 %shard_map.118 = (f32[128,1536]{1,0:T(8,128)S(1)}, f32[128,12]{1,0:T(8,128)S(1)}, f32[128,12]{1,0:T(8,128)S(1)}) custom-call(s32[128,1]{1,0:T(8,128)S(1)} %copy.43.rid_col_ref, s32[1,128]{1,0:T(1,128)S(1)} %copy-done.2, bf16[128,1536]{1,0:T(8,128)(2,1)S(1)} %copy-done, bf16[2,2048,256]{2,1,0:T(8,128)(2,1)S(1)} %bitcast.14, bf16[2,128,256]{2,1,0:T(8,128)(2,1)S(1)} %copy-done.1), custom_call_target="tpu_custom_call" | custom-call | tf_op jit(solution)/shard_map/pallas_call | solution.py:91
  69.4 0.0 copy-start.3
  69.4 0.0 collective-permute-done.pkv_ref
  69.5 8.6 %shard_map.119 = bf16[128,1536]{1,0:T(8,128)(2,1)S(1)} custom-call(bf16[128,1536]{1,0:T(8,128)(2,1)S(1)} %copy-done, bf16[2,2048,256]{2,1,0:T(8,128)(2,1)} %collective-permute-done.pkv_ref, f32[128,1536]{1,0:T(8,128)S(1)} %get-tuple-element.8.acc_ref, f32[128,12]{1,0:T(8,128)S(1)} %get-tuple-element.9.peak_ref, f32[128,12]{1,0:T(8,128)S(1)} %get-tuple-element.10.total_ref), custom_call_target="tpu_custom_call" | custom-call | tf_op jit(solution)/shard_map/pallas_call | solution.py:102
  78.0 0.0 copy-start.4
  78.0 0.0 all-gather.2.cloned.1.call-done
  78.1 0.0 copy-done.3
  78.1 3.2 %multiply_reduce_fusion = (f32[128]{0:T(128)S(1)}, f32[128,1536]{1,0:T(8,128)S(1)}) fusion(bf16[128,1536]{1,0:T(8,128)(2,1)S(1)} %shard_map.119, bf16[1536,1536]{1,0:T(8,128)(2,1)} %all-gather.2.cloned.1.call-done, bf16[128,1536]{1,0:T(8,128)(2,1)S(1)} %copy-done.3), kind=kOutput, calls=%fused_computation.12 | convolution fusion | flops 604766080 | bytes 6291968 | tf_op jit(solution)/shard_map/dot_general | solution.py:182
  81.3 0.0 copy-done.4
  81.3 0.9 convolution_convert_fusion
  82.2 34.7 %all_to_all.22 = bf16[32,24,1536]{2,1,0:T(8,128)(2,1)S(1)} all-to-all(bf16[32,24,1536]{2,1,0:T(8,128)(2,1)S(1)} %bitcast.17), channel_id=1, replica_groups=mesh['req'=8,'chip'=16,'core'=2] {'chip','core'}, dimensions={0} | all-to-all | bytes 4718592 | tf_op jit(solution)/shard_map/all_to_all | solution.py:213
  116.9 11.6 %shard_map.120 = bf16[768,1536]{1,0:T(8,128)(2,1)} custom-call(bf16[768,1536]{1,0:T(8,128)(2,1)S(1)} %bitcast.12, bf16[1,1536,768]{2,1,0:T(8,128)(2,1)} %gate_ref.1, bf16[1,1536,768]{2,1,0:T(8,128)(2,1)} %up_ref.1, bf16[1,768,1536]{2,1,0:T(8,128)(2,1)} %down_ref.1), custom_call_target="tpu_custom_call" | custom-call | tf_op jit(solution)/shard_map/pallas_call | solution.py:133
  128.5 0.0 copy-start.6
  128.5 4.0 %all-to-all-start.3 = ((bf16[32,24,1536]{2,1,0:T(8,128)(2,1)}), bf16[32,24,1536]{2,1,0:T(8,128)(2,1)S(1)}, u32[]{:S(2)}, u32[]{:S(2)}) async-start(bf16[32,24,1536]{2,1,0:T(8,128)(2,1)} %bitcast.5), calls=%async_computation.3 | async-start | bytes 4718592 | tf_op jit(solution)/shard_map/all_to_all | solution.py:218
  132.5 0.0 copy-done.6
  132.5 0.2 select_reduce_fusion
  132.7 31.0 %all-to-all-done.3 = bf16[32,24,1536]{2,1,0:T(8,128)(2,1)S(1)} async-done(((bf16[32,24,1536]{2,1,0:T(8,128)(2,1)}), bf16[32,24,1536]{2,1,0:T(8,128)(2,1)S(1)}, u32[]{:S(2)}, u32[]{:S(2)}) %all-to-all-start.3) | async-done | bytes 2359328 | tf_op jit(solution)/shard_map/all_to_all | solution.py:218
  163.7 1.8 %fusion = bf16[128,1536]{1,0:T(8,128)(2,1)} fusion(f32[128,1536]{1,0:T(8,128)S(1)} %get-tuple-element.12, f32[128,768]{1,0:T(8,128)S(1)} %select_reduce_fusion, bf16[768,1536]{1,0:T(8,128)(2,1)S(1)} %bitcast.16), kind=kOutput, calls=%fused_computation.3 | convolution fusion | flops 1812332544 | bytes 3932160 | tf_op jit(solution)/shard_map/dot_general | solution.py:220
  (3 shorter events, 0.0 us)
Async XLA Ops:
  6.5 71.5 %all-gather.2.cloned.1.call-start = ((), (), s32[]{:S(2)}) async-start(), calls=%async_computation.4 | async-start | bytes 5308416 | tf_op jit(solution)/shard_map/all_gather | solution.py:184
  57.8 3.5 %copy-start.2 = (s32[1,128]{1,0:T(1,128)S(1)}, s32[1,128]{1,0:T(1,128)}, u32[]{:S(2)}) copy-start(s32[1,128]{1,0:T(1,128)} %rid_row_ref.1) | copy-start | bytes 1540
  57.8 3.6 %copy-start.5 = (s32[128,4]{0,1:T(4,128)S(1)}, s32[128,4]{0,1:T(4,128)}, u32[]{:S(2)}) copy-start(s32[128,4]{0,1:T(4,128)} %param.19) | copy-start | bytes 6148
  57.8 4.6 %copy-start = (bf16[128,1536]{1,0:T(8,128)(2,1)S(1)}, bf16[128,1536]{1,0:T(8,128)(2,1)}, u32[]{:S(2)}) copy-start(bf16[128,1536]{1,0:T(8,128)(2,1)} %q_ref.3) | copy-start | bytes 1179652
  57.8 4.6 %copy-start.1 = (bf16[2,128,256]{2,1,0:T(8,128)(2,1)S(1)}, bf16[2,128,256]{2,1,0:T(8,128)(2,1)}, u32[]{:S(2)}) copy-start(bf16[2,128,256]{2,1,0:T(8,128)(2,1)} %skv_ref.1) | copy-start | bytes 393220
  58.0 11.5 %collective-permute-start = (bf16[2,2048,256]{2,1,0:T(8,128)(2,1)S(1)}, bf16[2,2048,256]{2,1,0:T(8,128)(2,1)}, u32[]{:S(2)}, u32[]{:S(2)}) collective-permute-start(bf16[2,2048,256]{2,1,0:T(8,128)(2,1)S(1)} %bitcast.13), channel_id=1, source_target_pairs={{0,1},{1,0},{2,3},{3,2},{4,5},{5,4},{6,7},{7,6},{8,9},{9,8},{10,11... | collective-permute-start | bytes 6291464 | tf_op jit(solution)/shard_map/ppermute | solution.py:178
  69.4 8.6 %copy-start.3 = (bf16[128,1536]{1,0:T(8,128)(2,1)S(1)}, bf16[128,1536]{1,0:T(8,128)(2,1)}, u32[]{:S(2)}) copy-start(bf16[128,1536]{1,0:T(8,128)(2,1)} %param.12) | copy-start | bytes 1179652
  78.0 3.3 %copy-start.4 = (f32[1536]{0:T(1024)S(1)}, f32[1536]{0:T(1024)}, u32[]{:S(2)}) copy-start(f32[1536]{0:T(1024)} %param.18) | copy-start | bytes 18436
  128.5 4.0 %copy-start.6 = (f32[128,4]{0,1:T(4,128)S(1)}, f32[128,4]{0,1:T(4,128)}, u32[]{:S(2)}) copy-start(f32[128,4]{0,1:T(4,128)} %param.20) | copy-start | bytes 6148
  128.5 35.2 %all-to-all-start.3 = ((bf16[32,24,1536]{2,1,0:T(8,128)(2,1)}), bf16[32,24,1536]{2,1,0:T(8,128)(2,1)S(1)}, u32[]{:S(2)}, u32[]{:S(2)}) async-start(bf16[32,24,1536]{2,1,0:T(8,128)(2,1)} %bitcast.5), calls=%async_computation.3 | async-start | bytes 4718592 | tf_op jit(solution)/shard_map/all_to_all | solution.py:218
Sparse Core Ops, SparseCore 0:
  9.1 63.2 all-gather.1

commit v14 on v11

--- a/solution.py
+++ b/solution.py
@@ -76,7 +76,7 @@
         own_scale = jnp.exp(own_peak - peak)
         total = total_ref[:, head : head + 1] * first_scale + own_total * own_scale
         summed = acc_ref[:, columns] * first_scale + own_acc * own_scale
-        out_ref[:, columns] = (summed / total).astype(out_ref.dtype)
+        out_ref[:, columns] = (summed * (1.0 / total)).astype(out_ref.dtype)
 
 
 def whole(shape):

time: 171 us -> 172 us (level)
  no operation moved by 1% of the time
where the time goes in v14:
time: 172 us; the launch traced here: 171 us
  blocking collectives  84.3 us (49%)
  waiting for transfers between devices  31.7 us (18%)
  Pallas kernels  25.9 us (15%)
  between operations  13.5 us (8%)
  starting transfers between devices  7.35 us (4%)
  matrix products  6.21 us (4%)
    all_to_all x1, blocking collectives, on_device(): lax.all_to_all(outgoing, EXP, split_axis=0, concat_axis=0, tiled=True)  34.7 us
    all_to_all x1, blocking collectives, on_device(): lax.all_to_all(spread, 'chip', split_axis=1, concat_axis=1, tiled=True)  33 us
    all_to_all x1, waiting for transfers between devices, on_device(): lax.all_to_all(computed, EXP, split_axis=0, concat_axis=0, tiled=True)  31 us
    all_to_all x1, blocking collectives, on_device(): lax.all_to_all(jnp.broadcast_to(prefix_key_values[:, None], (2, req_count...  16.6 us
    pallas_call x1, Pallas kernels, expert_ffn(): pl.pallas_call(expert_kernel, grid=(hidden // block,), in_specs=[pl.Block...  10.2 us
    pallas_call x1, Pallas kernels, attend_merge(): pl.pallas_call(merge_kernel, in_specs=[whole(x.shape) for x in inputs], o...  8.67 us
    pallas_call x1, Pallas kernels, attend_local(): pl.pallas_call(local_kernel, in_specs=[whole(x.shape) for x in inputs], o...  6.98 us
    all_to_all x1, starting transfers between devices, on_device(): lax.all_to_all(computed, EXP, split_axis=0, concat_axis=0, tiled=True)  3.99 us
  transfers between devices with their start and end apart: 3, of which 1 were waited for; matrix products, arithmetic and copies ran while one was open for 1% of the time, Pallas kernels for 9%

profile of v14, /device:TPU:1, one launch (start us, length us, event | category | flops | bytes accessed | tf_op | source)
XLA Modules:
  0.0 171.2 jit_solution(17939753368268505587)
XLA Ops:
  6.5 0.0 all-gather.2.cloned.1.call-start
  6.5 0.7 all-gather.2.cloned.1.call-update
  7.3 0.7 broadcast_in_dim.14
  8.0 16.6 %all_to_all.20 = bf16[2,8,16,256]{3,2,0,1:T(8,128)(2,1)S(1)} all-to-all(bf16[2,8,16,256]{3,2,0,1:T(8,128)(2,1)S(1)} %broadcast_in_dim.14), channel_id=1, replica_groups=mesh['req'=8,'chip'=16,'core'=2] {'req'}, dimensions={1} | all-to-all | bytes 262144 | tf_op jit(solution)/shard_map/all_to_all | solution.py:176
  24.6 0.2 broadcast_in_dim.32
  24.8 33.0 %all_to_all.21 = bf16[2,16,128,256]{3,2,0,1:T(8,128)(2,1)S(1)} all-to-all(bf16[2,16,128,256]{3,2,0,1:T(8,128)(2,1)S(1)} %broadcast_in_dim.32), channel_id=1, replica_groups=mesh['req'=8,'chip'=16,'core'=2] {'chip'}, dimensions={1} | all-to-all | bytes 4194304 | tf_op jit(solution)/shard_map/all_to_all | solution.py:184
  57.8 0.0 copy-start.2
  57.8 0.0 copy-start.5
  57.8 0.0 copy-start
  57.8 0.0 copy-start.1
  57.8 0.1 copy.42
  58.0 3.4 %collective-permute-start = (bf16[2,2048,256]{2,1,0:T(8,128)(2,1)S(1)}, bf16[2,2048,256]{2,1,0:T(8,128)(2,1)}, u32[]{:S(2)}, u32[]{:S(2)}) collective-permute-start(bf16[2,2048,256]{2,1,0:T(8,128)(2,1)S(1)} %bitcast.13), channel_id=1, source_target_pairs={{0,1},{1,0},{2,3},{3,2},{4,5},{5,4},{6,7},{7,6},{8,9},{9,8},{10,11... | collective-permute-start | bytes 6291464 | tf_op jit(solution)/shard_map/ppermute | solution.py:187
  61.3 0.0 copy-done.2
  61.3 0.1 copy.43.rid_col_ref
  61.4 0.0 copy-done.5
  61.4 0.1 copy.44
  61.6 0.1 eq.28
  61.7 0.3 fusion.3
  61.9 0.1 reduce_sum.30
  62.1 0.1 copy.45
  62.1 0.3 fusion.1
  62.4 0.0 copy-done
  62.4 0.0 copy-done.1
  62.4 7.0 %shard_map.118 = (f32[128,1536]{1,0:T(8,128)S(1)}, f32[128,12]{1,0:T(8,128)S(1)}, f32[128,12]{1,0:T(8,128)S(1)}) custom-call(s32[128,1]{1,0:T(8,128)S(1)} %copy.43.rid_col_ref, s32[1,128]{1,0:T(1,128)S(1)} %copy-done.2, bf16[128,1536]{1,0:T(8,128)(2,1)S(1)} %copy-done, bf16[2,2048,256]{2,1,0:T(8,128)(2,1)S(1)} %bitcast.14, bf16[2,128,256]{2,1,0:T(8,128)(2,1)S(1)} %copy-done.1), custom_call_target="tpu_custom_call" | custom-call | tf_op jit(solution)/shard_map/pallas_call | solution.py:91
  69.4 0.0 copy-start.3
  69.4 0.0 collective-permute-done.pkv_ref
  69.5 8.7 %shard_map.119 = bf16[128,1536]{1,0:T(8,128)(2,1)S(1)} custom-call(bf16[128,1536]{1,0:T(8,128)(2,1)S(1)} %copy-done, bf16[2,2048,256]{2,1,0:T(8,128)(2,1)} %collective-permute-done.pkv_ref, f32[128,1536]{1,0:T(8,128)S(1)} %get-tuple-element.8.acc_ref, f32[128,12]{1,0:T(8,128)S(1)} %get-tuple-element.9.peak_ref, f32[128,12]{1,0:T(8,128)S(1)} %get-tuple-element.10.total_ref), custom_call_target="tpu_custom_call" | custom-call | tf_op jit(solution)/shard_map/pallas_call | solution.py:102
  78.1 0.0 copy-start.4
  78.1 0.0 all-gather.2.cloned.1.call-done
  78.2 0.0 copy-done.3
  78.2 3.2 %multiply_reduce_fusion = (f32[128]{0:T(128)S(1)}, f32[128,1536]{1,0:T(8,128)S(1)}) fusion(bf16[128,1536]{1,0:T(8,128)(2,1)S(1)} %shard_map.119, bf16[1536,1536]{1,0:T(8,128)(2,1)} %all-gather.2.cloned.1.call-done, bf16[128,1536]{1,0:T(8,128)(2,1)S(1)} %copy-done.3), kind=kOutput, calls=%fused_computation.12 | convolution fusion | flops 604766080 | bytes 6291968 | tf_op jit(solution)/shard_map/dot_general | solution.py:191
  81.4 0.0 copy-done.4
  81.4 0.9 convolution_convert_fusion
  82.3 34.7 %all_to_all.22 = bf16[32,24,1536]{2,1,0:T(8,128)(2,1)S(1)} all-to-all(bf16[32,24,1536]{2,1,0:T(8,128)(2,1)S(1)} %bitcast.17), channel_id=1, replica_groups=mesh['req'=8,'chip'=16,'core'=2] {'chip','core'}, dimensions={0} | all-to-all | bytes 4718592 | tf_op jit(solution)/shard_map/all_to_all | solution.py:222
  117.0 10.2 %shard_map.120 = bf16[768,1536]{1,0:T(8,128)(2,1)} custom-call(bf16[768,1536]{1,0:T(8,128)(2,1)S(1)} %bitcast.12, bf16[1,1536,768]{2,1,0:T(8,128)(2,1)} %gate_ref.1, bf16[1,1536,768]{2,1,0:T(8,128)(2,1)} %up_ref.1, bf16[1,768,1536]{2,1,0:T(8,128)(2,1)} %down_ref.1), custom_call_target="tpu_custom_call" | custom-call | tf_op jit(solution)/shard_map/pallas_call | solution.py:142
  127.2 0.0 copy-start.6
  127.2 4.0 %all-to-all-start.3 = ((bf16[32,24,1536]{2,1,0:T(8,128)(2,1)}), bf16[32,24,1536]{2,1,0:T(8,128)(2,1)S(1)}, u32[]{:S(2)}, u32[]{:S(2)}) async-start(bf16[32,24,1536]{2,1,0:T(8,128)(2,1)} %bitcast.5), calls=%async_computation.3 | async-start | bytes 4718592 | tf_op jit(solution)/shard_map/all_to_all | solution.py:227
  131.2 0.0 copy-done.6
  131.3 0.2 select_reduce_fusion
  131.5 31.0 %all-to-all-done.3 = bf16[32,24,1536]{2,1,0:T(8,128)(2,1)S(1)} async-done(((bf16[32,24,1536]{2,1,0:T(8,128)(2,1)}), bf16[32,24,1536]{2,1,0:T(8,128)(2,1)S(1)}, u32[]{:S(2)}, u32[]{:S(2)}) %all-to-all-start.3) | async-done | bytes 2359328 | tf_op jit(solution)/shard_map/all_to_all | solution.py:227
  162.5 1.8 %fusion = bf16[128,1536]{1,0:T(8,128)(2,1)} fusion(f32[128,1536]{1,0:T(8,128)S(1)} %get-tuple-element.12, f32[128,768]{1,0:T(8,128)S(1)} %select_reduce_fusion, bf16[768,1536]{1,0:T(8,128)(2,1)S(1)} %bitcast.16), kind=kOutput, calls=%fused_computation.3 | convolution fusion | flops 1812332544 | bytes 3932160 | tf_op jit(solution)/shard_map/dot_general | solution.py:229
  (3 shorter events, 0.0 us)
Async XLA Ops:
  6.5 71.6 %all-gather.2.cloned.1.call-start = ((), (), s32[]{:S(2)}) async-start(), calls=%async_computation.4 | async-start | bytes 5308416 | tf_op jit(solution)/shard_map/all_gather | solution.py:193
  57.8 3.5 %copy-start.2 = (s32[1,128]{1,0:T(1,128)S(1)}, s32[1,128]{1,0:T(1,128)}, u32[]{:S(2)}) copy-start(s32[1,128]{1,0:T(1,128)} %rid_row_ref.1) | copy-start | bytes 1540
  57.8 3.6 %copy-start.5 = (s32[128,4]{0,1:T(4,128)S(1)}, s32[128,4]{0,1:T(4,128)}, u32[]{:S(2)}) copy-start(s32[128,4]{0,1:T(4,128)} %param.19) | copy-start | bytes 6148
  57.8 4.6 %copy-start = (bf16[128,1536]{1,0:T(8,128)(2,1)S(1)}, bf16[128,1536]{1,0:T(8,128)(2,1)}, u32[]{:S(2)}) copy-start(bf16[128,1536]{1,0:T(8,128)(2,1)} %q_ref.3) | copy-start | bytes 1179652
  57.8 4.6 %copy-start.1 = (bf16[2,128,256]{2,1,0:T(8,128)(2,1)S(1)}, bf16[2,128,256]{2,1,0:T(8,128)(2,1)}, u32[]{:S(2)}) copy-start(bf16[2,128,256]{2,1,0:T(8,128)(2,1)} %skv_ref.1) | copy-start | bytes 393220
  58.0 11.5 %collective-permute-start = (bf16[2,2048,256]{2,1,0:T(8,128)(2,1)S(1)}, bf16[2,2048,256]{2,1,0:T(8,128)(2,1)}, u32[]{:S(2)}, u32[]{:S(2)}) collective-permute-start(bf16[2,2048,256]{2,1,0:T(8,128)(2,1)S(1)} %bitcast.13), channel_id=1, source_target_pairs={{0,1},{1,0},{2,3},{3,2},{4,5},{5,4},{6,7},{7,6},{8,9},{9,8},{10,11... | collective-permute-start | bytes 6291464 | tf_op jit(solution)/shard_map/ppermute | solution.py:187
  69.4 8.7 %copy-start.3 = (bf16[128,1536]{1,0:T(8,128)(2,1)S(1)}, bf16[128,1536]{1,0:T(8,128)(2,1)}, u32[]{:S(2)}) copy-start(bf16[128,1536]{1,0:T(8,128)(2,1)} %param.12) | copy-start | bytes 1179652
  78.1 3.3 %copy-start.4 = (f32[1536]{0:T(1024)S(1)}, f32[1536]{0:T(1024)}, u32[]{:S(2)}) copy-start(f32[1536]{0:T(1024)} %param.18) | copy-start | bytes 18436
  127.2 4.0 %copy-start.6 = (f32[128,4]{0,1:T(4,128)S(1)}, f32[128,4]{0,1:T(4,128)}, u32[]{:S(2)}) copy-start(f32[128,4]{0,1:T(4,128)} %param.20) | copy-start | bytes 6148
  127.2 35.2 %all-to-all-start.3 = ((bf16[32,24,1536]{2,1,0:T(8,128)(2,1)}), bf16[32,24,1536]{2,1,0:T(8,128)(2,1)S(1)}, u32[]{:S(2)}, u32[]{:S(2)}) async-start(bf16[32,24,1536]{2,1,0:T(8,128)(2,1)} %bitcast.5), calls=%async_computation.3 | async-start | bytes 4718592 | tf_op jit(solution)/shard_map/all_to_all | solution.py:227
Sparse Core Ops, SparseCore 0:
  9.1 63.2 all-gather.1
